TPU v7x, 256 devices: a whole 4x4x8 slice. The times are simulated.
256 devices in a mesh: dp: 128 (over x, y_lo, z, core), section: 2 (over y_hi).
Axes of the slice: x: 4, y: 4 (y_hi: 2, y_lo: 2; y = y_hi * 2 + y_lo), z: 8, core: 2. Of those that a mesh axis runs over, the one named last changes fastest.
Arguments:
- replay_rows: bfloat16 [65536, 4, 4, 128], P('dp'), may hold values from -6 to 6
- qvalues: bfloat16 [65536, 18], P('dp'), may hold values from -5 to 129
- target_logits: bfloat16 [65536, 18], P('dp'), may hold values from -8 to 258
- replay_owner: int32 [32768], P(('dp', 'section')), may hold values from 0 to 127, as said below
- replay_slot: int32 [32768], P(('dp', 'section')), may hold values from 0 to 511
- sample_actions: int32 [32768, 20], P(('dp', 'section')), may hold values from 0 to 17
- weights: bfloat16 [2, 147456], replicated, may hold values from -0.1875 to 0.1875
- head: bfloat16 [128, 18], replicated, may hold values from -0.5 to 0.5
- master: float32 [2, 147456], P('section', 'dp'), may hold values from -0.0012 to 0.0012
- moment_first: float32 [2, 147456], P('section', 'dp'), may hold values from -0.0021 to 0.0021
- moment_second: float32 [2, 147456], P('section', 'dp'), may hold values from 9.9e-14 to 1.01e-06
Outputs:
- adam_step: float32 [2, 147456], P('section', 'dp')
- new_weights: bfloat16 [2, 147456], replicated
Inputs may be any that keep to these rules, and one draw needn't show every extreme that they name: `replay_owner`: among the 128 rows of one learner device no shard is named more than 2 times; in every draw one shard is named exactly 2 times by every learner device.
All inputs are finite; a program needn't handle non-finite values.
Results may differ from a plain program's by a relative error of at most 0.013.
Values may be sent and summed in bfloat16 or wider, within the bound.
No kernel may reach another device: no remote copies, remote signals or barrier semaphores. Data moves between devices by JAX's collectives and lax.ppermute only.
A program may use at most 192 MiB of HBM per device.

v0:
```python
import jax
import jax.numpy as jnp
from jax import lax
from jax.sharding import PartitionSpec as P

constant_entropy_scale = 0.5
trust_weight = 0.5
beta_first = 0.9
beta_second = 0.999
epsilon = 1e-08
learn_rate = 0.0001


def tap_stack(field):
    grid_side = field.shape[1]
    padded_rows = jnp.pad(field, ((0, 0), (1, 1), (1, 1), (0, 0)))
    return jnp.concatenate(
        [
            padded_rows[:, shift_row : shift_row + grid_side, shift_col : shift_col + grid_side, :]
            for shift_row in range(3)
            for shift_col in range(3)
        ],
        axis=-1,
    )


def layer_grads(
    features,
    move_return_estimates,
    reference_policy_entries,
    actions,
    row_scale,
    w_first,
    second_weight,
    head,
):
    row_count, grid_side, _, channels = features.shape
    positions = row_count * grid_side * grid_side
    taps_first = tap_stack(features).reshape(positions, 9 * channels)
    hidden = jax.nn.relu(jnp.dot(taps_first, w_first, preferred_element_type=jnp.float32)).astype(
        jnp.bfloat16
    )
    taps_second = tap_stack(hidden.reshape(features.shape)).reshape(positions, 9 * channels)
    summed = features.reshape(positions, channels).astype(jnp.float32) + jnp.dot(
        taps_second, second_weight, preferred_element_type=jnp.float32
    )
    block_out = jax.nn.relu(summed).astype(jnp.bfloat16)
    averaged_embedding = jnp.mean(
        block_out.astype(jnp.float32).reshape(row_count, grid_side * grid_side, channels), axis=1
    ).astype(jnp.bfloat16)
    logits = reference_policy_entries.astype(jnp.float32) + jnp.dot(
        averaged_embedding, head, preferred_element_type=jnp.float32
    )
    policy = jax.nn.softmax(logits, axis=-1)
    prior = jax.nn.softmax(reference_policy_entries.astype(jnp.float32), axis=-1)
    selected_moves = (actions[:, :, None] == jnp.arange(head.shape[1])[None, None, :]).astype(
        jnp.float32
    )
    move_logit_matrix = (
        jnp.einsum("vlu,vu->vl", selected_moves, move_return_estimates.astype(jnp.float32))
        / constant_entropy_scale
    )
    sample_weight = jax.nn.softmax(move_logit_matrix, axis=-1)
    logit_grad = (
        (1.0 + trust_weight) * policy
        - jnp.einsum("nk,nka->na", sample_weight, selected_moves)
        - trust_weight * prior
    ) * row_scale[:, None]
    pooled_grad = jnp.dot(logit_grad, head.astype(jnp.float32).T, precision=lax.Precision.HIGHEST)
    spread = jnp.broadcast_to(
        (pooled_grad / (grid_side * grid_side))[:, None, :],
        (row_count, grid_side * grid_side, channels),
    ).reshape(positions, channels)
    out_grad = jnp.where(block_out > 0, spread, 0.0).astype(jnp.bfloat16)
    grad_second = lax.dot_general(
        taps_second, out_grad, (((0,), (0,)), ((), ())), preferred_element_type=jnp.float32
    )
    flipped = (
        second_weight.reshape(9, channels, channels)[::-1]
        .transpose(0, 2, 1)
        .reshape(9 * channels, channels)
    )
    taps_back = tap_stack(out_grad.reshape(features.shape)).reshape(positions, 9 * channels)
    hidden_grad = jnp.where(
        hidden > 0, jnp.dot(taps_back, flipped, preferred_element_type=jnp.float32), 0.0
    ).astype(jnp.bfloat16)
    grad_first = lax.dot_general(
        taps_first, hidden_grad, (((0,), (0,)), ((), ())), preferred_element_type=jnp.float32
    )
    return (grad_first, grad_second)


def per_device(
    replay_rows,
    qvalues,
    target_logits,
    replay_owner,
    replay_slot,
    sample_actions,
    weights,
    head,
    master,
    moment_first,
    moment_second,
):
    rows_dev = replay_owner.shape[0]
    owners = lax.axis_size("dp")
    capacity = 2 * rows_dev // owners
    learn_rows = rows_dev * owners * lax.axis_size("section")
    channels = replay_rows.shape[3]
    w_first = weights[0].reshape(9 * channels, channels)
    second_weight = weights[1].reshape(9 * channels, channels)
    row_order = jnp.arange(rows_dev, dtype=jnp.int32)
    earlier = (replay_owner[None, :] == replay_owner[:, None]) & (
        row_order[None, :] < row_order[:, None]
    )
    rank_within = jnp.sum(earlier.astype(jnp.int32), axis=1)
    slot_index = replay_owner * capacity + rank_within
    matches = slot_index[None, :] == jnp.arange(owners * capacity, dtype=jnp.int32)[:, None]
    occupied_entries = jnp.any(matches, axis=1)
    source = jnp.sum(jnp.where(matches, row_order[None, :], 0), axis=1)
    request = jnp.where(occupied_entries, jnp.take(replay_slot, source), -1).reshape(
        owners, capacity
    )
    row_index = jnp.maximum(
        lax.all_to_all(request, "dp", split_axis=0, concat_axis=0, tiled=True), 0
    )
    row_width = replay_rows.shape[1] * replay_rows.shape[2] * channels
    actions_n = qvalues.shape[1]
    packed = jnp.concatenate(
        [
            jnp.take(replay_rows.reshape(-1, row_width), row_index, axis=0),
            jnp.take(qvalues, row_index, axis=0),
            jnp.take(target_logits, row_index, axis=0),
        ],
        axis=-1,
    )
    slots = lax.all_to_all(packed, "dp", split_axis=0, concat_axis=0, tiled=True)
    picked = jnp.take(slots.reshape(owners * capacity, -1), slot_index, axis=0)
    features = picked[:, :row_width].reshape((rows_dev,) + replay_rows.shape[1:])
    move_return_estimates = picked[:, row_width : row_width + actions_n]
    reference_policy_entries = picked[:, row_width + actions_n :]
    row_scale = jnp.full((rows_dev,), 1.0 / learn_rows, jnp.float32)
    grad_first, grad_second = layer_grads(
        features,
        move_return_estimates,
        reference_policy_entries,
        sample_actions,
        row_scale,
        w_first,
        second_weight,
        head,
    )
    loss_derivative = jnp.stack([grad_first.reshape(-1), grad_second.reshape(-1)])
    piece_len = loss_derivative.shape[1] // owners
    layer = lax.axis_index("section")
    swap = [(0, 1), (1, 0)]
    contributions = lax.all_to_all(
        loss_derivative.reshape(2, owners, piece_len).transpose(1, 0, 2),
        "dp",
        split_axis=0,
        concat_axis=0,
        tiled=True,
    )
    partial = jnp.sum(contributions, axis=0)
    from_partner = lax.ppermute(
        lax.dynamic_slice_in_dim(partial, 1 - layer, 1, axis=0), "section", swap
    )
    owned_grad = lax.dynamic_slice_in_dim(partial, layer, 1, axis=0) + from_partner
    first = beta_first * moment_first + (1.0 - beta_first) * owned_grad
    second = beta_second * moment_second + (1.0 - beta_second) * owned_grad * owned_grad
    adam_step = first / (jnp.sqrt(second) + epsilon)
    new_piece = (master - learn_rate * adam_step).astype(jnp.bfloat16)
    partner_piece = lax.ppermute(new_piece, "section", swap)
    both_layers = jnp.where(
        layer == 0,
        jnp.concatenate([new_piece, partner_piece]),
        jnp.concatenate([partner_piece, new_piece]),
    )
    collected = lax.all_to_all(
        jnp.broadcast_to(both_layers[None], (owners, 2, piece_len)),
        "dp",
        split_axis=0,
        concat_axis=0,
        tiled=True,
    )
    new_weights = collected.transpose(1, 0, 2).reshape(2, owners * piece_len)
    return (adam_step, new_weights)


def solution(mesh):
    placed = (
        P("dp", None, None, None),
        P("dp", None),
        P("dp", None),
        P(("dp", "section")),
        P(("dp", "section")),
        P(("dp", "section"), None),
        P(),
        P(),
        P("section", "dp"),
        P("section", "dp"),
        P("section", "dp"),
    )
    return jax.shard_map(
        per_device, mesh=mesh, in_specs=placed, out_specs=(P("section", "dp"), P()), check_vma=False
    )
```

profile of v0, /device:TPU:1, one launch (start us, length us, event | category | flops | bytes accessed | tf_op | source)
XLA Modules:
  0.0 206.5 jit_solution(15754503060017692109)
XLA Ops:
  2.8 1.9 gather_fusion
  5.5 14.8 %all-to-all-start = ((s32[128,1,2]{2,1,0:T(1,128)}), s32[128,1,2]{2,1,0:T(1,128)S(1)}, u32[]{:S(2)}, u32[]{:S(2)}) async-start(s32[128,1,2]{2,1,0:T(1,128)} %bitcast.3), calls=%async_computation | async-start | bytes 131072 | tf_op jit(solution)/shard_map/all_to_all | solution.py:126
  20.3 3.3 %reshape.225 = bf16[512,2048]{1,0:T(8,128)(2,1)S(1)} reshape(bf16[512,4,4,128]{3,2,1,0:T(4,128)(2,1)} %param.13) | data formatting | bytes 4194304 | tf_op jit(solution)/shard_map/reshape | solution.py:132
  23.9 7.0 %all-to-all-done = s32[128,1,2]{2,1,0:T(1,128)S(1)} async-done(((s32[128,1,2]{2,1,0:T(1,128)}), s32[128,1,2]{2,1,0:T(1,128)S(1)}, u32[]{:S(2)}, u32[]{:S(2)}) %all-to-all-start) | async-done | bytes 1056 | tf_op jit(solution)/shard_map/all_to_all | solution.py:126
  31.3 1.4 gather_fusion.1
  35.1 1.0 broadcast_select_fusion
  36.4 5.0 %concatenate.80 = bf16[128,2,2084]{2,1,0:T(2,128)(2,1)} concatenate(bf16[128,2,2048]{2,1,0:T(2,128)(2,1)S(1)} %broadcast_select_fusion, bf16[128,2,18]{2,1,0:T(2,128)(2,1)S(1)} %get-tuple-element.38, bf16[128,2,18]{2,1,0:T(2,128)(2,1)S(1)} %get-tuple-element.37), dimensions={2} | concatenate | bytes 2134016 | tf_op jit(solution)/shard_map/concatenate | solution.py:130
  41.4 5.8 %all-to-all-start.1 = ((bf16[128,2,2084]{2,1,0:T(2,128)(2,1)}), bf16[128,2,2084]{2,1,0:T(2,128)(2,1)S(1)}, u32[]{:S(2)}, u32[]{:S(2)}) async-start(bf16[128,2,2084]{2,1,0:T(2,128)(2,1)} %concatenate.80), calls=%async_computation.1 | async-start | bytes 2228224 | tf_op jit(solution)/shard_map/all_to_all | solution.py:138
  47.2 6.9 %slice_reduce_fusion = (bf16[147456]{0:T(1024)(128)(2,1)S(1)}, bf16[147456]{0:T(1024)(128)(2,1)}) fusion(bf16[2,147456]{1,0:T(2,128)(2,1)S(1)} %copy-done.1), kind=kLoop, calls=%fused_computation.44 | loop fusion | bytes 1179648 | tf_op jit(solution)/shard_map/slice | solution.py:112
  55.1 23.8 %all-to-all-done.1 = bf16[128,2,2084]{2,1,0:T(2,128)(2,1)S(1)} async-done(((bf16[128,2,2084]{2,1,0:T(2,128)(2,1)}), bf16[128,2,2084]{2,1,0:T(2,128)(2,1)S(1)}, u32[]{:S(2)}, u32[]{:S(2)}) %all-to-all-start.1) | async-done | bytes 1067040 | tf_op jit(solution)/shard_map/all_to_all | solution.py:138
  81.3 1.0 copy.49
  82.3 1.2 copy.48
  83.5 5.2 %pad_slice_fusion.16 = (bf16[128,4,4,128]{3,2,1,0:T(4,128)(2,1)S(1)}, bf16[128,4,4,128]{3,2,1,0:T(4,128)(2,1)}, bf16[128,4,4,128]{3,2,1,0:T(4,128)(2,1)}, bf16[1...) fusion(bf16[128,4,4,128]{3,2,1,0:T(4,128)(2,1)} %copy.48), kind=kLoop, calls=%fused_computation.21 | loop fusion | bytes 4718592 | tf_op jit(solution)/shard_map/slice | solution.py:19
  89.5 2.1 %concatenate.85 = bf16[2048,128]{1,0:T(8,128)(2,1)} reshape(bf16[128,2048]{1,0:T(8,128)(2,1)} %copy.49) | data formatting | bytes 1048576 | tf_op jit(solution)/shard_map/concatenate | solution.py:17
  91.6 1.9 constant_dynamic-update-slice_fusion.7
  93.5 1.9 constant_dynamic-update-slice_fusion.6
  96.3 1.9 constant_dynamic-update-slice_fusion.4
  101.8 3.7 %fusion.2 = bf16[2048,128]{1,0:T(8,128)(2,1)S(1)} fusion(bf16[2048,1152]{1,0:T(8,128)(2,1)} %constant_dynamic-update-slice_fusion, bf16[147456]{0:T(1024)(128)(2,1)S(1)} %copy-done.3), kind=kOutput, calls=%fused_computation.34 | convolution fusion | flops 604504064 | bytes 5537792 | tf_op jit(solution)/shard_map/dot_general | solution.py:40
  105.5 1.9 pad_slice_fusion.8
  108.7 1.5 convert_reduce_fusion
  111.0 1.4 fusion.43
  112.4 1.8 pad_slice_fusion
  115.4 2.2 %copy-done.5 = bf16[2048,1152]{1,0:T(8,128)(2,1)} copy-done((bf16[2048,1152]{1,0:T(8,128)(2,1)}, bf16[2048,1152]{1,0:T(8,128)(2,1)S(1)}, u32[]{:S(2)}) %copy-start.5) | copy-done | bytes 4718616
  117.6 8.0 %fusion.5 = f32[1152,128]{1,0:T(8,128)S(1)} fusion(bf16[2048,1152]{1,0:T(8,128)(2,1)} %constant_dynamic-update-slice_fusion, bf16[2048,1152]{1,0:T(8,128)(2,1)} %copy-done.5, bf16[1152,128]{1,0:T(8,128)(2,1)S(1)} %bitcast.113, bf16[2048,128]{1,0:T(8,128)(2,1)S(1)} %fusion.2), kind=kOutput, calls=%fused_computation.43 | convolution fusion | flops 1208745984 | bytes 10846208 | tf_op jit(solution)/shard_map/dot_general | solution.py:87
  125.6 2.1 %maximum_bitcast_fusion = f32[128,2,1152]{2,1,0:T(2,128)} fusion(f32[1,128,1152]{2,0,1:T(1,128)S(1)} %bitcast.82, f32[1,128,1152]{2,0,1:T(1,128)S(1)} %bitcast.112), kind=kLoop, calls=%fused_computation.37 | loop fusion | flops 294912 | bytes 2359296 | tf_op jit(solution)/shard_map/transpose | solution.py:159
  127.6 6.1 %all-to-all-start.2 = ((f32[128,2,1152]{2,1,0:T(2,128)}), f32[128,2,1152]{2,1,0:T(2,128)S(1)}, u32[]{:S(2)}, u32[]{:S(2)}) async-start(f32[128,2,1152]{2,1,0:T(2,128)} %maximum_bitcast_fusion), calls=%async_computation.2 | async-start | bytes 2359296 | tf_op jit(solution)/shard_map/all_to_all | solution.py:158
  133.7 32.9 %all-to-all-done.2 = f32[128,2,1152]{2,1,0:T(2,128)S(1)} async-done(((f32[128,2,1152]{2,1,0:T(2,128)}), f32[128,2,1152]{2,1,0:T(2,128)S(1)}, u32[]{:S(2)}, u32[]{:S(2)}) %all-to-all-start.2) | async-done | bytes 1179680 | tf_op jit(solution)/shard_map/all_to_all | solution.py:158
  167.1 2.7 %collective-permute-start = (f32[1,1152]{1,0:T(1,128)S(1)}, f32[1,1152]{1,0:T(1,128)S(1)}, u32[]{:S(2)}, u32[]{:S(2)}) collective-permute-start(f32[1,1152]{1,0:T(1,128)S(1)} %constant_dynamic-slice_fusion), channel_id=1, source_target_pairs={{0,1},{1,0},{2,3},{3,2},{4,5},{5,4},{6,7},{7,6},{8,9},{9,8},{10,11... | collective-permute-start | bytes 13832 | tf_op jit(solution)/shard_map/ppermute | solution.py:166
  169.8 1.3 collective-permute-done
  171.8 2.6 %collective-permute-start.1 = (bf16[1,1152]{1,0:T(2,128)(2,1)S(1)}, bf16[1,1152]{1,0:T(2,128)(2,1)S(1)}, u32[]{:S(2)}, u32[]{:S(2)}) collective-permute-start(bf16[1,1152]{1,0:T(2,128)(2,1)S(1)} %get-tuple-element.5), channel_id=1, source_target_pairs={{0,1},{1,0},{2,3},{3,2},{4,5},{5,4},{6,7},{7,6},{8,9},{9,8},{10,11... | collective-permute-start | bytes 6920 | tf_op jit(solution)/shard_map/ppermute | solution.py:174
  174.4 1.3 collective-permute-done.1
  176.1 29.6 %all_to_all.21 = bf16[128,2,1152]{2,1,0:T(2,128)(2,1)S(1)} all-to-all(bf16[128,2,1152]{2,1,0:T(2,128)(2,1)S(1)} %broadcast_in_dim.93), channel_id=1, replica_groups=mesh['dp'=128,'section'=2] {'dp'}, dimensions={0} | all-to-all | bytes 1179648 | tf_op jit(solution)/shard_map/all_to_all | solution.py:180
  (96 shorter events, 20.0 us)
Async XLA Ops:
  0.6 109.7 %copy-start = (bf16[128,18]{0,1:T(8,128)(2,1)S(1)}, bf16[128,18]{0,1:T(8,128)(2,1)}, u32[]{:S(2)}) copy-start(bf16[128,18]{0,1:T(8,128)(2,1)} %param.20) | copy-start | bytes 13828
  0.6 22.9 %copy-start.7 = (bf16[512,18]{0,1:T(8,128)(2,1)S(1)}, bf16[512,18]{0,1:T(8,128)(2,1)}, u32[]{:S(2)}) copy-start(bf16[512,18]{0,1:T(8,128)(2,1)} %param.15) | copy-start | bytes 55300
  0.7 23.1 %copy-start.8 = (bf16[512,18]{0,1:T(8,128)(2,1)S(1)}, bf16[512,18]{0,1:T(8,128)(2,1)}, u32[]{:S(2)}) copy-start(bf16[512,18]{0,1:T(8,128)(2,1)} %param.14) | copy-start | bytes 55300
  5.5 25.4 %all-to-all-start = ((s32[128,1,2]{2,1,0:T(1,128)}), s32[128,1,2]{2,1,0:T(1,128)S(1)}, u32[]{:S(2)}, u32[]{:S(2)}) async-start(s32[128,1,2]{2,1,0:T(1,128)} %bitcast.3), calls=%async_computation | async-start | bytes 131072 | tf_op jit(solution)/shard_map/all_to_all | solution.py:126
  33.4 13.8 %copy-start.1 = (bf16[2,147456]{1,0:T(2,128)(2,1)S(1)}, bf16[2,147456]{1,0:T(2,128)(2,1)}, u32[]{:S(2)}) copy-start(bf16[2,147456]{1,0:T(2,128)(2,1)} %param.19) | copy-start | bytes 1769476
  41.4 37.6 %all-to-all-start.1 = ((bf16[128,2,2084]{2,1,0:T(2,128)(2,1)}), bf16[128,2,2084]{2,1,0:T(2,128)(2,1)S(1)}, u32[]{:S(2)}, u32[]{:S(2)}) async-start(bf16[128,2,2084]{2,1,0:T(2,128)(2,1)} %concatenate.80), calls=%async_computation.1 | async-start | bytes 2228224 | tf_op jit(solution)/shard_map/all_to_all | solution.py:138
  91.6 10.2 %copy-start.3 = (bf16[147456]{0:T(1024)(128)(2,1)S(1)}, bf16[147456]{0:T(1024)(128)(2,1)}, u32[]{:S(2)}) copy-start(bf16[147456]{0:T(1024)(128)(2,1)} %get-tuple-element.4) | copy-start | bytes 884740
  107.5 1.2 copy-start.2
  108.5 1.7 copy-start.6
  114.2 3.4 %copy-start.4 = (bf16[9,128,128]{2,1,0:T(8,128)(2,1)S(1)}, bf16[9,128,128]{2,1,0:T(8,128)(2,1)}, u32[]{:S(2)}) copy-start(bf16[9,128,128]{2,1,0:T(8,128)(2,1)} %copy.50) | copy-start | bytes 884740
  115.4 2.2 %copy-start.5 = (bf16[2048,1152]{1,0:T(8,128)(2,1)}, bf16[2048,1152]{1,0:T(8,128)(2,1)S(1)}, u32[]{:S(2)}) copy-start(bf16[2048,1152]{1,0:T(8,128)(2,1)S(1)} %constant_dynamic-update-slice_fusion.18) | copy-start | bytes 14155780
  125.5 45.6 %copy-start.9 = (f32[1,1152]{1,0:T(1,128)S(1)}, f32[1,1152]{1,0:T(1,128)}, u32[]{:S(2)}) copy-start(f32[1,1152]{1,0:T(1,128)} %param.21) | copy-start | bytes 13828
  125.5 45.6 %copy-start.10 = (f32[1,1152]{1,0:T(1,128)S(1)}, f32[1,1152]{1,0:T(1,128)}, u32[]{:S(2)}) copy-start(f32[1,1152]{1,0:T(1,128)} %param.23) | copy-start | bytes 13828
  125.6 45.6 %copy-start.11 = (f32[1,1152]{1,0:T(1,128)S(1)}, f32[1,1152]{1,0:T(1,128)}, u32[]{:S(2)}) copy-start(f32[1,1152]{1,0:T(1,128)} %param.22) | copy-start | bytes 13828
  127.6 39.0 %all-to-all-start.2 = ((f32[128,2,1152]{2,1,0:T(2,128)}), f32[128,2,1152]{2,1,0:T(2,128)S(1)}, u32[]{:S(2)}, u32[]{:S(2)}) async-start(f32[128,2,1152]{2,1,0:T(2,128)} %maximum_bitcast_fusion), calls=%async_computation.2 | async-start | bytes 2359296 | tf_op jit(solution)/shard_map/all_to_all | solution.py:158
  167.1 4.1 %collective-permute-start = (f32[1,1152]{1,0:T(1,128)S(1)}, f32[1,1152]{1,0:T(1,128)S(1)}, u32[]{:S(2)}, u32[]{:S(2)}) collective-permute-start(f32[1,1152]{1,0:T(1,128)S(1)} %constant_dynamic-slice_fusion), channel_id=1, source_target_pairs={{0,1},{1,0},{2,3},{3,2},{4,5},{5,4},{6,7},{7,6},{8,9},{9,8},{10,11... | collective-permute-start | bytes 13832 | tf_op jit(solution)/shard_map/ppermute | solution.py:166
  171.8 4.0 %collective-permute-start.1 = (bf16[1,1152]{1,0:T(2,128)(2,1)S(1)}, bf16[1,1152]{1,0:T(2,128)(2,1)S(1)}, u32[]{:S(2)}, u32[]{:S(2)}) collective-permute-start(bf16[1,1152]{1,0:T(2,128)(2,1)S(1)} %get-tuple-element.5), channel_id=1, source_target_pairs={{0,1},{1,0},{2,3},{3,2},{4,5},{5,4},{6,7},{7,6},{8,9},{9,8},{10,11... | collective-permute-start | bytes 6920 | tf_op jit(solution)/shard_map/ppermute | solution.py:174
where the time goes:
time: 207 us
  waiting for transfers between devices  66.5 us (32%)
  local copies, waits for them, and re-layouts  54.7 us (26%)
  starting transfers between devices  32 us (15%)
  blocking collectives  29.6 us (14%)
  matrix products  15 us (7%)
  other arithmetic  7.5 us (4%)
    all_to_all x1, waiting for transfers between devices, per_device(): lax.all_to_all(loss_derivative.reshape(2, owners, piece_len).transpose(1,...  32.9 us
    all_to_all x1, blocking collectives, per_device(): lax.all_to_all(jnp.broadcast_to(both_layers[None], (owners, 2, piece_len)...  29.6 us
    all_to_all x1, waiting for transfers between devices, per_device(): lax.all_to_all(packed, 'dp', split_axis=0, concat_axis=0, tiled=True)  23.8 us
    unnamed x51, local copies, waits for them, and re-layouts  15.5 us
    all_to_all x1, starting transfers between devices, per_device(): lax.all_to_all(request, 'dp', split_axis=0, concat_axis=0, tiled=True)  14.8 us
    slice x3, local copies, waits for them, and re-layouts, tap_stack(): padded_rows[:, shift_row:shift_row + grid_side, shift_col:shift_col + gri...  8.82 us
    dot_general x1, matrix products, layer_grads(): lax.dot_general(taps_first, hidden_grad, (((0,), (0,)), ((), ())), prefer...  7.96 us
    all_to_all x1, waiting for transfers between devices, per_device(): lax.all_to_all(request, 'dp', split_axis=0, concat_axis=0, tiled=True)  7.05 us
  transfers between devices with their start and end apart: 5, of which 5 were waited for; matrix products, arithmetic and copies ran while one was open for 6% of the time, Pallas kernels for 0%

commit v1 on v0

--- a/solution.py
+++ b/solution.py
@@ -110,6 +110,15 @@
     channels = replay_rows.shape[3]
     w_first = weights[0].reshape(9 * channels, channels)
     second_weight = weights[1].reshape(9 * channels, channels)
+    layer = lax.axis_index("section")
+    swap = [(0, 1), (1, 0)]
+    own_state = jnp.concatenate([master, moment_first, moment_second])
+    partner_state = lax.ppermute(own_state, "section", swap)
+    state = jnp.where(
+        layer == 0,
+        jnp.stack([own_state, partner_state], axis=1),
+        jnp.stack([partner_state, own_state], axis=1),
+    )
     row_order = jnp.arange(rows_dev, dtype=jnp.int32)
     earlier = (replay_owner[None, :] == replay_owner[:, None]) & (
         row_order[None, :] < row_order[:, None]
@@ -153,8 +162,6 @@
     )
     loss_derivative = jnp.stack([grad_first.reshape(-1), grad_second.reshape(-1)])
     piece_len = loss_derivative.shape[1] // owners
-    layer = lax.axis_index("section")
-    swap = [(0, 1), (1, 0)]
     contributions = lax.all_to_all(
         loss_derivative.reshape(2, owners, piece_len).transpose(1, 0, 2),
         "dp",
@@ -163,20 +170,12 @@
         tiled=True,
     )
     partial = jnp.sum(contributions, axis=0)
-    from_partner = lax.ppermute(
-        lax.dynamic_slice_in_dim(partial, 1 - layer, 1, axis=0), "section", swap
-    )
-    owned_grad = lax.dynamic_slice_in_dim(partial, layer, 1, axis=0) + from_partner
-    first = beta_first * moment_first + (1.0 - beta_first) * owned_grad
-    second = beta_second * moment_second + (1.0 - beta_second) * owned_grad * owned_grad
-    adam_step = first / (jnp.sqrt(second) + epsilon)
-    new_piece = (master - learn_rate * adam_step).astype(jnp.bfloat16)
-    partner_piece = lax.ppermute(new_piece, "section", swap)
-    both_layers = jnp.where(
-        layer == 0,
-        jnp.concatenate([new_piece, partner_piece]),
-        jnp.concatenate([partner_piece, new_piece]),
-    )
+    owned_grad = partial + lax.ppermute(partial, "section", swap)
+    first = beta_first * state[1] + (1.0 - beta_first) * owned_grad
+    second = beta_second * state[2] + (1.0 - beta_second) * owned_grad * owned_grad
+    both_steps = first / (jnp.sqrt(second) + epsilon)
+    both_layers = (state[0] - learn_rate * both_steps).astype(jnp.bfloat16)
+    adam_step = lax.dynamic_slice_in_dim(both_steps, layer, 1, axis=0)
     collected = lax.all_to_all(
         jnp.broadcast_to(both_layers[None], (owners, 2, piece_len)),
         "dp",

time: 207 us -> 203 us (0.981)
  blocking collectives: 29.6 us -> 0 us
  waiting for transfers between devices: 66.5 us -> 83 us
  starting transfers between devices: 32 us -> 39.4 us
    all_to_all x1 -> x0, blocking collectives: 29.6 us -> none  [per_device(): lax.all_to_all(jnp.broadcast_to(both_layers[None], (owners, 2, piece_len)...]
    all_to_all x0 -> x1, waiting for transfers between devices: none -> 20.7 us  [per_device(): lax.all_to_all(jnp.broadcast_to(both_layers[None], (owners, 2, piece_len)...]
    all_to_all x0 -> x1, starting transfers between devices: none -> 7.35 us  [per_device(): lax.all_to_all(jnp.broadcast_to(both_layers[None], (owners, 2, piece_len)...]
    all_to_all x1, waiting for transfers between devices: 32.9 us -> 28.3 us  [per_device(): lax.all_to_all(loss_derivative.reshape(2, owners, piece_len).transpose(1,...]
  transfers between devices with their start and end apart: 5 -> 6, of which waited for: 5 -> 6; matrix products, arithmetic and copies ran while one was open for 6% -> 6% of each run, Pallas kernels for 0% -> 0%
where the time goes in v1:
time: 203 us; the launch traced here: 202 us
  waiting for transfers between devices  83 us (41%)
  local copies, waits for them, and re-layouts  56.2 us (28%)
  starting transfers between devices  39.4 us (19%)
  matrix products  15 us (7%)
  other arithmetic  6.94 us (3%)
    all_to_all x1, waiting for transfers between devices, per_device(): lax.all_to_all(loss_derivative.reshape(2, owners, piece_len).transpose(1,...  28.3 us
    all_to_all x1, waiting for transfers between devices, per_device(): lax.all_to_all(packed, 'dp', split_axis=0, concat_axis=0, tiled=True)  23.8 us
    all_to_all x1, waiting for transfers between devices, per_device(): lax.all_to_all(jnp.broadcast_to(both_layers[None], (owners, 2, piece_len)...  20.7 us
    unnamed x51, local copies, waits for them, and re-layouts  15.5 us
    all_to_all x1, starting transfers between devices, per_device(): lax.all_to_all(request, 'dp', split_axis=0, concat_axis=0, tiled=True)  14.8 us
    slice x3, local copies, waits for them, and re-layouts, tap_stack(): padded_rows[:, shift_row:shift_row + grid_side, shift_col:shift_col + gri...  8.82 us
    dot_general x1, matrix products, layer_grads(): lax.dot_general(taps_first, hidden_grad, (((0,), (0,)), ((), ())), prefer...  7.96 us
    all_to_all x1, starting transfers between devices, per_device(): lax.all_to_all(jnp.broadcast_to(both_layers[None], (owners, 2, piece_len)...  7.35 us
  transfers between devices with their start and end apart: 6, of which 6 were waited for; matrix products, arithmetic and copies ran while one was open for 6% of the time, Pallas kernels for 0%

profile of v1, /device:TPU:1, one launch (start us, length us, event | category | flops | bytes accessed | tf_op | source)
XLA Modules:
  0.0 201.8 jit_solution(1478042683267352231)
XLA Ops:
  2.8 1.9 gather_fusion
  5.5 14.8 %all-to-all-start = ((s32[128,1,2]{2,1,0:T(1,128)}), s32[128,1,2]{2,1,0:T(1,128)S(1)}, u32[]{:S(2)}, u32[]{:S(2)}) async-start(s32[128,1,2]{2,1,0:T(1,128)} %bitcast.4), calls=%async_computation | async-start | bytes 131072 | tf_op jit(solution)/shard_map/all_to_all | solution.py:135
  20.3 3.3 %reshape.201 = bf16[512,2048]{1,0:T(8,128)(2,1)S(1)} reshape(bf16[512,4,4,128]{3,2,1,0:T(4,128)(2,1)} %param.13) | data formatting | bytes 4194304 | tf_op jit(solution)/shard_map/reshape | solution.py:141
  23.9 7.0 %all-to-all-done = s32[128,1,2]{2,1,0:T(1,128)S(1)} async-done(((s32[128,1,2]{2,1,0:T(1,128)}), s32[128,1,2]{2,1,0:T(1,128)S(1)}, u32[]{:S(2)}, u32[]{:S(2)}) %all-to-all-start) | async-done | bytes 1056 | tf_op jit(solution)/shard_map/all_to_all | solution.py:135
  31.3 1.4 gather_fusion.1
  36.4 5.0 %concatenate.70 = bf16[128,2,2084]{2,1,0:T(2,128)(2,1)} concatenate(bf16[128,2,2048]{2,1,0:T(2,128)(2,1)S(1)} %broadcast_select_fusion, bf16[128,2,18]{2,1,0:T(2,128)(2,1)S(1)} %get-tuple-element.38, bf16[128,2,18]{2,1,0:T(2,128)(2,1)S(1)} %get-tuple-element.37), dimensions={2} | concatenate | bytes 2134016 | tf_op jit(solution)/shard_map/concatenate | solution.py:139
  41.4 5.8 %all-to-all-start.1 = ((bf16[128,2,2084]{2,1,0:T(2,128)(2,1)}), bf16[128,2,2084]{2,1,0:T(2,128)(2,1)S(1)}, u32[]{:S(2)}, u32[]{:S(2)}) async-start(bf16[128,2,2084]{2,1,0:T(2,128)(2,1)} %concatenate.70), calls=%async_computation.1 | async-start | bytes 2228224 | tf_op jit(solution)/shard_map/all_to_all | solution.py:147
  47.2 6.9 %slice_reduce_fusion = (bf16[147456]{0:T(1024)(128)(2,1)S(1)}, bf16[147456]{0:T(1024)(128)(2,1)}) fusion(bf16[2,147456]{1,0:T(2,128)(2,1)S(1)} %copy-done.1), kind=kLoop, calls=%fused_computation.44 | loop fusion | bytes 1179648 | tf_op jit(solution)/shard_map/slice | solution.py:112
  55.1 23.8 %all-to-all-done.1 = bf16[128,2,2084]{2,1,0:T(2,128)(2,1)S(1)} async-done(((bf16[128,2,2084]{2,1,0:T(2,128)(2,1)}), bf16[128,2,2084]{2,1,0:T(2,128)(2,1)S(1)}, u32[]{:S(2)}, u32[]{:S(2)}) %all-to-all-start.1) | async-done | bytes 1067040 | tf_op jit(solution)/shard_map/all_to_all | solution.py:147
  82.3 1.2 copy.48
  83.5 5.2 %pad_slice_fusion.16 = (bf16[128,4,4,128]{3,2,1,0:T(4,128)(2,1)S(1)}, bf16[128,4,4,128]{3,2,1,0:T(4,128)(2,1)}, bf16[128,4,4,128]{3,2,1,0:T(4,128)(2,1)}, bf16[1...) fusion(bf16[128,4,4,128]{3,2,1,0:T(4,128)(2,1)} %copy.48), kind=kLoop, calls=%fused_computation.21 | loop fusion | bytes 4718592 | tf_op jit(solution)/shard_map/slice | solution.py:19
  89.5 2.1 %concatenate.75 = bf16[2048,128]{1,0:T(8,128)(2,1)} reshape(bf16[128,2048]{1,0:T(8,128)(2,1)} %copy.49) | data formatting | bytes 1048576 | tf_op jit(solution)/shard_map/concatenate | solution.py:17
  91.6 1.9 constant_dynamic-update-slice_fusion.7
  93.5 1.9 constant_dynamic-update-slice_fusion.6
  96.3 1.9 constant_dynamic-update-slice_fusion.4
  101.8 3.7 %fusion.2 = bf16[2048,128]{1,0:T(8,128)(2,1)S(1)} fusion(bf16[2048,1152]{1,0:T(8,128)(2,1)} %constant_dynamic-update-slice_fusion, bf16[147456]{0:T(1024)(128)(2,1)S(1)} %copy-done.3), kind=kOutput, calls=%fused_computation.34 | convolution fusion | flops 604504064 | bytes 5537792 | tf_op jit(solution)/shard_map/dot_general | solution.py:40
  105.5 1.9 pad_slice_fusion.8
  108.7 1.5 convert_reduce_fusion
  111.0 1.4 fusion.52
  112.4 1.8 pad_slice_fusion
  115.4 2.2 %copy-done.5 = bf16[2048,1152]{1,0:T(8,128)(2,1)} copy-done((bf16[2048,1152]{1,0:T(8,128)(2,1)}, bf16[2048,1152]{1,0:T(8,128)(2,1)S(1)}, u32[]{:S(2)}) %copy-start.5) | copy-done | bytes 4718616
  117.6 8.0 %fusion.5 = f32[1152,128]{1,0:T(8,128)S(1)} fusion(bf16[2048,1152]{1,0:T(8,128)(2,1)} %constant_dynamic-update-slice_fusion, bf16[2048,1152]{1,0:T(8,128)(2,1)} %copy-done.5, bf16[1152,128]{1,0:T(8,128)(2,1)S(1)} %bitcast.131, bf16[2048,128]{1,0:T(8,128)(2,1)S(1)} %fusion.2), kind=kOutput, calls=%fused_computation.43 | convolution fusion | flops 1208745984 | bytes 10846208 | tf_op jit(solution)/shard_map/dot_general | solution.py:87
  125.6 2.1 %maximum_bitcast_fusion = f32[128,2,1152]{2,1,0:T(2,128)} fusion(f32[1,128,1152]{2,0,1:T(1,128)S(1)} %bitcast.100, f32[1,128,1152]{2,0,1:T(1,128)S(1)} %bitcast.130), kind=kLoop, calls=%fused_computation.37 | loop fusion | flops 294912 | bytes 2359296 | tf_op jit(solution)/shard_map/transpose | solution.py:166
  127.6 6.1 %all-to-all-start.2 = ((f32[128,2,1152]{2,1,0:T(2,128)}), f32[128,2,1152]{2,1,0:T(2,128)S(1)}, u32[]{:S(2)}, u32[]{:S(2)}) async-start(f32[128,2,1152]{2,1,0:T(2,128)} %maximum_bitcast_fusion), calls=%async_computation.2 | async-start | bytes 2359296 | tf_op jit(solution)/shard_map/all_to_all | solution.py:165
  133.8 2.7 %collective-permute-start = (f32[3,1152]{1,0:T(4,128)S(1)}, f32[3,1152]{1,0:T(4,128)S(1)}, u32[]{:S(2)}, u32[]{:S(2)}) collective-permute-start(f32[3,1152]{1,0:T(4,128)S(1)} %pad_maximum_fusion), channel_id=1, source_target_pairs={{0,1},{1,0},{2,3},{3,2},{4,5},{5,4},{6,7},{7,6},{8,9},{9,8},{10,11... | collective-permute-start | bytes 41480 | tf_op jit(solution)/shard_map/ppermute | solution.py:116
  136.5 1.8 collective-permute-done
  138.3 28.3 %all-to-all-done.2 = f32[128,2,1152]{2,1,0:T(2,128)S(1)} async-done(((f32[128,2,1152]{2,1,0:T(2,128)}), f32[128,2,1152]{2,1,0:T(2,128)S(1)}, u32[]{:S(2)}, u32[]{:S(2)}) %all-to-all-start.2) | async-done | bytes 1179680 | tf_op jit(solution)/shard_map/all_to_all | solution.py:165
  167.1 2.7 %collective-permute-start.1 = (f32[2,1152]{1,0:T(2,128)S(1)}, f32[2,1152]{1,0:T(2,128)S(1)}, u32[]{:S(2)}, u32[]{:S(2)}) collective-permute-start(f32[2,1152]{1,0:T(2,128)S(1)} %reduce_sum.75), channel_id=1, source_target_pairs={{0,1},{1,0},{2,3},{3,2},{4,5},{5,4},{6,7},{7,6},{8,9},{9,8},{10,11... | collective-permute-start | bytes 27656 | tf_op jit(solution)/shard_map/ppermute | solution.py:173
  169.8 1.3 collective-permute-done.1
  171.2 1.1 broadcast_in_dim.93
  172.3 7.4 %all-to-all-start.3 = ((bf16[128,2,1152]{2,1,0:T(2,128)(2,1)}), bf16[128,2,1152]{2,1,0:T(2,128)(2,1)S(1)}, u32[]{:S(2)}, u32[]{:S(2)}) async-start(bf16[128,2,1152]{2,1,0:T(2,128)(2,1)} %broadcast_in_dim.93), calls=%async_computation.3 | async-start | bytes 1179648 | tf_op jit(solution)/shard_map/all_to_all | solution.py:179
  180.3 20.7 %all-to-all-done.3 = bf16[128,2,1152]{2,1,0:T(2,128)(2,1)S(1)} async-done(((bf16[128,2,1152]{2,1,0:T(2,128)(2,1)}), bf16[128,2,1152]{2,1,0:T(2,128)(2,1)S(1)}, u32[]{:S(2)}, u32[]{:S(2)}) %all-to-all-start.3) | async-done | bytes 589856 | tf_op jit(solution)/shard_map/all_to_all | solution.py:179
  (100 shorter events, 21.8 us)
Async XLA Ops:
  0.6 109.7 %copy-start = (bf16[128,18]{0,1:T(8,128)(2,1)S(1)}, bf16[128,18]{0,1:T(8,128)(2,1)}, u32[]{:S(2)}) copy-start(bf16[128,18]{0,1:T(8,128)(2,1)} %param.20) | copy-start | bytes 13828
  0.6 22.9 %copy-start.7 = (bf16[512,18]{0,1:T(8,128)(2,1)S(1)}, bf16[512,18]{0,1:T(8,128)(2,1)}, u32[]{:S(2)}) copy-start(bf16[512,18]{0,1:T(8,128)(2,1)} %param.15) | copy-start | bytes 55300
  0.7 23.1 %copy-start.8 = (bf16[512,18]{0,1:T(8,128)(2,1)S(1)}, bf16[512,18]{0,1:T(8,128)(2,1)}, u32[]{:S(2)}) copy-start(bf16[512,18]{0,1:T(8,128)(2,1)} %param.14) | copy-start | bytes 55300
  5.5 25.4 %all-to-all-start = ((s32[128,1,2]{2,1,0:T(1,128)}), s32[128,1,2]{2,1,0:T(1,128)S(1)}, u32[]{:S(2)}, u32[]{:S(2)}) async-start(s32[128,1,2]{2,1,0:T(1,128)} %bitcast.4), calls=%async_computation | async-start | bytes 131072 | tf_op jit(solution)/shard_map/all_to_all | solution.py:135
  33.4 13.8 %copy-start.1 = (bf16[2,147456]{1,0:T(2,128)(2,1)S(1)}, bf16[2,147456]{1,0:T(2,128)(2,1)}, u32[]{:S(2)}) copy-start(bf16[2,147456]{1,0:T(2,128)(2,1)} %param.19) | copy-start | bytes 1769476
  41.4 37.6 %all-to-all-start.1 = ((bf16[128,2,2084]{2,1,0:T(2,128)(2,1)}), bf16[128,2,2084]{2,1,0:T(2,128)(2,1)S(1)}, u32[]{:S(2)}, u32[]{:S(2)}) async-start(bf16[128,2,2084]{2,1,0:T(2,128)(2,1)} %concatenate.70), calls=%async_computation.1 | async-start | bytes 2228224 | tf_op jit(solution)/shard_map/all_to_all | solution.py:147
  91.6 10.2 %copy-start.3 = (bf16[147456]{0:T(1024)(128)(2,1)S(1)}, bf16[147456]{0:T(1024)(128)(2,1)}, u32[]{:S(2)}) copy-start(bf16[147456]{0:T(1024)(128)(2,1)} %get-tuple-element.4) | copy-start | bytes 884740
  107.5 1.2 copy-start.2
  108.5 1.7 copy-start.6
  114.2 3.4 %copy-start.4 = (bf16[9,128,128]{2,1,0:T(8,128)(2,1)S(1)}, bf16[9,128,128]{2,1,0:T(8,128)(2,1)}, u32[]{:S(2)}) copy-start(bf16[9,128,128]{2,1,0:T(8,128)(2,1)} %copy.50) | copy-start | bytes 884740
  115.4 2.2 %copy-start.5 = (bf16[2048,1152]{1,0:T(8,128)(2,1)}, bf16[2048,1152]{1,0:T(8,128)(2,1)S(1)}, u32[]{:S(2)}) copy-start(bf16[2048,1152]{1,0:T(8,128)(2,1)S(1)} %constant_dynamic-update-slice_fusion.18) | copy-start | bytes 14155780
  125.5 8.2 %copy-start.9 = (f32[1,1152]{1,0:T(1,128)S(1)}, f32[1,1152]{1,0:T(1,128)}, u32[]{:S(2)}) copy-start(f32[1,1152]{1,0:T(1,128)} %param.23) | copy-start | bytes 13828
  125.5 8.2 %copy-start.10 = (f32[1,1152]{1,0:T(1,128)S(1)}, f32[1,1152]{1,0:T(1,128)}, u32[]{:S(2)}) copy-start(f32[1,1152]{1,0:T(1,128)} %param.22) | copy-start | bytes 13828
  125.5 8.2 %copy-start.11 = (f32[1,1152]{1,0:T(1,128)S(1)}, f32[1,1152]{1,0:T(1,128)}, u32[]{:S(2)}) copy-start(f32[1,1152]{1,0:T(1,128)} %param.21) | copy-start | bytes 13828
  127.6 39.0 %all-to-all-start.2 = ((f32[128,2,1152]{2,1,0:T(2,128)}), f32[128,2,1152]{2,1,0:T(2,128)S(1)}, u32[]{:S(2)}, u32[]{:S(2)}) async-start(f32[128,2,1152]{2,1,0:T(2,128)} %maximum_bitcast_fusion), calls=%async_computation.2 | async-start | bytes 2359296 | tf_op jit(solution)/shard_map/all_to_all | solution.py:165
  133.8 4.5 %collective-permute-start = (f32[3,1152]{1,0:T(4,128)S(1)}, f32[3,1152]{1,0:T(4,128)S(1)}, u32[]{:S(2)}, u32[]{:S(2)}) collective-permute-start(f32[3,1152]{1,0:T(4,128)S(1)} %pad_maximum_fusion), channel_id=1, source_target_pairs={{0,1},{1,0},{2,3},{3,2},{4,5},{5,4},{6,7},{7,6},{8,9},{9,8},{10,11... | collective-permute-start | bytes 41480 | tf_op jit(solution)/shard_map/ppermute | solution.py:116
  167.1 4.1 %collective-permute-start.1 = (f32[2,1152]{1,0:T(2,128)S(1)}, f32[2,1152]{1,0:T(2,128)S(1)}, u32[]{:S(2)}, u32[]{:S(2)}) collective-permute-start(f32[2,1152]{1,0:T(2,128)S(1)} %reduce_sum.75), channel_id=1, source_target_pairs={{0,1},{1,0},{2,3},{3,2},{4,5},{5,4},{6,7},{7,6},{8,9},{9,8},{10,11... | collective-permute-start | bytes 27656 | tf_op jit(solution)/shard_map/ppermute | solution.py:173
  172.3 28.7 %all-to-all-start.3 = ((bf16[128,2,1152]{2,1,0:T(2,128)(2,1)}), bf16[128,2,1152]{2,1,0:T(2,128)(2,1)S(1)}, u32[]{:S(2)}, u32[]{:S(2)}) async-start(bf16[128,2,1152]{2,1,0:T(2,128)(2,1)} %broadcast_in_dim.93), calls=%async_computation.3 | async-start | bytes 1179648 | tf_op jit(solution)/shard_map/all_to_all | solution.py:179

commit v2 on v1

--- a/solution.py
+++ b/solution.py
@@ -22,6 +22,33 @@
         ],
         axis=-1,
     )
+
+
+def conv_taps(field, kernel):
+    channels = field.shape[3]
+    return lax.conv_general_dilated(
+        field,
+        kernel.reshape(3, 3, channels, -1),
+        (1, 1),
+        ((1, 1), (1, 1)),
+        dimension_numbers=("NHWC", "HWIO", "NHWC"),
+        preferred_element_type=jnp.float32,
+    )
+
+
+def conv_kernel_grad(field, out_grad):
+    numbers = lax.ConvDimensionNumbers(
+        lhs_spec=(3, 0, 1, 2), rhs_spec=(3, 0, 1, 2), out_spec=(2, 3, 0, 1)
+    )
+    grad = lax.conv_general_dilated(
+        field,
+        out_grad,
+        (1, 1),
+        ((1, 1), (1, 1)),
+        dimension_numbers=numbers,
+        preferred_element_type=jnp.float32,
+    )
+    return grad.reshape(9 * field.shape[3], out_grad.shape[3])
 
 
 def layer_grads(
@@ -36,14 +63,10 @@
 ):
     row_count, grid_side, _, channels = features.shape
     positions = row_count * grid_side * grid_side
-    taps_first = tap_stack(features).reshape(positions, 9 * channels)
-    hidden = jax.nn.relu(jnp.dot(taps_first, w_first, preferred_element_type=jnp.float32)).astype(
-        jnp.bfloat16
-    )
-    taps_second = tap_stack(hidden.reshape(features.shape)).reshape(positions, 9 * channels)
-    summed = features.reshape(positions, channels).astype(jnp.float32) + jnp.dot(
-        taps_second, second_weight, preferred_element_type=jnp.float32
-    )
+    hidden = jax.nn.relu(conv_taps(features, w_first)).astype(jnp.bfloat16)
+    summed = features.reshape(positions, channels).astype(jnp.float32) + conv_taps(
+        hidden, second_weight
+    ).reshape(positions, channels)
     block_out = jax.nn.relu(summed).astype(jnp.bfloat16)
     averaged_embedding = jnp.mean(
         block_out.astype(jnp.float32).reshape(row_count, grid_side * grid_side, channels), axis=1
@@ -72,21 +95,16 @@
         (row_count, grid_side * grid_side, channels),
     ).reshape(positions, channels)
     out_grad = jnp.where(block_out > 0, spread, 0.0).astype(jnp.bfloat16)
-    grad_second = lax.dot_general(
-        taps_second, out_grad, (((0,), (0,)), ((), ())), preferred_element_type=jnp.float32
-    )
+    grad_second = conv_kernel_grad(hidden, out_grad.reshape(features.shape))
     flipped = (
         second_weight.reshape(9, channels, channels)[::-1]
         .transpose(0, 2, 1)
         .reshape(9 * channels, channels)
     )
-    taps_back = tap_stack(out_grad.reshape(features.shape)).reshape(positions, 9 * channels)
     hidden_grad = jnp.where(
-        hidden > 0, jnp.dot(taps_back, flipped, preferred_element_type=jnp.float32), 0.0
+        hidden > 0, conv_taps(out_grad.reshape(features.shape), flipped), 0.0
     ).astype(jnp.bfloat16)
-    grad_first = lax.dot_general(
-        taps_first, hidden_grad, (((0,), (0,)), ((), ())), preferred_element_type=jnp.float32
-    )
+    grad_first = conv_kernel_grad(features, hidden_grad)
     return (grad_first, grad_second)
 
 

time: 203 us -> 169 us (0.83)
  local copies, waits for them, and re-layouts: 56.2 us -> 27 us
  matrix products: 15 us -> 9.63 us
    dot_general x4 -> x0, matrix products: 14.6 us -> none  [the longest x1 7.96 us: layer_grads(): lax.dot_general(taps_first, hidden_grad, (((0,), (0,)), ((), ())), prefer...]
    unnamed x51 -> x21, local copies, waits for them, and re-layouts: 15.5 us -> 1.16 us
    conv_general_dilated x0 -> x4, matrix products: none -> 9.2 us  [the longest x2 6.34 us: conv_kernel_grad(): lax.conv_general_dilated(field, out_grad, (1, 1), ((1, 1), (1, 1)), dimen...]
    slice x3 -> x0, local copies, waits for them, and re-layouts: 8.82 us -> none  [tap_stack(): padded_rows[:, shift_row:shift_row + grid_side, shift_col:shift_col + gri...]
    concatenate x4 -> x0, local copies, waits for them, and re-layouts: 3.19 us -> none  [tap_stack(): jnp.concatenate([padded_rows[:, shift_row:shift_row + grid_side, shift_co...]
  transfers between devices with their start and end apart: 6 -> 6, of which waited for: 6 -> 6; matrix products, arithmetic and copies ran while one was open for 6% -> 7% of each run, Pallas kernels for 0% -> 0%
where the time goes in v2:
time: 169 us; the launch traced here: 168 us
  waiting for transfers between devices  83.9 us (50%)
  starting transfers between devices  39.7 us (23%)
  local copies, waits for them, and re-layouts  27 us (16%)
  matrix products  9.63 us (6%)
  other arithmetic  7.17 us (4%)
    all_to_all x1, waiting for transfers between devices, per_device(): lax.all_to_all(loss_derivative.reshape(2, owners, piece_len).transpose(1,...  28.3 us
    all_to_all x1, waiting for transfers between devices, per_device(): lax.all_to_all(packed, 'dp', split_axis=0, concat_axis=0, tiled=True)  24.7 us
    all_to_all x1, waiting for transfers between devices, per_device(): lax.all_to_all(jnp.broadcast_to(both_layers[None], (owners, 2, piece_len)...  20.7 us
    all_to_all x1, starting transfers between devices, per_device(): lax.all_to_all(request, 'dp', split_axis=0, concat_axis=0, tiled=True)  14.8 us
    all_to_all x1, starting transfers between devices, per_device(): lax.all_to_all(jnp.broadcast_to(both_layers[None], (owners, 2, piece_len)...  7.35 us
    all_to_all x1, waiting for transfers between devices, per_device(): lax.all_to_all(request, 'dp', split_axis=0, concat_axis=0, tiled=True)  7.02 us
    conv_general_dilated x2, matrix products, conv_kernel_grad(): lax.conv_general_dilated(field, out_grad, (1, 1), ((1, 1), (1, 1)), dimen...  6.34 us
    slice x1, local copies, waits for them, and re-layouts, per_device(): second_weight = weights[1].reshape(9 * channels, channels)  6.22 us
  transfers between devices with their start and end apart: 6, of which 6 were waited for; matrix products, arithmetic and copies ran while one was open for 7% of the time, Pallas kernels for 0%

profile of v2, /device:TPU:1, one launch (start us, length us, event | category | flops | bytes accessed | tf_op | source)
XLA Modules:
  0.0 168.4 jit_solution(8943039533358862509)
XLA Ops:
  0.6 0.9 convert_reduce_fusion.1
  2.8 1.9 %gather_fusion = s32[256]{0:T(256)S(1)} fusion(s32[128]{0:T(128)} %param.17, s32[1024]{0:T(1024)S(1)} %pad_clamp_fusion.3), kind=kCustom, calls=%fused_computation.2 | custom fusion | bytes 3072 | tf_op jit(solution)/shard_map/jit(_take)/gather | solution.py:149
  5.5 14.8 %all-to-all-start = ((s32[128,1,2]{2,1,0:T(1,128)}), s32[128,1,2]{2,1,0:T(1,128)S(1)}, u32[]{:S(2)}, u32[]{:S(2)}) async-start(s32[128,1,2]{2,1,0:T(1,128)} %bitcast.4), calls=%async_computation | async-start | bytes 131072 | tf_op jit(solution)/shard_map/all_to_all | solution.py:153
  20.3 3.3 %reshape.160 = bf16[512,2048]{1,0:T(8,128)(2,1)S(1)} reshape(bf16[512,4,4,128]{3,2,1,0:T(4,128)(2,1)} %param.13) | data formatting | bytes 4194304 | tf_op jit(solution)/shard_map/reshape | solution.py:159
  23.9 7.0 %all-to-all-done = s32[128,1,2]{2,1,0:T(1,128)S(1)} async-done(((s32[128,1,2]{2,1,0:T(1,128)}), s32[128,1,2]{2,1,0:T(1,128)S(1)}, u32[]{:S(2)}, u32[]{:S(2)}) %all-to-all-start) | async-done | bytes 1056 | tf_op jit(solution)/shard_map/all_to_all | solution.py:153
  31.2 1.4 gather_fusion.1
  32.5 0.7 reshape.189
  33.4 0.9 gather_fusion.4
  34.3 0.9 gather_fusion.3
  35.1 1.0 broadcast_select_fusion
  36.4 5.0 %concatenate.8 = bf16[128,2,2084]{2,1,0:T(2,128)(2,1)} concatenate(bf16[128,2,2048]{2,1,0:T(2,128)(2,1)S(1)} %broadcast_select_fusion, bf16[128,2,18]{2,1,0:T(2,128)(2,1)S(1)} %get-tuple-element.14, bf16[128,2,18]{2,1,0:T(2,128)(2,1)S(1)} %get-tuple-element.13), dimensions={2} | concatenate | bytes 2134016 | tf_op jit(solution)/shard_map/concatenate | solution.py:157
  41.4 6.0 %all-to-all-start.1 = ((bf16[128,2,2084]{2,1,0:T(2,128)(2,1)}), bf16[128,2,2084]{2,1,0:T(2,128)(2,1)S(1)}, u32[]{:S(2)}, u32[]{:S(2)}) async-start(bf16[128,2,2084]{2,1,0:T(2,128)(2,1)} %concatenate.8), calls=%async_computation.1 | async-start | bytes 2228224 | tf_op jit(solution)/shard_map/all_to_all | solution.py:165
  47.3 6.2 %slice_reduce_fusion = (bf16[147456]{0:T(1024)(128)(2,1)S(1)}, bf16[147456]{0:T(1024)(128)(2,1)S(1)}) fusion(bf16[2,147456]{1,0:T(2,128)(2,1)S(1)} %copy-done.1), kind=kLoop, calls=%fused_computation.25 | loop fusion | bytes 1179648 | tf_op jit(solution)/shard_map/slice | solution.py:130
  53.6 0.7 rev.3
  54.3 24.7 %all-to-all-done.1 = bf16[128,2,2084]{2,1,0:T(2,128)(2,1)S(1)} async-done(((bf16[128,2,2084]{2,1,0:T(2,128)(2,1)}), bf16[128,2,2084]{2,1,0:T(2,128)(2,1)S(1)}, u32[]{:S(2)}, u32[]{:S(2)}) %all-to-all-start.1) | async-done | bytes 1067040 | tf_op jit(solution)/shard_map/all_to_all | solution.py:165
  79.1 0.9 reshape.161
  79.9 1.0 gather_fusion.2
  81.7 1.4 fusion.15
  83.3 1.4 convert_reduce_fusion
  85.7 1.4 fusion.5
  87.1 4.9 %fusion.4 = f32[3,3,128,128]{3,2,1,0:T(8,128)S(1)} fusion(bf16[128,4,4,128]{0,3,2,1:T(8,128)(2,1)S(1)} %bitcast.64, pred[128,4,4,128]{3,0,2,1:T(32,128)(4,1)S(1)} %and_convert_fusion.1, bf16[3,3,128,128]{2,3,1,0:T(8,128)(2,1)S(1)} %bitcast.71, bf16[128,128]{1,0:T(8,128)(2,1)S(1)} %convolution_multiply_fusion, u8[128,4,128]{2,0,1:T(8,128)(4,1)S(1)} %fusion.16), kind=kOutput, calls=%fused_computation.13 | convolution fusion | flops 840695808 | bytes 1769472 | tf_op jit(solution)/shard_map/conv_general_dilated | solution.py:43
  92.0 2.1 %maximum_bitcast_fusion = f32[128,2,1152]{2,1,0:T(2,128)} fusion(f32[1,128,1152]{2,0,1:T(1,128)S(1)} %bitcast.68, f32[1,128,1152]{2,0,1:T(1,128)S(1)} %bitcast.69), kind=kLoop, calls=%fused_computation.14 | loop fusion | flops 294912 | bytes 2359296 | tf_op jit(solution)/shard_map/transpose | solution.py:184
  94.1 6.2 %all-to-all-start.2 = ((f32[128,2,1152]{2,1,0:T(2,128)}), f32[128,2,1152]{2,1,0:T(2,128)S(1)}, u32[]{:S(2)}, u32[]{:S(2)}) async-start(f32[128,2,1152]{2,1,0:T(2,128)} %maximum_bitcast_fusion), calls=%async_computation.2 | async-start | bytes 2359296 | tf_op jit(solution)/shard_map/all_to_all | solution.py:183
  100.4 2.7 %collective-permute-start = (f32[3,1152]{1,0:T(4,128)S(1)}, f32[3,1152]{1,0:T(4,128)S(1)}, u32[]{:S(2)}, u32[]{:S(2)}) collective-permute-start(f32[3,1152]{1,0:T(4,128)S(1)} %pad_maximum_fusion), channel_id=1, source_target_pairs={{0,1},{1,0},{2,3},{3,2},{4,5},{5,4},{6,7},{7,6},{8,9},{9,8},{10,11... | collective-permute-start | bytes 41480 | tf_op jit(solution)/shard_map/ppermute | solution.py:134
  103.1 1.8 %collective-permute-done = f32[3,1152]{1,0:T(4,128)S(1)} collective-permute-done((f32[3,1152]{1,0:T(4,128)S(1)}, f32[3,1152]{1,0:T(4,128)S(1)}, u32[]{:S(2)}, u32[]{:S(2)}) %collective-permute-start) | collective-permute-done | bytes 13856 | tf_op jit(solution)/shard_map/ppermute | solution.py:134
  104.9 28.3 %all-to-all-done.2 = f32[128,2,1152]{2,1,0:T(2,128)S(1)} async-done(((f32[128,2,1152]{2,1,0:T(2,128)}), f32[128,2,1152]{2,1,0:T(2,128)S(1)}, u32[]{:S(2)}, u32[]{:S(2)}) %all-to-all-start.2) | async-done | bytes 1179680 | tf_op jit(solution)/shard_map/all_to_all | solution.py:183
  133.7 2.7 %collective-permute-start.1 = (f32[2,1152]{1,0:T(2,128)S(1)}, f32[2,1152]{1,0:T(2,128)S(1)}, u32[]{:S(2)}, u32[]{:S(2)}) collective-permute-start(f32[2,1152]{1,0:T(2,128)S(1)} %reduce_sum.75), channel_id=1, source_target_pairs={{0,1},{1,0},{2,3},{3,2},{4,5},{5,4},{6,7},{7,6},{8,9},{9,8},{10,11... | collective-permute-start | bytes 27656 | tf_op jit(solution)/shard_map/ppermute | solution.py:191
  136.4 1.3 collective-permute-done.1
  137.8 1.1 broadcast_in_dim.94
  138.9 7.4 %all-to-all-start.3 = ((bf16[128,2,1152]{2,1,0:T(2,128)(2,1)}), bf16[128,2,1152]{2,1,0:T(2,128)(2,1)S(1)}, u32[]{:S(2)}, u32[]{:S(2)}) async-start(bf16[128,2,1152]{2,1,0:T(2,128)(2,1)} %broadcast_in_dim.94), calls=%async_computation.3 | async-start | bytes 1179648 | tf_op jit(solution)/shard_map/all_to_all | solution.py:197
  146.9 20.7 %all-to-all-done.3 = bf16[128,2,1152]{2,1,0:T(2,128)(2,1)S(1)} async-done(((bf16[128,2,1152]{2,1,0:T(2,128)(2,1)}), bf16[128,2,1152]{2,1,0:T(2,128)(2,1)S(1)}, u32[]{:S(2)}, u32[]{:S(2)}) %all-to-all-start.3) | async-done | bytes 589856 | tf_op jit(solution)/shard_map/all_to_all | solution.py:197
  167.6 0.8 copy.57
  (62 shorter events, 5.9 us)
Async XLA Ops:
  0.6 84.6 %copy-start = (bf16[128,18]{0,1:T(8,128)(2,1)S(1)}, bf16[128,18]{0,1:T(8,128)(2,1)}, u32[]{:S(2)}) copy-start(bf16[128,18]{0,1:T(8,128)(2,1)} %param.20) | copy-start | bytes 13828
  5.5 25.4 %all-to-all-start = ((s32[128,1,2]{2,1,0:T(1,128)}), s32[128,1,2]{2,1,0:T(1,128)S(1)}, u32[]{:S(2)}, u32[]{:S(2)}) async-start(s32[128,1,2]{2,1,0:T(1,128)} %bitcast.4), calls=%async_computation | async-start | bytes 131072 | tf_op jit(solution)/shard_map/all_to_all | solution.py:153
  20.3 3.3 %copy-start.4 = (bf16[512,18]{0,1:T(8,128)(2,1)S(1)}, bf16[512,18]{0,1:T(8,128)(2,1)}, u32[]{:S(2)}) copy-start(bf16[512,18]{0,1:T(8,128)(2,1)} %param.15) | copy-start | bytes 55300
  20.3 3.5 %copy-start.5 = (bf16[512,18]{0,1:T(8,128)(2,1)S(1)}, bf16[512,18]{0,1:T(8,128)(2,1)}, u32[]{:S(2)}) copy-start(bf16[512,18]{0,1:T(8,128)(2,1)} %param.14) | copy-start | bytes 55300
  41.4 6.0 %copy-start.1 = (bf16[2,147456]{1,0:T(2,128)(2,1)S(1)}, bf16[2,147456]{1,0:T(2,128)(2,1)}, u32[]{:S(2)}) copy-start(bf16[2,147456]{1,0:T(2,128)(2,1)} %param.19) | copy-start | bytes 1769476
  41.4 37.7 %all-to-all-start.1 = ((bf16[128,2,2084]{2,1,0:T(2,128)(2,1)}), bf16[128,2,2084]{2,1,0:T(2,128)(2,1)S(1)}, u32[]{:S(2)}, u32[]{:S(2)}) async-start(bf16[128,2,2084]{2,1,0:T(2,128)(2,1)} %concatenate.8), calls=%async_computation.1 | async-start | bytes 2228224 | tf_op jit(solution)/shard_map/all_to_all | solution.py:165
  81.4 1.8 %copy-start.3 = (s32[128,20]{0,1:T(8,128)S(1)}, s32[128,20]{0,1:T(8,128)}, u32[]{:S(2)}) copy-start(s32[128,20]{0,1:T(8,128)} %param.18) | copy-start | bytes 30724
  84.9 2.1 %copy-start.2 = (bf16[9,128,128]{2,1,0:T(8,128)(2,1)S(1)}, bf16[9,128,128]{2,1,0:T(8,128)(2,1)}, u32[]{:S(2)}) copy-start(bf16[9,128,128]{2,1,0:T(8,128)(2,1)} %rev.3) | copy-start | bytes 884740
  94.1 6.2 %copy-start.6 = (f32[1,1152]{1,0:T(1,128)S(1)}, f32[1,1152]{1,0:T(1,128)}, u32[]{:S(2)}) copy-start(f32[1,1152]{1,0:T(1,128)} %param.23) | copy-start | bytes 13828
  94.1 6.2 %copy-start.7 = (f32[1,1152]{1,0:T(1,128)S(1)}, f32[1,1152]{1,0:T(1,128)}, u32[]{:S(2)}) copy-start(f32[1,1152]{1,0:T(1,128)} %param.22) | copy-start | bytes 13828
  94.1 6.2 %copy-start.8 = (f32[1,1152]{1,0:T(1,128)S(1)}, f32[1,1152]{1,0:T(1,128)}, u32[]{:S(2)}) copy-start(f32[1,1152]{1,0:T(1,128)} %param.21) | copy-start | bytes 13828
  94.1 39.1 %all-to-all-start.2 = ((f32[128,2,1152]{2,1,0:T(2,128)}), f32[128,2,1152]{2,1,0:T(2,128)S(1)}, u32[]{:S(2)}, u32[]{:S(2)}) async-start(f32[128,2,1152]{2,1,0:T(2,128)} %maximum_bitcast_fusion), calls=%async_computation.2 | async-start | bytes 2359296 | tf_op jit(solution)/shard_map/all_to_all | solution.py:183
  100.4 4.5 %collective-permute-start = (f32[3,1152]{1,0:T(4,128)S(1)}, f32[3,1152]{1,0:T(4,128)S(1)}, u32[]{:S(2)}, u32[]{:S(2)}) collective-permute-start(f32[3,1152]{1,0:T(4,128)S(1)} %pad_maximum_fusion), channel_id=1, source_target_pairs={{0,1},{1,0},{2,3},{3,2},{4,5},{5,4},{6,7},{7,6},{8,9},{9,8},{10,11... | collective-permute-start | bytes 41480 | tf_op jit(solution)/shard_map/ppermute | solution.py:134
  133.7 4.1 %collective-permute-start.1 = (f32[2,1152]{1,0:T(2,128)S(1)}, f32[2,1152]{1,0:T(2,128)S(1)}, u32[]{:S(2)}, u32[]{:S(2)}) collective-permute-start(f32[2,1152]{1,0:T(2,128)S(1)} %reduce_sum.75), channel_id=1, source_target_pairs={{0,1},{1,0},{2,3},{3,2},{4,5},{5,4},{6,7},{7,6},{8,9},{9,8},{10,11... | collective-permute-start | bytes 27656 | tf_op jit(solution)/shard_map/ppermute | solution.py:191
  138.9 28.7 %all-to-all-start.3 = ((bf16[128,2,1152]{2,1,0:T(2,128)(2,1)}), bf16[128,2,1152]{2,1,0:T(2,128)(2,1)S(1)}, u32[]{:S(2)}, u32[]{:S(2)}) async-start(bf16[128,2,1152]{2,1,0:T(2,128)(2,1)} %broadcast_in_dim.94), calls=%async_computation.3 | async-start | bytes 1179648 | tf_op jit(solution)/shard_map/all_to_all | solution.py:197

commit v3 on v2

--- a/solution.py
+++ b/solution.py
@@ -152,21 +152,30 @@
     row_index = jnp.maximum(
         lax.all_to_all(request, "dp", split_axis=0, concat_axis=0, tiled=True), 0
     )
-    row_width = replay_rows.shape[1] * replay_rows.shape[2] * channels
+    cells = replay_rows.shape[1] * replay_rows.shape[2]
     actions_n = qvalues.shape[1]
+    side = jnp.concatenate(
+        [
+            jnp.take(qvalues, row_index, axis=0),
+            jnp.take(target_logits, row_index, axis=0),
+            jnp.zeros(row_index.shape + (channels - 2 * actions_n,), qvalues.dtype),
+        ],
+        axis=-1,
+    )
     packed = jnp.concatenate(
         [
-            jnp.take(replay_rows.reshape(-1, row_width), row_index, axis=0),
-            jnp.take(qvalues, row_index, axis=0),
-            jnp.take(target_logits, row_index, axis=0),
+            jnp.take(replay_rows.reshape(-1, cells, channels), row_index, axis=0),
+            side[:, :, None, :],
         ],
-        axis=-1,
+        axis=2,
     )
     slots = lax.all_to_all(packed, "dp", split_axis=0, concat_axis=0, tiled=True)
-    picked = jnp.take(slots.reshape(owners * capacity, -1), slot_index, axis=0)
-    features = picked[:, :row_width].reshape((rows_dev,) + replay_rows.shape[1:])
-    move_return_estimates = picked[:, row_width : row_width + actions_n]
-    reference_policy_entries = picked[:, row_width + actions_n :]
+    picked = jnp.take(
+        slots.reshape((owners * capacity,) + slots.shape[2:]), slot_index, axis=0
+    )
+    features = picked[:, :cells].reshape((rows_dev,) + replay_rows.shape[1:])
+    move_return_estimates = picked[:, cells, :actions_n]
+    reference_policy_entries = picked[:, cells, actions_n : 2 * actions_n]
     row_scale = jnp.full((rows_dev,), 1.0 / learn_rows, jnp.float32)
     grad_first, grad_second = layer_grads(
         features,

time: 169 us -> 183 us (1.083)
  matrix products: 9.63 us -> 15.9 us
  other arithmetic: 7.17 us -> 12.9 us
    conv_general_dilated x2, matrix products: 6.34 us -> 9.82 us  [conv_kernel_grad(): lax.conv_general_dilated(field, out_grad, (1, 1), ((1, 1), (1, 1)), dimen...]
    all_to_all x1, waiting for transfers between devices: 7.02 us -> 10.3 us  [per_device(): lax.all_to_all(request, 'dp', split_axis=0, concat_axis=0, tiled=True)]
    reshape x3 -> x1, local copies, waits for them, and re-layouts: 4.46 us -> 1.33 us  [layer_grads(): summed = features.reshape(positions, channels).astype(jnp.float32) + conv...]
    concatenate x1 -> x2, local copies, waits for them, and re-layouts: 4.98 us -> 1.96 us  [the longest x1 1.89 us: per_device(): jnp.concatenate([jnp.take(replay_rows.reshape(-1, cells, channels), row_i...]
    all_to_all x1, waiting for transfers between devices: 24.7 us -> 22.8 us  [per_device(): lax.all_to_all(packed, 'dp', split_axis=0, concat_axis=0, tiled=True)]
    slice x1, local copies, waits for them, and re-layouts: 6.22 us -> 8.15 us  [per_device(): second_weight = weights[1].reshape(9 * channels, channels)]
    gather x4 -> x3, local copies, waits for them, and re-layouts: 3.35 us -> 4.22 us  [the longest x2 3.38 us: per_device(): jnp.take(slots.reshape((owners * capacity,) + slots.shape[2:]), slot_inde...]
  transfers between devices with their start and end apart: 6 -> 6, of which waited for: 6 -> 6; matrix products, arithmetic and copies ran while one was open for 7% -> 5% of each run, Pallas kernels for 0% -> 0%
where the time goes in v3:
time: 183 us; the launch traced here: 182 us
  waiting for transfers between devices  85.2 us (47%)
  starting transfers between devices  39.5 us (22%)
  local copies, waits for them, and re-layouts  27.8 us (15%)
  matrix products  15.9 us (9%)
  other arithmetic  12.9 us (7%)
    all_to_all x1, waiting for transfers between devices, per_device(): lax.all_to_all(loss_derivative.reshape(2, owners, piece_len).transpose(1,...  28.3 us
    all_to_all x1, waiting for transfers between devices, per_device(): lax.all_to_all(packed, 'dp', split_axis=0, concat_axis=0, tiled=True)  22.8 us
    all_to_all x1, waiting for transfers between devices, per_device(): lax.all_to_all(jnp.broadcast_to(both_layers[None], (owners, 2, piece_len)...  20.7 us
    all_to_all x1, starting transfers between devices, per_device(): lax.all_to_all(request, 'dp', split_axis=0, concat_axis=0, tiled=True)  14.8 us
    all_to_all x1, waiting for transfers between devices, per_device(): lax.all_to_all(request, 'dp', split_axis=0, concat_axis=0, tiled=True)  10.3 us
    conv_general_dilated x2, matrix products, conv_kernel_grad(): lax.conv_general_dilated(field, out_grad, (1, 1), ((1, 1), (1, 1)), dimen...  9.82 us
    slice x1, local copies, waits for them, and re-layouts, per_device(): second_weight = weights[1].reshape(9 * channels, channels)  8.15 us
    all_to_all x1, starting transfers between devices, per_device(): lax.all_to_all(jnp.broadcast_to(both_layers[None], (owners, 2, piece_len)...  7.35 us
  transfers between devices with their start and end apart: 6, of which 6 were waited for; matrix products, arithmetic and copies ran while one was open for 5% of the time, Pallas kernels for 0%

profile of v3, /device:TPU:1, one launch (start us, length us, event | category | flops | bytes accessed | tf_op | source)
XLA Modules:
  0.0 182.4 jit_solution(12177869045352475085)
XLA Ops:
  0.7 1.0 convert_reduce_fusion.1
  2.7 1.9 %gather_fusion = s32[256]{0:T(256)S(1)} fusion(s32[128]{0:T(128)} %param.17, s32[1024]{0:T(1024)S(1)} %pad_clamp_fusion.3), kind=kCustom, calls=%fused_computation.2 | custom fusion | bytes 3072 | tf_op jit(solution)/shard_map/jit(_take)/gather | solution.py:149
  5.6 14.8 %all-to-all-start = ((s32[128,1,2]{2,1,0:T(1,128)}), s32[128,1,2]{2,1,0:T(1,128)S(1)}, u32[]{:S(2)}, u32[]{:S(2)}) async-start(s32[128,1,2]{2,1,0:T(1,128)} %bitcast.4), calls=%async_computation | async-start | bytes 131072 | tf_op jit(solution)/shard_map/all_to_all | solution.py:153
  20.8 10.3 %all-to-all-done = s32[128,1,2]{2,1,0:T(1,128)S(1)} async-done(((s32[128,1,2]{2,1,0:T(1,128)}), s32[128,1,2]{2,1,0:T(1,128)S(1)}, u32[]{:S(2)}, u32[]{:S(2)}) %all-to-all-start) | async-done | bytes 1056 | tf_op jit(solution)/shard_map/all_to_all | solution.py:153
  35.2 1.9 %copy.77 = bf16[128,2,17,128]{3,1,2,0:T(2,128)(2,1)} copy(bf16[128,2,17,128]{3,2,1,0:T(8,128)(2,1)S(1)} %pad_maximum_fusion) | data formatting | bytes 2228224 | tf_op jit(solution)/shard_map/concatenate | solution.py:165
  37.1 5.8 %all-to-all-start.1 = ((bf16[128,2,17,128]{3,1,2,0:T(2,128)(2,1)}), bf16[128,2,17,128]{3,1,2,0:T(2,128)(2,1)S(1)}, u32[]{:S(2)}, u32[]{:S(2)}) async-start(bf16[128,2,17,128]{3,1,2,0:T(2,128)(2,1)} %copy.77), calls=%async_computation.1 | async-start | bytes 2228224 | tf_op jit(solution)/shard_map/all_to_all | solution.py:172
  42.9 8.1 %slice_reduce_fusion = (bf16[147456]{0:T(1024)(128)(2,1)S(1)}, bf16[147456]{0:T(1024)(128)(2,1)}) fusion(bf16[2,147456]{1,0:T(2,128)(2,1)} %param.19), kind=kLoop, calls=%fused_computation.25 | loop fusion | bytes 1179648 | tf_op jit(solution)/shard_map/slice | solution.py:130
  51.9 22.8 %all-to-all-done.1 = bf16[128,2,17,128]{3,1,2,0:T(2,128)(2,1)S(1)} async-done(((bf16[128,2,17,128]{3,1,2,0:T(2,128)(2,1)}), bf16[128,2,17,128]{3,1,2,0:T(2,128)(2,1)S(1)}, u32[]{:S(2)}, u32[]{:S(2)}) %all-to-all-start.1) | async-done | bytes 1114144 | tf_op jit(solution)/shard_map/all_to_all | solution.py:172
  74.7 1.4 copy.78
  76.1 2.2 %gather_fusion.2 = bf16[128,17,128]{2,1,0:T(8,128)(2,1)S(1)} fusion(bf16[256,17,128]{2,1,0:T(8,128)(2,1)} %bitcast.82, s32[1024]{0:T(1024)S(1)} %pad_clamp_fusion), kind=kCustom, calls=%fused_computation.4 | custom fusion | bytes 1114624 | tf_op jit(solution)/shard_map/jit(_take)/gather | solution.py:173
  78.3 1.2 copy.79
  79.5 1.1 broadcast_select_fusion.1
  81.5 1.0 copy.80
  82.5 2.1 %fusion.13 = (u8[128,4,128]{2,0,1:T(8,128)(4,1)}, bf16[128,4,4,128]{3,0,2,1:T(8,128)(2,1)S(1)}) fusion(bf16[128,4,4,128]{0,3,2,1:T(8,128)(2,1)S(1)} %bitcast.87, bf16[3,3,128,128]{3,2,1,0:T(8,128)(2,1)S(1)} %bitcast.94), kind=kOutput, calls=%fused_computation.34 | convolution fusion | flops 421724160 | bytes 1409024 | tf_op jit(solution)/shard_map/conv_general_dilated | solution.py:29
  84.5 2.1 %fusion.14 = (u8[128,4,128]{2,0,1:T(8,128)(4,1)}, f32[128,4,4,128]{3,0,2,1:T(8,128)S(1)}) fusion(bf16[128,4,4,128]{3,0,2,1:T(8,128)(2,1)S(1)} %bitcast.83, bf16[128,4,4,128]{3,0,2,1:T(8,128)(2,1)S(1)} %get-tuple-element.20, bf16[3,3,128,128]{3,2,1,0:T(8,128)(2,1)S(1)} %bitcast.85), kind=kOutput, calls=%fused_computation.35 | convolution fusion | flops 422248448 | bytes 2457600 | tf_op jit(solution)/shard_map/conv_general_dilated | solution.py:29
  86.6 1.3 copy.81
  87.9 1.6 convert_reduce_fusion
  90.4 1.8 and_convert_fusion.1
  92.2 1.0 fusion.65
  93.9 1.0 convolution_multiply_fusion
  94.9 3.1 %fusion.3 = f32[3,3,128,128]{3,2,1,0:T(8,128)} fusion(bf16[128,4,4,128]{3,0,2,1:T(8,128)(2,1)S(1)} %copy-done.4, bf16[128,128]{1,0:T(8,128)(2,1)S(1)} %convolution_multiply_fusion, u8[128,4,128]{2,0,1:T(8,128)(4,1)} %get-tuple-element.17), kind=kOutput, calls=%fused_computation.24 | convolution fusion | flops 420741120 | bytes 1212416 | tf_op jit(solution)/shard_map/conv_general_dilated | solution.py:43
  98.0 6.8 %fusion.2 = f32[3,3,128,128]{3,2,1,0:T(8,128)} fusion(bf16[128,4,4,128]{0,3,2,1:T(8,128)(2,1)S(1)} %bitcast.88, pred[128,4,4,128]{3,0,2,1:T(32,128)(4,1)} %and_convert_fusion.1, bf16[3,3,128,128]{2,3,1,0:T(8,128)(2,1)S(1)} %bitcast.95, bf16[128,128]{1,0:T(8,128)(2,1)} %copy-done.17, u8[128,4,128]{2,0,1:T(8,128)(4,1)S(1)} %copy-done.9), kind=kOutput, calls=%fused_computation.10 | convolution fusion | flops 840695808 | bytes 1769472 | tf_op jit(solution)/shard_map/conv_general_dilated | solution.py:43
  104.8 3.3 %maximum_bitcast_fusion = f32[128,2,1152]{2,1,0:T(2,128)} fusion(f32[1,128,1152]{2,0,1:T(1,128)} %bitcast.92, f32[1,128,1152]{2,0,1:T(1,128)} %bitcast.93), kind=kLoop, calls=%fused_computation.11 | loop fusion | flops 294912 | bytes 2359296 | tf_op jit(solution)/shard_map/transpose | solution.py:193
  108.1 6.2 %all-to-all-start.2 = ((f32[128,2,1152]{2,1,0:T(2,128)}), f32[128,2,1152]{2,1,0:T(2,128)S(1)}, u32[]{:S(2)}, u32[]{:S(2)}) async-start(f32[128,2,1152]{2,1,0:T(2,128)} %maximum_bitcast_fusion), calls=%async_computation.2 | async-start | bytes 2359296 | tf_op jit(solution)/shard_map/all_to_all | solution.py:192
  114.3 2.7 %collective-permute-start = (f32[3,1152]{1,0:T(4,128)S(1)}, f32[3,1152]{1,0:T(4,128)S(1)}, u32[]{:S(2)}, u32[]{:S(2)}) collective-permute-start(f32[3,1152]{1,0:T(4,128)S(1)} %pad_maximum_fusion.1), channel_id=1, source_target_pairs={{0,1},{1,0},{2,3},{3,2},{4,5},{5,4},{6,7},{7,6},{8,9},{9,8},{10,11... | collective-permute-start | bytes 41480 | tf_op jit(solution)/shard_map/ppermute | solution.py:134
  117.1 1.8 collective-permute-done
  118.8 28.3 %all-to-all-done.2 = f32[128,2,1152]{2,1,0:T(2,128)S(1)} async-done(((f32[128,2,1152]{2,1,0:T(2,128)}), f32[128,2,1152]{2,1,0:T(2,128)S(1)}, u32[]{:S(2)}, u32[]{:S(2)}) %all-to-all-start.2) | async-done | bytes 1179680 | tf_op jit(solution)/shard_map/all_to_all | solution.py:192
  147.6 2.7 %collective-permute-start.1 = (f32[2,1152]{1,0:T(2,128)S(1)}, f32[2,1152]{1,0:T(2,128)S(1)}, u32[]{:S(2)}, u32[]{:S(2)}) collective-permute-start(f32[2,1152]{1,0:T(2,128)S(1)} %reduce_sum.75), channel_id=1, source_target_pairs={{0,1},{1,0},{2,3},{3,2},{4,5},{5,4},{6,7},{7,6},{8,9},{9,8},{10,11... | collective-permute-start | bytes 27656 | tf_op jit(solution)/shard_map/ppermute | solution.py:200
  150.4 1.3 collective-permute-done.1
  151.7 1.1 broadcast_in_dim.102
  152.9 7.4 %all-to-all-start.3 = ((bf16[128,2,1152]{2,1,0:T(2,128)(2,1)}), bf16[128,2,1152]{2,1,0:T(2,128)(2,1)S(1)}, u32[]{:S(2)}, u32[]{:S(2)}) async-start(bf16[128,2,1152]{2,1,0:T(2,128)(2,1)} %broadcast_in_dim.102), calls=%async_computation.3 | async-start | bytes 1179648 | tf_op jit(solution)/shard_map/all_to_all | solution.py:206
  160.8 20.7 %all-to-all-done.3 = bf16[128,2,1152]{2,1,0:T(2,128)(2,1)S(1)} async-done(((bf16[128,2,1152]{2,1,0:T(2,128)(2,1)}), bf16[128,2,1152]{2,1,0:T(2,128)(2,1)S(1)}, u32[]{:S(2)}, u32[]{:S(2)}) %all-to-all-start.3) | async-done | bytes 589856 | tf_op jit(solution)/shard_map/all_to_all | solution.py:206
  (86 shorter events, 11.7 us)
Async XLA Ops:
  0.6 32.9 %copy-start = (bf16[512,4,4,128]{3,2,1,0:T(4,128)(2,1)S(1)}, bf16[512,4,4,128]{3,2,1,0:T(4,128)(2,1)}, u32[]{:S(2)}) copy-start(bf16[512,4,4,128]{3,2,1,0:T(4,128)(2,1)} %param.13) | copy-start | bytes 6291460
  0.6 19.7 %copy-start.11 = (bf16[512,18]{0,1:T(8,128)(2,1)S(1)}, bf16[512,18]{0,1:T(8,128)(2,1)}, u32[]{:S(2)}) copy-start(bf16[512,18]{0,1:T(8,128)(2,1)} %param.15) | copy-start | bytes 55300
  0.7 19.9 %copy-start.12 = (bf16[512,18]{0,1:T(8,128)(2,1)S(1)}, bf16[512,18]{0,1:T(8,128)(2,1)}, u32[]{:S(2)}) copy-start(bf16[512,18]{0,1:T(8,128)(2,1)} %param.14) | copy-start | bytes 55300
  5.6 25.4 %all-to-all-start = ((s32[128,1,2]{2,1,0:T(1,128)}), s32[128,1,2]{2,1,0:T(1,128)S(1)}, u32[]{:S(2)}, u32[]{:S(2)}) async-start(s32[128,1,2]{2,1,0:T(1,128)} %bitcast.4), calls=%async_computation | async-start | bytes 131072 | tf_op jit(solution)/shard_map/all_to_all | solution.py:153
  37.1 37.6 %all-to-all-start.1 = ((bf16[128,2,17,128]{3,1,2,0:T(2,128)(2,1)}), bf16[128,2,17,128]{3,1,2,0:T(2,128)(2,1)S(1)}, u32[]{:S(2)}, u32[]{:S(2)}) async-start(bf16[128,2,17,128]{3,1,2,0:T(2,128)(2,1)} %copy.77), calls=%async_computation.1 | async-start | bytes 2228224 | tf_op jit(solution)/shard_map/all_to_all | solution.py:172
  79.5 3.0 %copy-start.7 = (bf16[147456]{0:T(1024)(128)(2,1)S(1)}, bf16[147456]{0:T(1024)(128)(2,1)}, u32[]{:S(2)}) copy-start(bf16[147456]{0:T(1024)(128)(2,1)} %get-tuple-element.4) | copy-start | bytes 884740
  80.6 0.8 copy-start.1
  81.4 3.1 %copy-start.5 = (bf16[128,16,128]{0,2,1:T(8,128)(2,1)}, bf16[128,16,128]{0,2,1:T(8,128)(2,1)S(1)}, u32[]{:S(2)}) copy-start(bf16[128,16,128]{0,2,1:T(8,128)(2,1)S(1)} %slice.43) | copy-start | bytes 1572868
  82.5 2.1 %copy-start.2 = (bf16[128,16,128]{2,0,1:T(8,128)(2,1)S(1)}, bf16[128,16,128]{2,0,1:T(8,128)(2,1)}, u32[]{:S(2)}) copy-start(bf16[128,16,128]{2,0,1:T(8,128)(2,1)} %copy.80) | copy-start | bytes 1572868
  84.5 2.1 %copy-start.3 = (bf16[128,4,4,128]{3,0,2,1:T(8,128)(2,1)}, bf16[128,4,4,128]{3,0,2,1:T(8,128)(2,1)S(1)}, u32[]{:S(2)}) copy-start(bf16[128,4,4,128]{3,0,2,1:T(8,128)(2,1)S(1)} %get-tuple-element.20) | copy-start | bytes 1572868
  86.6 3.6 %copy-start.10 = (s32[128,20]{0,1:T(8,128)S(1)}, s32[128,20]{0,1:T(8,128)}, u32[]{:S(2)}) copy-start(s32[128,20]{0,1:T(8,128)} %param.18) | copy-start | bytes 30724
  87.9 4.2 %copy-start.13 = (bf16[128,18]{0,1:T(8,128)(2,1)S(1)}, bf16[128,18]{0,1:T(8,128)(2,1)}, u32[]{:S(2)}) copy-start(bf16[128,18]{0,1:T(8,128)(2,1)} %param.20) | copy-start | bytes 13828
  87.9 7.0 %copy-start.4 = (bf16[128,4,4,128]{3,0,2,1:T(8,128)(2,1)S(1)}, bf16[128,4,4,128]{3,0,2,1:T(8,128)(2,1)}, u32[]{:S(2)}) copy-start(bf16[128,4,4,128]{3,0,2,1:T(8,128)(2,1)} %copy-done.3) | copy-start | bytes 1572868
  89.5 8.5 %copy-start.6 = (bf16[128,16,128]{0,2,1:T(8,128)(2,1)S(1)}, bf16[128,16,128]{0,2,1:T(8,128)(2,1)}, u32[]{:S(2)}) copy-start(bf16[128,16,128]{0,2,1:T(8,128)(2,1)} %copy-done.5) | copy-start | bytes 1572868
  89.5 8.5 %copy-start.8 = (bf16[9,128,128]{2,1,0:T(8,128)(2,1)S(1)}, bf16[9,128,128]{2,1,0:T(8,128)(2,1)}, u32[]{:S(2)}) copy-start(bf16[9,128,128]{2,1,0:T(8,128)(2,1)} %rev.3) | copy-start | bytes 884740
  90.2 7.7 %copy-start.9 = (u8[128,4,128]{2,0,1:T(8,128)(4,1)S(1)}, u8[128,4,128]{2,0,1:T(8,128)(4,1)}, u32[]{:S(2)}) copy-start(u8[128,4,128]{2,0,1:T(8,128)(4,1)} %get-tuple-element.17) | copy-start | bytes 196612
  94.9 3.1 %copy-start.17 = (bf16[128,128]{1,0:T(8,128)(2,1)}, bf16[128,128]{1,0:T(8,128)(2,1)S(1)}, u32[]{:S(2)}) copy-start(bf16[128,128]{1,0:T(8,128)(2,1)S(1)} %convolution_multiply_fusion) | copy-start | bytes 98308
  108.1 6.2 %copy-start.14 = (f32[1,1152]{1,0:T(1,128)S(1)}, f32[1,1152]{1,0:T(1,128)}, u32[]{:S(2)}) copy-start(f32[1,1152]{1,0:T(1,128)} %param.23) | copy-start | bytes 13828
  108.1 6.2 %copy-start.15 = (f32[1,1152]{1,0:T(1,128)S(1)}, f32[1,1152]{1,0:T(1,128)}, u32[]{:S(2)}) copy-start(f32[1,1152]{1,0:T(1,128)} %param.22) | copy-start | bytes 13828
  108.1 6.2 %copy-start.16 = (f32[1,1152]{1,0:T(1,128)S(1)}, f32[1,1152]{1,0:T(1,128)}, u32[]{:S(2)}) copy-start(f32[1,1152]{1,0:T(1,128)} %param.21) | copy-start | bytes 13828
  108.1 39.1 %all-to-all-start.2 = ((f32[128,2,1152]{2,1,0:T(2,128)}), f32[128,2,1152]{2,1,0:T(2,128)S(1)}, u32[]{:S(2)}, u32[]{:S(2)}) async-start(f32[128,2,1152]{2,1,0:T(2,128)} %maximum_bitcast_fusion), calls=%async_computation.2 | async-start | bytes 2359296 | tf_op jit(solution)/shard_map/all_to_all | solution.py:192
  114.3 4.5 %collective-permute-start = (f32[3,1152]{1,0:T(4,128)S(1)}, f32[3,1152]{1,0:T(4,128)S(1)}, u32[]{:S(2)}, u32[]{:S(2)}) collective-permute-start(f32[3,1152]{1,0:T(4,128)S(1)} %pad_maximum_fusion.1), channel_id=1, source_target_pairs={{0,1},{1,0},{2,3},{3,2},{4,5},{5,4},{6,7},{7,6},{8,9},{9,8},{10,11... | collective-permute-start | bytes 41480 | tf_op jit(solution)/shard_map/ppermute | solution.py:134
  147.6 4.1 %collective-permute-start.1 = (f32[2,1152]{1,0:T(2,128)S(1)}, f32[2,1152]{1,0:T(2,128)S(1)}, u32[]{:S(2)}, u32[]{:S(2)}) collective-permute-start(f32[2,1152]{1,0:T(2,128)S(1)} %reduce_sum.75), channel_id=1, source_target_pairs={{0,1},{1,0},{2,3},{3,2},{4,5},{5,4},{6,7},{7,6},{8,9},{9,8},{10,11... | collective-permute-start | bytes 27656 | tf_op jit(solution)/shard_map/ppermute | solution.py:200
  152.9 28.7 %all-to-all-start.3 = ((bf16[128,2,1152]{2,1,0:T(2,128)(2,1)}), bf16[128,2,1152]{2,1,0:T(2,128)(2,1)S(1)}, u32[]{:S(2)}, u32[]{:S(2)}) async-start(bf16[128,2,1152]{2,1,0:T(2,128)(2,1)} %broadcast_in_dim.102), calls=%async_computation.3 | async-start | bytes 1179648 | tf_op jit(solution)/shard_map/all_to_all | solution.py:206

commit v4 on v2

--- a/solution.py
+++ b/solution.py
@@ -154,19 +154,22 @@
     )
     row_width = replay_rows.shape[1] * replay_rows.shape[2] * channels
     actions_n = qvalues.shape[1]
-    packed = jnp.concatenate(
+    side = jnp.concatenate(
         [
-            jnp.take(replay_rows.reshape(-1, row_width), row_index, axis=0),
             jnp.take(qvalues, row_index, axis=0),
             jnp.take(target_logits, row_index, axis=0),
+            jnp.zeros(row_index.shape + (channels - 2 * actions_n,), qvalues.dtype),
         ],
         axis=-1,
+    )
+    packed = jnp.concatenate(
+        [jnp.take(replay_rows.reshape(-1, row_width), row_index, axis=0), side], axis=-1
     )
     slots = lax.all_to_all(packed, "dp", split_axis=0, concat_axis=0, tiled=True)
     picked = jnp.take(slots.reshape(owners * capacity, -1), slot_index, axis=0)
     features = picked[:, :row_width].reshape((rows_dev,) + replay_rows.shape[1:])
     move_return_estimates = picked[:, row_width : row_width + actions_n]
-    reference_policy_entries = picked[:, row_width + actions_n :]
+    reference_policy_entries = picked[:, row_width + actions_n : row_width + 2 * actions_n]
     row_scale = jnp.full((rows_dev,), 1.0 / learn_rows, jnp.float32)
     grad_first, grad_second = layer_grads(
         features,

time: 169 us -> 169 us (level)
  no operation moved by 1% of the time
where the time goes in v4:
time: 169 us; the launch traced here: 168 us
  waiting for transfers between devices  83.7 us (50%)
  starting transfers between devices  39.9 us (24%)
  local copies, waits for them, and re-layouts  26.9 us (16%)
  matrix products  9.62 us (6%)
  other arithmetic  7.13 us (4%)
    all_to_all x1, waiting for transfers between devices, per_device(): lax.all_to_all(loss_derivative.reshape(2, owners, piece_len).transpose(1,...  27.9 us
    all_to_all x1, waiting for transfers between devices, per_device(): lax.all_to_all(packed, 'dp', split_axis=0, concat_axis=0, tiled=True)  24.7 us
    all_to_all x1, waiting for transfers between devices, per_device(): lax.all_to_all(jnp.broadcast_to(both_layers[None], (owners, 2, piece_len)...  20.7 us
    all_to_all x1, starting transfers between devices, per_device(): lax.all_to_all(request, 'dp', split_axis=0, concat_axis=0, tiled=True)  14.8 us
    all_to_all x1, starting transfers between devices, per_device(): lax.all_to_all(jnp.broadcast_to(both_layers[None], (owners, 2, piece_len)...  7.35 us
    all_to_all x1, waiting for transfers between devices, per_device(): lax.all_to_all(request, 'dp', split_axis=0, concat_axis=0, tiled=True)  7.02 us
    conv_general_dilated x2, matrix products, conv_kernel_grad(): lax.conv_general_dilated(field, out_grad, (1, 1), ((1, 1), (1, 1)), dimen...  6.34 us
    slice x1, local copies, waits for them, and re-layouts, per_device(): second_weight = weights[1].reshape(9 * channels, channels)  6.22 us
  transfers between devices with their start and end apart: 6, of which 6 were waited for; matrix products, arithmetic and copies ran while one was open for 7% of the time, Pallas kernels for 0%

profile of v4, /device:TPU:1, one launch (start us, length us, event | category | flops | bytes accessed | tf_op | source)
XLA Modules:
  0.0 168.3 jit_solution(6264889399915532213)
XLA Ops:
  0.6 0.9 convert_reduce_fusion.1
  1.6 0.7 compare_and_fusion.1
  2.8 1.9 %gather_fusion = s32[256]{0:T(256)S(1)} fusion(s32[128]{0:T(128)} %param.17, s32[1024]{0:T(1024)S(1)} %pad_clamp_fusion.3), kind=kCustom, calls=%fused_computation.2 | custom fusion | bytes 3072 | tf_op jit(solution)/shard_map/jit(_take)/gather | solution.py:149
  5.5 14.8 %all-to-all-start = ((s32[128,1,2]{2,1,0:T(1,128)}), s32[128,1,2]{2,1,0:T(1,128)S(1)}, u32[]{:S(2)}, u32[]{:S(2)}) async-start(s32[128,1,2]{2,1,0:T(1,128)} %bitcast.4), calls=%async_computation | async-start | bytes 131072 | tf_op jit(solution)/shard_map/all_to_all | solution.py:153
  20.3 3.3 %reshape.160 = bf16[512,2048]{1,0:T(8,128)(2,1)S(1)} reshape(bf16[512,4,4,128]{3,2,1,0:T(4,128)(2,1)} %param.13) | data formatting | bytes 4194304 | tf_op jit(solution)/shard_map/reshape | solution.py:166
  23.9 7.0 %all-to-all-done = s32[128,1,2]{2,1,0:T(1,128)S(1)} async-done(((s32[128,1,2]{2,1,0:T(1,128)}), s32[128,1,2]{2,1,0:T(1,128)S(1)}, u32[]{:S(2)}, u32[]{:S(2)}) %all-to-all-start) | async-done | bytes 1056 | tf_op jit(solution)/shard_map/all_to_all | solution.py:153
  31.2 1.4 gather_fusion.1
  32.5 0.7 reshape.189
  33.4 0.9 gather_fusion.4
  34.3 0.9 gather_fusion.3
  35.1 1.0 broadcast_select_fusion
  36.4 5.3 %concatenate.8 = bf16[128,2,2176]{2,1,0:T(2,128)(2,1)} concatenate(bf16[128,2,2048]{2,1,0:T(2,128)(2,1)S(1)} %broadcast_select_fusion, bf16[128,2,18]{2,1,0:T(2,128)(2,1)S(1)} %get-tuple-element.14, bf16[128,2,18]{2,1,0:T(2,128)(2,1)S(1)} %get-tuple-element.13, bf16[128,2,92]{2,1,0:T(2,128)(2,1)S(1)} %broadcast_in_dim.94), dimensions={2} | concatenate | bytes 2228224 | tf_op jit(solution)/shard_map/concatenate | solution.py:165
  41.7 6.0 %all-to-all-start.1 = ((bf16[128,2,2176]{2,1,0:T(2,128)(2,1)}), bf16[128,2,2176]{2,1,0:T(2,128)(2,1)S(1)}, u32[]{:S(2)}, u32[]{:S(2)}) async-start(bf16[128,2,2176]{2,1,0:T(2,128)(2,1)} %concatenate.8), calls=%async_computation.1 | async-start | bytes 2228224 | tf_op jit(solution)/shard_map/all_to_all | solution.py:168
  47.7 6.2 %slice_reduce_fusion = (bf16[147456]{0:T(1024)(128)(2,1)S(1)}, bf16[147456]{0:T(1024)(128)(2,1)S(1)}) fusion(bf16[2,147456]{1,0:T(2,128)(2,1)S(1)} %copy-done.1), kind=kLoop, calls=%fused_computation.25 | loop fusion | bytes 1179648 | tf_op jit(solution)/shard_map/slice | solution.py:130
  53.9 0.7 rev.3
  54.6 24.7 %all-to-all-done.1 = bf16[128,2,2176]{2,1,0:T(2,128)(2,1)S(1)} async-done(((bf16[128,2,2176]{2,1,0:T(2,128)(2,1)}), bf16[128,2,2176]{2,1,0:T(2,128)(2,1)S(1)}, u32[]{:S(2)}, u32[]{:S(2)}) %all-to-all-start.1) | async-done | bytes 1114144 | tf_op jit(solution)/shard_map/all_to_all | solution.py:168
  79.8 1.0 gather_fusion.2
  81.6 1.4 fusion.15
  83.2 1.4 convert_reduce_fusion
  85.6 1.4 fusion.5
  87.0 4.9 %fusion.4 = f32[3,3,128,128]{3,2,1,0:T(8,128)S(1)} fusion(bf16[128,4,4,128]{0,3,2,1:T(8,128)(2,1)S(1)} %bitcast.64, pred[128,4,4,128]{3,0,2,1:T(32,128)(4,1)S(1)} %and_convert_fusion.1, bf16[3,3,128,128]{2,3,1,0:T(8,128)(2,1)S(1)} %bitcast.71, bf16[128,128]{1,0:T(8,128)(2,1)S(1)} %convolution_multiply_fusion, u8[128,4,128]{2,0,1:T(8,128)(4,1)S(1)} %fusion.16), kind=kOutput, calls=%fused_computation.13 | convolution fusion | flops 840695808 | bytes 1769472 | tf_op jit(solution)/shard_map/conv_general_dilated | solution.py:43
  91.9 2.1 %maximum_bitcast_fusion = f32[128,2,1152]{2,1,0:T(2,128)} fusion(f32[1,128,1152]{2,0,1:T(1,128)S(1)} %bitcast.68, f32[1,128,1152]{2,0,1:T(1,128)S(1)} %bitcast.69), kind=kLoop, calls=%fused_computation.14 | loop fusion | flops 294912 | bytes 2359296 | tf_op jit(solution)/shard_map/transpose | solution.py:187
  94.0 6.2 %all-to-all-start.2 = ((f32[128,2,1152]{2,1,0:T(2,128)}), f32[128,2,1152]{2,1,0:T(2,128)S(1)}, u32[]{:S(2)}, u32[]{:S(2)}) async-start(f32[128,2,1152]{2,1,0:T(2,128)} %maximum_bitcast_fusion), calls=%async_computation.2 | async-start | bytes 2359296 | tf_op jit(solution)/shard_map/all_to_all | solution.py:186
  100.3 2.9 %collective-permute-start = (f32[3,1152]{1,0:T(4,128)S(1)}, f32[3,1152]{1,0:T(4,128)S(1)}, u32[]{:S(2)}, u32[]{:S(2)}) collective-permute-start(f32[3,1152]{1,0:T(4,128)S(1)} %pad_maximum_fusion), channel_id=1, source_target_pairs={{0,1},{1,0},{2,3},{3,2},{4,5},{5,4},{6,7},{7,6},{8,9},{9,8},{10,11... | collective-permute-start | bytes 41480 | tf_op jit(solution)/shard_map/ppermute | solution.py:134
  103.2 2.0 %collective-permute-done = f32[3,1152]{1,0:T(4,128)S(1)} collective-permute-done((f32[3,1152]{1,0:T(4,128)S(1)}, f32[3,1152]{1,0:T(4,128)S(1)}, u32[]{:S(2)}, u32[]{:S(2)}) %collective-permute-start) | collective-permute-done | bytes 13856 | tf_op jit(solution)/shard_map/ppermute | solution.py:134
  105.2 27.9 %all-to-all-done.2 = f32[128,2,1152]{2,1,0:T(2,128)S(1)} async-done(((f32[128,2,1152]{2,1,0:T(2,128)}), f32[128,2,1152]{2,1,0:T(2,128)S(1)}, u32[]{:S(2)}, u32[]{:S(2)}) %all-to-all-start.2) | async-done | bytes 1179680 | tf_op jit(solution)/shard_map/all_to_all | solution.py:186
  133.6 2.7 %collective-permute-start.1 = (f32[2,1152]{1,0:T(2,128)S(1)}, f32[2,1152]{1,0:T(2,128)S(1)}, u32[]{:S(2)}, u32[]{:S(2)}) collective-permute-start(f32[2,1152]{1,0:T(2,128)S(1)} %reduce_sum.75), channel_id=1, source_target_pairs={{0,1},{1,0},{2,3},{3,2},{4,5},{5,4},{6,7},{7,6},{8,9},{9,8},{10,11... | collective-permute-start | bytes 27656 | tf_op jit(solution)/shard_map/ppermute | solution.py:194
  136.3 1.4 collective-permute-done.1
  137.7 1.1 broadcast_in_dim.98
  138.8 7.4 %all-to-all-start.3 = ((bf16[128,2,1152]{2,1,0:T(2,128)(2,1)}), bf16[128,2,1152]{2,1,0:T(2,128)(2,1)S(1)}, u32[]{:S(2)}, u32[]{:S(2)}) async-start(bf16[128,2,1152]{2,1,0:T(2,128)(2,1)} %broadcast_in_dim.98), calls=%async_computation.3 | async-start | bytes 1179648 | tf_op jit(solution)/shard_map/all_to_all | solution.py:200
  146.8 20.7 %all-to-all-done.3 = bf16[128,2,1152]{2,1,0:T(2,128)(2,1)S(1)} async-done(((bf16[128,2,1152]{2,1,0:T(2,128)(2,1)}), bf16[128,2,1152]{2,1,0:T(2,128)(2,1)S(1)}, u32[]{:S(2)}, u32[]{:S(2)}) %all-to-all-start.3) | async-done | bytes 589856 | tf_op jit(solution)/shard_map/all_to_all | solution.py:200
  167.5 0.8 copy.57
  (63 shorter events, 5.7 us)
Async XLA Ops:
  0.6 84.4 %copy-start = (bf16[128,18]{0,1:T(8,128)(2,1)S(1)}, bf16[128,18]{0,1:T(8,128)(2,1)}, u32[]{:S(2)}) copy-start(bf16[128,18]{0,1:T(8,128)(2,1)} %param.20) | copy-start | bytes 13828
  5.5 25.4 %all-to-all-start = ((s32[128,1,2]{2,1,0:T(1,128)}), s32[128,1,2]{2,1,0:T(1,128)S(1)}, u32[]{:S(2)}, u32[]{:S(2)}) async-start(s32[128,1,2]{2,1,0:T(1,128)} %bitcast.4), calls=%async_computation | async-start | bytes 131072 | tf_op jit(solution)/shard_map/all_to_all | solution.py:153
  20.3 3.3 %copy-start.4 = (bf16[512,18]{0,1:T(8,128)(2,1)S(1)}, bf16[512,18]{0,1:T(8,128)(2,1)}, u32[]{:S(2)}) copy-start(bf16[512,18]{0,1:T(8,128)(2,1)} %param.15) | copy-start | bytes 55300
  20.3 3.5 %copy-start.5 = (bf16[512,18]{0,1:T(8,128)(2,1)S(1)}, bf16[512,18]{0,1:T(8,128)(2,1)}, u32[]{:S(2)}) copy-start(bf16[512,18]{0,1:T(8,128)(2,1)} %param.14) | copy-start | bytes 55300
  41.7 6.0 %copy-start.1 = (bf16[2,147456]{1,0:T(2,128)(2,1)S(1)}, bf16[2,147456]{1,0:T(2,128)(2,1)}, u32[]{:S(2)}) copy-start(bf16[2,147456]{1,0:T(2,128)(2,1)} %param.19) | copy-start | bytes 1769476
  41.7 37.7 %all-to-all-start.1 = ((bf16[128,2,2176]{2,1,0:T(2,128)(2,1)}), bf16[128,2,2176]{2,1,0:T(2,128)(2,1)S(1)}, u32[]{:S(2)}, u32[]{:S(2)}) async-start(bf16[128,2,2176]{2,1,0:T(2,128)(2,1)} %concatenate.8), calls=%async_computation.1 | async-start | bytes 2228224 | tf_op jit(solution)/shard_map/all_to_all | solution.py:168
  81.3 1.8 %copy-start.3 = (s32[128,20]{0,1:T(8,128)S(1)}, s32[128,20]{0,1:T(8,128)}, u32[]{:S(2)}) copy-start(s32[128,20]{0,1:T(8,128)} %param.18) | copy-start | bytes 30724
  84.8 2.2 %copy-start.2 = (bf16[9,128,128]{2,1,0:T(8,128)(2,1)S(1)}, bf16[9,128,128]{2,1,0:T(8,128)(2,1)}, u32[]{:S(2)}) copy-start(bf16[9,128,128]{2,1,0:T(8,128)(2,1)} %rev.3) | copy-start | bytes 884740
  94.0 6.2 %copy-start.6 = (f32[1,1152]{1,0:T(1,128)S(1)}, f32[1,1152]{1,0:T(1,128)}, u32[]{:S(2)}) copy-start(f32[1,1152]{1,0:T(1,128)} %param.23) | copy-start | bytes 13828
  94.0 6.2 %copy-start.7 = (f32[1,1152]{1,0:T(1,128)S(1)}, f32[1,1152]{1,0:T(1,128)}, u32[]{:S(2)}) copy-start(f32[1,1152]{1,0:T(1,128)} %param.22) | copy-start | bytes 13828
  94.0 6.2 %copy-start.8 = (f32[1,1152]{1,0:T(1,128)S(1)}, f32[1,1152]{1,0:T(1,128)}, u32[]{:S(2)}) copy-start(f32[1,1152]{1,0:T(1,128)} %param.21) | copy-start | bytes 13828
  94.0 39.1 %all-to-all-start.2 = ((f32[128,2,1152]{2,1,0:T(2,128)}), f32[128,2,1152]{2,1,0:T(2,128)S(1)}, u32[]{:S(2)}, u32[]{:S(2)}) async-start(f32[128,2,1152]{2,1,0:T(2,128)} %maximum_bitcast_fusion), calls=%async_computation.2 | async-start | bytes 2359296 | tf_op jit(solution)/shard_map/all_to_all | solution.py:186
  100.3 4.9 %collective-permute-start = (f32[3,1152]{1,0:T(4,128)S(1)}, f32[3,1152]{1,0:T(4,128)S(1)}, u32[]{:S(2)}, u32[]{:S(2)}) collective-permute-start(f32[3,1152]{1,0:T(4,128)S(1)} %pad_maximum_fusion), channel_id=1, source_target_pairs={{0,1},{1,0},{2,3},{3,2},{4,5},{5,4},{6,7},{7,6},{8,9},{9,8},{10,11... | collective-permute-start | bytes 41480 | tf_op jit(solution)/shard_map/ppermute | solution.py:134
  133.6 4.1 %collective-permute-start.1 = (f32[2,1152]{1,0:T(2,128)S(1)}, f32[2,1152]{1,0:T(2,128)S(1)}, u32[]{:S(2)}, u32[]{:S(2)}) collective-permute-start(f32[2,1152]{1,0:T(2,128)S(1)} %reduce_sum.75), channel_id=1, source_target_pairs={{0,1},{1,0},{2,3},{3,2},{4,5},{5,4},{6,7},{7,6},{8,9},{9,8},{10,11... | collective-permute-start | bytes 27656 | tf_op jit(solution)/shard_map/ppermute | solution.py:194
  138.8 28.7 %all-to-all-start.3 = ((bf16[128,2,1152]{2,1,0:T(2,128)(2,1)}), bf16[128,2,1152]{2,1,0:T(2,128)(2,1)S(1)}, u32[]{:S(2)}, u32[]{:S(2)}) async-start(bf16[128,2,1152]{2,1,0:T(2,128)(2,1)} %broadcast_in_dim.98), calls=%async_computation.3 | async-start | bytes 1179648 | tf_op jit(solution)/shard_map/all_to_all | solution.py:200

commit v5 on v4

--- a/solution.py
+++ b/solution.py
@@ -152,7 +152,7 @@
     row_index = jnp.maximum(
         lax.all_to_all(request, "dp", split_axis=0, concat_axis=0, tiled=True), 0
     )
-    row_width = replay_rows.shape[1] * replay_rows.shape[2] * channels
+    grid_rows, grid_cols = replay_rows.shape[1], replay_rows.shape[2]
     actions_n = qvalues.shape[1]
     side = jnp.concatenate(
         [
@@ -162,14 +162,15 @@
         ],
         axis=-1,
     )
-    packed = jnp.concatenate(
-        [jnp.take(replay_rows.reshape(-1, row_width), row_index, axis=0), side], axis=-1
-    )
+    side = jnp.pad(side[:, :, None, None, :], ((0, 0), (0, 0), (0, 0), (0, grid_cols - 1), (0, 0)))
+    packed = jnp.concatenate([jnp.take(replay_rows, row_index, axis=0), side], axis=2)
     slots = lax.all_to_all(packed, "dp", split_axis=0, concat_axis=0, tiled=True)
-    picked = jnp.take(slots.reshape(owners * capacity, -1), slot_index, axis=0)
-    features = picked[:, :row_width].reshape((rows_dev,) + replay_rows.shape[1:])
-    move_return_estimates = picked[:, row_width : row_width + actions_n]
-    reference_policy_entries = picked[:, row_width + actions_n : row_width + 2 * actions_n]
+    picked = jnp.take(
+        slots.reshape((owners * capacity,) + slots.shape[2:]), slot_index, axis=0
+    )
+    features = picked[:, :grid_rows]
+    move_return_estimates = picked[:, grid_rows, 0, :actions_n]
+    reference_policy_entries = picked[:, grid_rows, 0, actions_n : 2 * actions_n]
     row_scale = jnp.full((rows_dev,), 1.0 / learn_rows, jnp.float32)
     grad_first, grad_second = layer_grads(
         features,

time: 169 us -> 172 us (1.018)
  waiting for transfers between devices: 83.7 us -> 88 us
  local copies, waits for them, and re-layouts: 26.9 us -> 23.5 us
  other arithmetic: 7.13 us -> 10.4 us
    concatenate x1, local copies, waits for them, and re-layouts: 5.25 us -> 0.08 us  [per_device(): jnp.concatenate([jnp.take(qvalues, row_index, axis=0), jnp.take(target_lo...]
    reshape x3 -> x0, local copies, waits for them, and re-layouts: 4.04 us -> none  [the longest x1 3.3 us: per_device(): replay_rows.reshape(-1, row_width)]
    all_to_all x1, waiting for transfers between devices: 7.02 us -> 10.3 us  [per_device(): lax.all_to_all(request, 'dp', split_axis=0, concat_axis=0, tiled=True)]
    slice x1, local copies, waits for them, and re-layouts: 6.22 us -> 8.13 us  [per_device(): second_weight = weights[1].reshape(9 * channels, channels)]
    gather x4 -> x3, local copies, waits for them, and re-layouts: 3.38 us -> 5.09 us  [the longest x2 3.56 us: per_device(): jnp.take(slots.reshape((owners * capacity,) + slots.shape[2:]), slot_inde...]
  transfers between devices with their start and end apart: 6 -> 6, of which waited for: 6 -> 6; matrix products, arithmetic and copies ran while one was open for 7% -> 6% of each run, Pallas kernels for 0% -> 0%
where the time goes in v5:
time: 172 us
  waiting for transfers between devices  88 us (51%)
  starting transfers between devices  40 us (23%)
  local copies, waits for them, and re-layouts  23.5 us (14%)
  other arithmetic  10.4 us (6%)
  matrix products  8.7 us (5%)
    all_to_all x1, waiting for transfers between devices, per_device(): lax.all_to_all(loss_derivative.reshape(2, owners, piece_len).transpose(1,...  28.3 us
    all_to_all x1, waiting for transfers between devices, per_device(): lax.all_to_all(packed, 'dp', split_axis=0, concat_axis=0, tiled=True)  25.6 us
    all_to_all x1, waiting for transfers between devices, per_device(): lax.all_to_all(jnp.broadcast_to(both_layers[None], (owners, 2, piece_len)...  20.7 us
    all_to_all x1, starting transfers between devices, per_device(): lax.all_to_all(request, 'dp', split_axis=0, concat_axis=0, tiled=True)  14.8 us
    all_to_all x1, waiting for transfers between devices, per_device(): lax.all_to_all(request, 'dp', split_axis=0, concat_axis=0, tiled=True)  10.3 us
    slice x1, local copies, waits for them, and re-layouts, per_device(): second_weight = weights[1].reshape(9 * channels, channels)  8.13 us
    all_to_all x1, starting transfers between devices, per_device(): lax.all_to_all(jnp.broadcast_to(both_layers[None], (owners, 2, piece_len)...  7.35 us
    all_to_all x1, starting transfers between devices, per_device(): lax.all_to_all(loss_derivative.reshape(2, owners, piece_len).transpose(1,...  6.67 us
  transfers between devices with their start and end apart: 6, of which 6 were waited for; matrix products, arithmetic and copies ran while one was open for 6% of the time, Pallas kernels for 0%

profile of v5, /device:TPU:1, one launch (start us, length us, event | category | flops | bytes accessed | tf_op | source)
XLA Modules:
  0.0 171.6 jit_solution(15801082946149794229)
XLA Ops:
  0.7 1.0 convert_reduce_fusion.1
  2.7 1.9 %gather_fusion = s32[256]{0:T(256)S(1)} fusion(s32[128]{0:T(128)} %param.17, s32[1024]{0:T(1024)S(1)} %pad_clamp_fusion.3), kind=kCustom, calls=%fused_computation.2 | custom fusion | bytes 3072 | tf_op jit(solution)/shard_map/jit(_take)/gather | solution.py:149
  5.6 14.8 %all-to-all-start = ((s32[128,1,2]{2,1,0:T(1,128)}), s32[128,1,2]{2,1,0:T(1,128)S(1)}, u32[]{:S(2)}, u32[]{:S(2)}) async-start(s32[128,1,2]{2,1,0:T(1,128)} %bitcast.4), calls=%async_computation | async-start | bytes 131072 | tf_op jit(solution)/shard_map/all_to_all | solution.py:153
  20.8 10.3 %all-to-all-done = s32[128,1,2]{2,1,0:T(1,128)S(1)} async-done(((s32[128,1,2]{2,1,0:T(1,128)}), s32[128,1,2]{2,1,0:T(1,128)S(1)}, u32[]{:S(2)}, u32[]{:S(2)}) %all-to-all-start) | async-done | bytes 1056 | tf_op jit(solution)/shard_map/all_to_all | solution.py:153
  31.3 0.9 gather_fusion.3
  32.1 0.9 gather_fusion.4
  33.6 1.5 gather_fusion.1
  35.1 0.7 broadcast_select_fusion
  35.8 1.7 %fusion.2 = bf16[128,2,5,4,128]{4,3,2,1,0:T(4,128)(2,1)} fusion(bf16[128,2,1,1,128]{4,3,2,1,0:T(2,128)(2,1)S(1)} %copy.104, bf16[128,2,4,4,128]{4,3,2,1,0:T(4,128)(2,1)S(1)} %broadcast_select_fusion), kind=kLoop, calls=%fused_computation.11 | loop fusion | flops 3932160 | bytes 2424832 | tf_op jit(solution)/shard_map/concatenate | solution.py:166
  37.6 5.8 %all-to-all-start.1 = ((bf16[128,2,5,4,128]{4,3,2,1,0:T(4,128)(2,1)}), bf16[128,2,5,4,128]{4,3,2,1,0:T(4,128)(2,1)S(1)}, u32[]{:S(2)}, u32[]{:S(2)}) async-start(bf16[128,2,5,4,128]{4,3,2,1,0:T(4,128)(2,1)} %fusion.2), calls=%async_computation.1 | async-start | bytes 2621440 | tf_op jit(solution)/shard_map/all_to_all | solution.py:167
  43.4 8.1 %slice_reduce_fusion = (bf16[147456]{0:T(1024)(128)(2,1)}, bf16[147456]{0:T(1024)(128)(2,1)}) fusion(bf16[2,147456]{1,0:T(2,128)(2,1)} %param.19), kind=kLoop, calls=%fused_computation.29 | loop fusion | bytes 1179648 | tf_op jit(solution)/shard_map/slice | solution.py:130
  51.5 1.7 rev.3
  53.2 25.6 %all-to-all-done.1 = bf16[128,2,5,4,128]{4,3,2,1,0:T(4,128)(2,1)S(1)} async-done(((bf16[128,2,5,4,128]{4,3,2,1,0:T(4,128)(2,1)}), bf16[128,2,5,4,128]{4,3,2,1,0:T(4,128)(2,1)S(1)}, u32[]{:S(2)}, u32[]{:S(2)}) %all-to-all-start.1) | async-done | bytes 1310752 | tf_op jit(solution)/shard_map/all_to_all | solution.py:167
  78.8 2.0 %gather_fusion.2 = bf16[128,5,4,128]{3,2,1,0:T(4,128)(2,1)} fusion(bf16[256,5,4,128]{3,2,1,0:T(4,128)(2,1)S(1)} %bitcast.73, s32[1024]{0:T(1024)S(1)} %pad_clamp_fusion), kind=kCustom, calls=%fused_computation.4 | custom fusion | bytes 1311232 | tf_op jit(solution)/shard_map/jit(_take)/gather | solution.py:168
  80.8 1.6 copy.84
  82.5 0.8 copy-done.3
  83.4 0.9 fusion.19
  84.4 0.9 convert_reduce_fusion
  86.4 0.9 and_convert_fusion.1
  87.3 2.4 %fusion.7 = f32[3,3,128,128]{3,2,1,0:T(8,128)S(1)} fusion(bf16[128,4,4,128]{0,3,2,1:T(8,128)(2,1)} %copy-done.2, bf16[128,128]{0,1:T(8,128)(2,1)S(1)} %copy.88, u8[128,4,128]{0,2,1:T(8,128)(4,1)S(1)} %fusion.20), kind=kOutput, calls=%fused_computation.28 | convolution fusion | flops 420741120 | bytes 1212416 | tf_op jit(solution)/shard_map/conv_general_dilated | solution.py:43
  89.8 4.0 %fusion.6 = f32[3,3,128,128]{3,2,1,0:T(8,128)} fusion(pred[128,4,4,128]{0,3,2,1:T(32,128)(4,1)} %and_convert_fusion.1, bf16[3,3,128,128]{2,3,1,0:T(8,128)(2,1)} %bitcast.83, bf16[128,128]{0,1:T(8,128)(2,1)S(1)} %copy.88, bf16[128,5,4,128]{0,3,2,1:T(8,128)(2,1)S(1)} %broadcast_select_fusion.1, u8[128,4,128]{0,2,1:T(8,128)(4,1)S(1)} %fusion.20), kind=kOutput, calls=%fused_computation.15 | convolution fusion | flops 840695808 | bytes 1769472 | tf_op jit(solution)/shard_map/conv_general_dilated | solution.py:43
  93.7 3.1 %maximum_bitcast_fusion = f32[128,2,1152]{2,1,0:T(2,128)} fusion(f32[1,128,1152]{2,0,1:T(1,128)S(1)} %bitcast.80, f32[1,128,1152]{2,0,1:T(1,128)} %bitcast.81), kind=kLoop, calls=%fused_computation.16 | loop fusion | flops 294912 | bytes 2359296 | tf_op jit(solution)/shard_map/transpose | solution.py:188
  96.9 6.7 %all-to-all-start.2 = ((f32[128,2,1152]{2,1,0:T(2,128)}), f32[128,2,1152]{2,1,0:T(2,128)S(1)}, u32[]{:S(2)}, u32[]{:S(2)}) async-start(f32[128,2,1152]{2,1,0:T(2,128)} %maximum_bitcast_fusion), calls=%async_computation.2 | async-start | bytes 2359296 | tf_op jit(solution)/shard_map/all_to_all | solution.py:187
  103.6 2.7 %collective-permute-start = (f32[3,1152]{1,0:T(4,128)S(1)}, f32[3,1152]{1,0:T(4,128)S(1)}, u32[]{:S(2)}, u32[]{:S(2)}) collective-permute-start(f32[3,1152]{1,0:T(4,128)S(1)} %pad_maximum_fusion), channel_id=1, source_target_pairs={{0,1},{1,0},{2,3},{3,2},{4,5},{5,4},{6,7},{7,6},{8,9},{9,8},{10,11... | collective-permute-start | bytes 41480 | tf_op jit(solution)/shard_map/ppermute | solution.py:134
  106.3 1.8 %collective-permute-done = f32[3,1152]{1,0:T(4,128)S(1)} collective-permute-done((f32[3,1152]{1,0:T(4,128)S(1)}, f32[3,1152]{1,0:T(4,128)S(1)}, u32[]{:S(2)}, u32[]{:S(2)}) %collective-permute-start) | collective-permute-done | bytes 13856 | tf_op jit(solution)/shard_map/ppermute | solution.py:134
  108.1 28.3 %all-to-all-done.2 = f32[128,2,1152]{2,1,0:T(2,128)S(1)} async-done(((f32[128,2,1152]{2,1,0:T(2,128)}), f32[128,2,1152]{2,1,0:T(2,128)S(1)}, u32[]{:S(2)}, u32[]{:S(2)}) %all-to-all-start.2) | async-done | bytes 1179680 | tf_op jit(solution)/shard_map/all_to_all | solution.py:187
  136.9 2.7 %collective-permute-start.1 = (f32[2,1152]{1,0:T(2,128)S(1)}, f32[2,1152]{1,0:T(2,128)S(1)}, u32[]{:S(2)}, u32[]{:S(2)}) collective-permute-start(f32[2,1152]{1,0:T(2,128)S(1)} %reduce_sum.75), channel_id=1, source_target_pairs={{0,1},{1,0},{2,3},{3,2},{4,5},{5,4},{6,7},{7,6},{8,9},{9,8},{10,11... | collective-permute-start | bytes 27656 | tf_op jit(solution)/shard_map/ppermute | solution.py:195
  139.6 1.3 collective-permute-done.1
  141.0 1.1 broadcast_in_dim.102
  142.1 7.4 %all-to-all-start.3 = ((bf16[128,2,1152]{2,1,0:T(2,128)(2,1)}), bf16[128,2,1152]{2,1,0:T(2,128)(2,1)S(1)}, u32[]{:S(2)}, u32[]{:S(2)}) async-start(bf16[128,2,1152]{2,1,0:T(2,128)(2,1)} %broadcast_in_dim.102), calls=%async_computation.3 | async-start | bytes 1179648 | tf_op jit(solution)/shard_map/all_to_all | solution.py:201
  150.1 20.7 %all-to-all-done.3 = bf16[128,2,1152]{2,1,0:T(2,128)(2,1)S(1)} async-done(((bf16[128,2,1152]{2,1,0:T(2,128)(2,1)}), bf16[128,2,1152]{2,1,0:T(2,128)(2,1)S(1)}, u32[]{:S(2)}, u32[]{:S(2)}) %all-to-all-start.3) | async-done | bytes 589856 | tf_op jit(solution)/shard_map/all_to_all | solution.py:201
  170.8 0.8 copy.110
  (68 shorter events, 5.4 us)
Async XLA Ops:
  0.6 32.9 %copy-start = (bf16[512,4,4,128]{3,2,1,0:T(4,128)(2,1)S(1)}, bf16[512,4,4,128]{3,2,1,0:T(4,128)(2,1)}, u32[]{:S(2)}) copy-start(bf16[512,4,4,128]{3,2,1,0:T(4,128)(2,1)} %param.13) | copy-start | bytes 6291460
  0.6 19.7 %copy-start.5 = (bf16[512,18]{0,1:T(8,128)(2,1)S(1)}, bf16[512,18]{0,1:T(8,128)(2,1)}, u32[]{:S(2)}) copy-start(bf16[512,18]{0,1:T(8,128)(2,1)} %param.14) | copy-start | bytes 55300
  0.7 19.9 %copy-start.6 = (bf16[512,18]{0,1:T(8,128)(2,1)S(1)}, bf16[512,18]{0,1:T(8,128)(2,1)}, u32[]{:S(2)}) copy-start(bf16[512,18]{0,1:T(8,128)(2,1)} %param.15) | copy-start | bytes 55300
  5.6 25.4 %all-to-all-start = ((s32[128,1,2]{2,1,0:T(1,128)}), s32[128,1,2]{2,1,0:T(1,128)S(1)}, u32[]{:S(2)}, u32[]{:S(2)}) async-start(s32[128,1,2]{2,1,0:T(1,128)} %bitcast.4), calls=%async_computation | async-start | bytes 131072 | tf_op jit(solution)/shard_map/all_to_all | solution.py:153
  37.6 41.3 %all-to-all-start.1 = ((bf16[128,2,5,4,128]{4,3,2,1,0:T(4,128)(2,1)}), bf16[128,2,5,4,128]{4,3,2,1,0:T(4,128)(2,1)S(1)}, u32[]{:S(2)}, u32[]{:S(2)}) async-start(bf16[128,2,5,4,128]{4,3,2,1,0:T(4,128)(2,1)} %fusion.2), calls=%async_computation.1 | async-start | bytes 2621440 | tf_op jit(solution)/shard_map/all_to_all | solution.py:167
  82.4 1.0 copy-start.3
  82.4 1.9 %copy-start.1 = (bf16[147456]{0:T(1024)(128)(2,1)S(1)}, bf16[147456]{0:T(1024)(128)(2,1)}, u32[]{:S(2)}) copy-start(bf16[147456]{0:T(1024)(128)(2,1)} %get-tuple-element.3) | copy-start | bytes 884740
  84.3 1.0 copy-start.2
  84.3 1.1 copy-start.4
  84.4 1.2 copy-start.7
  96.9 6.7 %copy-start.8 = (f32[1,1152]{1,0:T(1,128)S(1)}, f32[1,1152]{1,0:T(1,128)}, u32[]{:S(2)}) copy-start(f32[1,1152]{1,0:T(1,128)} %param.23) | copy-start | bytes 13828
  96.9 6.7 %copy-start.9 = (f32[1,1152]{1,0:T(1,128)S(1)}, f32[1,1152]{1,0:T(1,128)}, u32[]{:S(2)}) copy-start(f32[1,1152]{1,0:T(1,128)} %param.22) | copy-start | bytes 13828
  96.9 6.7 %copy-start.10 = (f32[1,1152]{1,0:T(1,128)S(1)}, f32[1,1152]{1,0:T(1,128)}, u32[]{:S(2)}) copy-start(f32[1,1152]{1,0:T(1,128)} %param.21) | copy-start | bytes 13828
  96.9 39.6 %all-to-all-start.2 = ((f32[128,2,1152]{2,1,0:T(2,128)}), f32[128,2,1152]{2,1,0:T(2,128)S(1)}, u32[]{:S(2)}, u32[]{:S(2)}) async-start(f32[128,2,1152]{2,1,0:T(2,128)} %maximum_bitcast_fusion), calls=%async_computation.2 | async-start | bytes 2359296 | tf_op jit(solution)/shard_map/all_to_all | solution.py:187
  103.6 4.5 %collective-permute-start = (f32[3,1152]{1,0:T(4,128)S(1)}, f32[3,1152]{1,0:T(4,128)S(1)}, u32[]{:S(2)}, u32[]{:S(2)}) collective-permute-start(f32[3,1152]{1,0:T(4,128)S(1)} %pad_maximum_fusion), channel_id=1, source_target_pairs={{0,1},{1,0},{2,3},{3,2},{4,5},{5,4},{6,7},{7,6},{8,9},{9,8},{10,11... | collective-permute-start | bytes 41480 | tf_op jit(solution)/shard_map/ppermute | solution.py:134
  136.9 4.1 %collective-permute-start.1 = (f32[2,1152]{1,0:T(2,128)S(1)}, f32[2,1152]{1,0:T(2,128)S(1)}, u32[]{:S(2)}, u32[]{:S(2)}) collective-permute-start(f32[2,1152]{1,0:T(2,128)S(1)} %reduce_sum.75), channel_id=1, source_target_pairs={{0,1},{1,0},{2,3},{3,2},{4,5},{5,4},{6,7},{7,6},{8,9},{9,8},{10,11... | collective-permute-start | bytes 27656 | tf_op jit(solution)/shard_map/ppermute | solution.py:195
  142.1 28.7 %all-to-all-start.3 = ((bf16[128,2,1152]{2,1,0:T(2,128)(2,1)}), bf16[128,2,1152]{2,1,0:T(2,128)(2,1)S(1)}, u32[]{:S(2)}, u32[]{:S(2)}) async-start(bf16[128,2,1152]{2,1,0:T(2,128)(2,1)} %broadcast_in_dim.102), calls=%async_computation.3 | async-start | bytes 1179648 | tf_op jit(solution)/shard_map/all_to_all | solution.py:201

commit v6 on v2

--- a/solution.py
+++ b/solution.py
@@ -154,19 +154,21 @@
     )
     row_width = replay_rows.shape[1] * replay_rows.shape[2] * channels
     actions_n = qvalues.shape[1]
-    packed = jnp.concatenate(
+    table = jnp.concatenate(
         [
-            jnp.take(replay_rows.reshape(-1, row_width), row_index, axis=0),
-            jnp.take(qvalues, row_index, axis=0),
-            jnp.take(target_logits, row_index, axis=0),
+            replay_rows.reshape(-1, row_width),
+            qvalues,
+            target_logits,
+            jnp.zeros((qvalues.shape[0], channels - 2 * actions_n), qvalues.dtype),
         ],
         axis=-1,
     )
+    packed = jnp.take(table, row_index, axis=0)
     slots = lax.all_to_all(packed, "dp", split_axis=0, concat_axis=0, tiled=True)
     picked = jnp.take(slots.reshape(owners * capacity, -1), slot_index, axis=0)
     features = picked[:, :row_width].reshape((rows_dev,) + replay_rows.shape[1:])
     move_return_estimates = picked[:, row_width : row_width + actions_n]
-    reference_policy_entries = picked[:, row_width + actions_n :]
+    reference_policy_entries = picked[:, row_width + actions_n : row_width + 2 * actions_n]
     row_scale = jnp.full((rows_dev,), 1.0 / learn_rows, jnp.float32)
     grad_first, grad_second = layer_grads(
         features,

time: 169 us -> 167 us (0.988)
  starting transfers between devices: 39.7 us -> 44.3 us
  waiting for transfers between devices: 83.9 us -> 79.4 us
  local copies, waits for them, and re-layouts: 27 us -> 23.8 us
    all_to_all x1, waiting for transfers between devices: 7.02 us -> 2.19 us  [per_device(): lax.all_to_all(request, 'dp', split_axis=0, concat_axis=0, tiled=True)]
    all_to_all x1, starting transfers between devices: 5.96 us -> 10.3 us  [per_device(): lax.all_to_all(packed, 'dp', split_axis=0, concat_axis=0, tiled=True)]
    gather x4 -> x2, local copies, waits for them, and re-layouts: 3.78 us -> 1.96 us  [per_device(): packed = jnp.take(table, row_index, axis=0)]
  transfers between devices with their start and end apart: 6 -> 6, of which waited for: 6 -> 6; matrix products, arithmetic and copies ran while one was open for 7% -> 9% of each run, Pallas kernels for 0% -> 0%
where the time goes in v6:
time: 167 us; the launch traced here: 166 us
  waiting for transfers between devices  79.4 us (48%)
  starting transfers between devices  44.3 us (27%)
  local copies, waits for them, and re-layouts  23.8 us (14%)
  matrix products  9.62 us (6%)
  other arithmetic  7.96 us (5%)
    all_to_all x1, waiting for transfers between devices, per_device(): lax.all_to_all(loss_derivative.reshape(2, owners, piece_len).transpose(1,...  27.9 us
    all_to_all x1, waiting for transfers between devices, per_device(): lax.all_to_all(packed, 'dp', split_axis=0, concat_axis=0, tiled=True)  25.3 us
    all_to_all x1, waiting for transfers between devices, per_device(): lax.all_to_all(jnp.broadcast_to(both_layers[None], (owners, 2, piece_len)...  20.7 us
    all_to_all x1, starting transfers between devices, per_device(): lax.all_to_all(request, 'dp', split_axis=0, concat_axis=0, tiled=True)  14.8 us
    all_to_all x1, starting transfers between devices, per_device(): lax.all_to_all(packed, 'dp', split_axis=0, concat_axis=0, tiled=True)  10.3 us
    all_to_all x1, starting transfers between devices, per_device(): lax.all_to_all(jnp.broadcast_to(both_layers[None], (owners, 2, piece_len)...  7.35 us
    conv_general_dilated x2, matrix products, conv_kernel_grad(): lax.conv_general_dilated(field, out_grad, (1, 1), ((1, 1), (1, 1)), dimen...  6.34 us
    slice x1, local copies, waits for them, and re-layouts, per_device(): second_weight = weights[1].reshape(9 * channels, channels)  6.22 us
  transfers between devices with their start and end apart: 6, of which 6 were waited for; matrix products, arithmetic and copies ran while one was open for 9% of the time, Pallas kernels for 0%

profile of v6, /device:TPU:1, one launch (start us, length us, event | category | flops | bytes accessed | tf_op | source)
XLA Modules:
  0.0 166.1 jit_solution(6514541084510769252)
XLA Ops:
  0.6 0.9 convert_reduce_fusion.1
  1.6 0.7 compare_and_fusion
  2.8 1.9 %gather_fusion = s32[256]{0:T(256)S(1)} fusion(s32[128]{0:T(128)} %param.15, s32[1024]{0:T(1024)S(1)} %pad_clamp_fusion.2), kind=kCustom, calls=%fused_computation | custom fusion | bytes 3072 | tf_op jit(solution)/shard_map/jit(_take)/gather | solution.py:149
  4.8 0.7 select_select_fusion
  5.5 14.8 %all-to-all-start = ((s32[128,1,2]{2,1,0:T(1,128)}), s32[128,1,2]{2,1,0:T(1,128)S(1)}, u32[]{:S(2)}, u32[]{:S(2)}) async-start(s32[128,1,2]{2,1,0:T(1,128)} %bitcast.4), calls=%async_computation | async-start | bytes 131072 | tf_op jit(solution)/shard_map/all_to_all | solution.py:153
  20.3 4.5 %reshape.157 = bf16[512,2048]{1,0:T(8,128)(2,1)} reshape(bf16[512,4,4,128]{3,2,1,0:T(4,128)(2,1)} %param.11) | data formatting | bytes 4194304 | tf_op jit(solution)/shard_map/reshape | solution.py:159
  25.1 3.6 %concatenate.8 = bf16[512,2176]{1,0:T(8,128)(2,1)S(1)} concatenate(bf16[512,2048]{1,0:T(8,128)(2,1)} %reshape.157, bf16[512,18]{1,0:T(8,128)(2,1)S(1)} %copy.36, bf16[512,18]{1,0:T(8,128)(2,1)S(1)} %copy.37, bf16[512,92]{1,0:T(8,128)(2,1)S(1)} %broadcast_in_dim.84), dimensions={1} | concatenate | bytes 4456448 | tf_op jit(solution)/shard_map/concatenate | solution.py:157
  28.7 2.2 %all-to-all-done = s32[128,1,2]{2,1,0:T(1,128)S(1)} async-done(((s32[128,1,2]{2,1,0:T(1,128)}), s32[128,1,2]{2,1,0:T(1,128)S(1)}, u32[]{:S(2)}, u32[]{:S(2)}) %all-to-all-start) | async-done | bytes 1056 | tf_op jit(solution)/shard_map/all_to_all | solution.py:153
  31.1 1.5 gather_fusion.1
  32.6 0.5 reshape.170
  33.1 2.1 %broadcast_select_fusion = bf16[128,2,2176]{2,1,0:T(2,128)(2,1)} fusion(bf16[128,2,2176]{2,1,0:T(2,128)(2,1)S(1)} %reshape.170, pred[128,2]{1,0:T(8,128)(4,1)S(1)} %compare_bitcast_fusion), kind=kLoop, calls=%fused_computation.3 | loop fusion | flops 557056 | bytes 2228480 | tf_op jit(solution)/shard_map/jit(_take)/select_n | solution.py:166
  35.2 10.3 %all-to-all-start.1 = ((bf16[128,2,2176]{2,1,0:T(2,128)(2,1)}), bf16[128,2,2176]{2,1,0:T(2,128)(2,1)S(1)}, u32[]{:S(2)}, u32[]{:S(2)}) async-start(bf16[128,2,2176]{2,1,0:T(2,128)(2,1)} %broadcast_select_fusion), calls=%async_computation.1 | async-start | bytes 2228224 | tf_op jit(solution)/shard_map/all_to_all | solution.py:167
  45.5 6.2 %slice_reduce_fusion = (bf16[147456]{0:T(1024)(128)(2,1)S(1)}, bf16[147456]{0:T(1024)(128)(2,1)S(1)}) fusion(bf16[2,147456]{1,0:T(2,128)(2,1)S(1)} %copy-done.1), kind=kLoop, calls=%fused_computation.23 | loop fusion | bytes 1179648 | tf_op jit(solution)/shard_map/slice | solution.py:130
  51.8 25.3 %all-to-all-done.1 = bf16[128,2,2176]{2,1,0:T(2,128)(2,1)S(1)} async-done(((bf16[128,2,2176]{2,1,0:T(2,128)(2,1)}), bf16[128,2,2176]{2,1,0:T(2,128)(2,1)S(1)}, u32[]{:S(2)}, u32[]{:S(2)}) %all-to-all-start.1) | async-done | bytes 1114144 | tf_op jit(solution)/shard_map/all_to_all | solution.py:167
  77.6 1.0 gather_fusion.2
  79.4 1.4 fusion.15
  81.0 1.4 convert_reduce_fusion
  83.3 1.4 fusion.5
  84.7 4.9 %fusion.4 = f32[3,3,128,128]{3,2,1,0:T(8,128)S(1)} fusion(bf16[128,4,4,128]{0,3,2,1:T(8,128)(2,1)S(1)} %bitcast.59, pred[128,4,4,128]{3,0,2,1:T(32,128)(4,1)S(1)} %and_convert_fusion.1, bf16[3,3,128,128]{2,3,1,0:T(8,128)(2,1)S(1)} %bitcast.65, bf16[128,128]{1,0:T(8,128)(2,1)S(1)} %convolution_multiply_fusion, u8[128,4,128]{2,0,1:T(8,128)(4,1)S(1)} %fusion.16), kind=kOutput, calls=%fused_computation.11 | convolution fusion | flops 840695808 | bytes 1769472 | tf_op jit(solution)/shard_map/conv_general_dilated | solution.py:43
  89.7 2.1 %maximum_bitcast_fusion = f32[128,2,1152]{2,1,0:T(2,128)} fusion(f32[1,128,1152]{2,0,1:T(1,128)S(1)} %bitcast.62, f32[1,128,1152]{2,0,1:T(1,128)S(1)} %bitcast.63), kind=kLoop, calls=%fused_computation.12 | loop fusion | flops 294912 | bytes 2359296 | tf_op jit(solution)/shard_map/transpose | solution.py:186
  91.8 6.2 %all-to-all-start.2 = ((f32[128,2,1152]{2,1,0:T(2,128)}), f32[128,2,1152]{2,1,0:T(2,128)S(1)}, u32[]{:S(2)}, u32[]{:S(2)}) async-start(f32[128,2,1152]{2,1,0:T(2,128)} %maximum_bitcast_fusion), calls=%async_computation.2 | async-start | bytes 2359296 | tf_op jit(solution)/shard_map/all_to_all | solution.py:185
  98.0 2.9 %collective-permute-start = (f32[3,1152]{1,0:T(4,128)S(1)}, f32[3,1152]{1,0:T(4,128)S(1)}, u32[]{:S(2)}, u32[]{:S(2)}) collective-permute-start(f32[3,1152]{1,0:T(4,128)S(1)} %pad_maximum_fusion), channel_id=1, source_target_pairs={{0,1},{1,0},{2,3},{3,2},{4,5},{5,4},{6,7},{7,6},{8,9},{9,8},{10,11... | collective-permute-start | bytes 41480 | tf_op jit(solution)/shard_map/ppermute | solution.py:134
  101.0 2.0 %collective-permute-done = f32[3,1152]{1,0:T(4,128)S(1)} collective-permute-done((f32[3,1152]{1,0:T(4,128)S(1)}, f32[3,1152]{1,0:T(4,128)S(1)}, u32[]{:S(2)}, u32[]{:S(2)}) %collective-permute-start) | collective-permute-done | bytes 13856 | tf_op jit(solution)/shard_map/ppermute | solution.py:134
  103.0 27.9 %all-to-all-done.2 = f32[128,2,1152]{2,1,0:T(2,128)S(1)} async-done(((f32[128,2,1152]{2,1,0:T(2,128)}), f32[128,2,1152]{2,1,0:T(2,128)S(1)}, u32[]{:S(2)}, u32[]{:S(2)}) %all-to-all-start.2) | async-done | bytes 1179680 | tf_op jit(solution)/shard_map/all_to_all | solution.py:185
  130.9 0.5 reduce_sum.75
  131.3 2.7 %collective-permute-start.1 = (f32[2,1152]{1,0:T(2,128)S(1)}, f32[2,1152]{1,0:T(2,128)S(1)}, u32[]{:S(2)}, u32[]{:S(2)}) collective-permute-start(f32[2,1152]{1,0:T(2,128)S(1)} %reduce_sum.75), channel_id=1, source_target_pairs={{0,1},{1,0},{2,3},{3,2},{4,5},{5,4},{6,7},{7,6},{8,9},{9,8},{10,11... | collective-permute-start | bytes 27656 | tf_op jit(solution)/shard_map/ppermute | solution.py:193
  134.1 1.3 collective-permute-done.1
  135.5 1.1 broadcast_in_dim.89
  136.6 7.4 %all-to-all-start.3 = ((bf16[128,2,1152]{2,1,0:T(2,128)(2,1)}), bf16[128,2,1152]{2,1,0:T(2,128)(2,1)S(1)}, u32[]{:S(2)}, u32[]{:S(2)}) async-start(bf16[128,2,1152]{2,1,0:T(2,128)(2,1)} %broadcast_in_dim.89), calls=%async_computation.3 | async-start | bytes 1179648 | tf_op jit(solution)/shard_map/all_to_all | solution.py:199
  143.9 0.6 constant_dynamic-slice_fusion
  144.6 20.7 %all-to-all-done.3 = bf16[128,2,1152]{2,1,0:T(2,128)(2,1)S(1)} async-done(((bf16[128,2,1152]{2,1,0:T(2,128)(2,1)}), bf16[128,2,1152]{2,1,0:T(2,128)(2,1)S(1)}, u32[]{:S(2)}, u32[]{:S(2)}) %all-to-all-start.3) | async-done | bytes 589856 | tf_op jit(solution)/shard_map/all_to_all | solution.py:199
  165.3 0.8 copy.57
  (55 shorter events, 3.6 us)
Async XLA Ops:
  0.6 82.2 %copy-start = (bf16[128,18]{0,1:T(8,128)(2,1)S(1)}, bf16[128,18]{0,1:T(8,128)(2,1)}, u32[]{:S(2)}) copy-start(bf16[128,18]{0,1:T(8,128)(2,1)} %param.18) | copy-start | bytes 13828
  5.5 25.4 %all-to-all-start = ((s32[128,1,2]{2,1,0:T(1,128)}), s32[128,1,2]{2,1,0:T(1,128)S(1)}, u32[]{:S(2)}, u32[]{:S(2)}) async-start(s32[128,1,2]{2,1,0:T(1,128)} %bitcast.4), calls=%async_computation | async-start | bytes 131072 | tf_op jit(solution)/shard_map/all_to_all | solution.py:153
  20.3 4.5 %copy-start.3 = (bf16[512,18]{0,1:T(8,128)(2,1)S(1)}, bf16[512,18]{0,1:T(8,128)(2,1)}, u32[]{:S(2)}) copy-start(bf16[512,18]{0,1:T(8,128)(2,1)} %param.12) | copy-start | bytes 55300
  20.3 4.7 %copy-start.4 = (bf16[512,18]{0,1:T(8,128)(2,1)S(1)}, bf16[512,18]{0,1:T(8,128)(2,1)}, u32[]{:S(2)}) copy-start(bf16[512,18]{0,1:T(8,128)(2,1)} %param.13) | copy-start | bytes 55300
  35.2 10.3 %copy-start.1 = (bf16[2,147456]{1,0:T(2,128)(2,1)S(1)}, bf16[2,147456]{1,0:T(2,128)(2,1)}, u32[]{:S(2)}) copy-start(bf16[2,147456]{1,0:T(2,128)(2,1)} %param.17) | copy-start | bytes 1769476
  35.2 41.9 %all-to-all-start.1 = ((bf16[128,2,2176]{2,1,0:T(2,128)(2,1)}), bf16[128,2,2176]{2,1,0:T(2,128)(2,1)S(1)}, u32[]{:S(2)}, u32[]{:S(2)}) async-start(bf16[128,2,2176]{2,1,0:T(2,128)(2,1)} %broadcast_select_fusion), calls=%async_computation.1 | async-start | bytes 2228224 | tf_op jit(solution)/shard_map/all_to_all | solution.py:167
  79.1 1.8 %copy-start.2 = (s32[128,20]{0,1:T(8,128)S(1)}, s32[128,20]{0,1:T(8,128)}, u32[]{:S(2)}) copy-start(s32[128,20]{0,1:T(8,128)} %param.16) | copy-start | bytes 30724
  91.7 6.2 %copy-start.5 = (f32[1,1152]{1,0:T(1,128)S(1)}, f32[1,1152]{1,0:T(1,128)}, u32[]{:S(2)}) copy-start(f32[1,1152]{1,0:T(1,128)} %param.21) | copy-start | bytes 13828
  91.7 6.2 %copy-start.6 = (f32[1,1152]{1,0:T(1,128)S(1)}, f32[1,1152]{1,0:T(1,128)}, u32[]{:S(2)}) copy-start(f32[1,1152]{1,0:T(1,128)} %param.20) | copy-start | bytes 13828
  91.8 6.2 %copy-start.7 = (f32[1,1152]{1,0:T(1,128)S(1)}, f32[1,1152]{1,0:T(1,128)}, u32[]{:S(2)}) copy-start(f32[1,1152]{1,0:T(1,128)} %param.19) | copy-start | bytes 13828
  91.8 39.1 %all-to-all-start.2 = ((f32[128,2,1152]{2,1,0:T(2,128)}), f32[128,2,1152]{2,1,0:T(2,128)S(1)}, u32[]{:S(2)}, u32[]{:S(2)}) async-start(f32[128,2,1152]{2,1,0:T(2,128)} %maximum_bitcast_fusion), calls=%async_computation.2 | async-start | bytes 2359296 | tf_op jit(solution)/shard_map/all_to_all | solution.py:185
  98.0 4.9 %collective-permute-start = (f32[3,1152]{1,0:T(4,128)S(1)}, f32[3,1152]{1,0:T(4,128)S(1)}, u32[]{:S(2)}, u32[]{:S(2)}) collective-permute-start(f32[3,1152]{1,0:T(4,128)S(1)} %pad_maximum_fusion), channel_id=1, source_target_pairs={{0,1},{1,0},{2,3},{3,2},{4,5},{5,4},{6,7},{7,6},{8,9},{9,8},{10,11... | collective-permute-start | bytes 41480 | tf_op jit(solution)/shard_map/ppermute | solution.py:134
  131.3 4.1 %collective-permute-start.1 = (f32[2,1152]{1,0:T(2,128)S(1)}, f32[2,1152]{1,0:T(2,128)S(1)}, u32[]{:S(2)}, u32[]{:S(2)}) collective-permute-start(f32[2,1152]{1,0:T(2,128)S(1)} %reduce_sum.75), channel_id=1, source_target_pairs={{0,1},{1,0},{2,3},{3,2},{4,5},{5,4},{6,7},{7,6},{8,9},{9,8},{10,11... | collective-permute-start | bytes 27656 | tf_op jit(solution)/shard_map/ppermute | solution.py:193
  136.6 28.7 %all-to-all-start.3 = ((bf16[128,2,1152]{2,1,0:T(2,128)(2,1)}), bf16[128,2,1152]{2,1,0:T(2,128)(2,1)S(1)}, u32[]{:S(2)}, u32[]{:S(2)}) async-start(bf16[128,2,1152]{2,1,0:T(2,128)(2,1)} %broadcast_in_dim.89), calls=%async_computation.3 | async-start | bytes 1179648 | tf_op jit(solution)/shard_map/all_to_all | solution.py:199

commit v7 on v6

--- a/solution.py
+++ b/solution.py
@@ -144,9 +144,7 @@
     rank_within = jnp.sum(earlier.astype(jnp.int32), axis=1)
     slot_index = replay_owner * capacity + rank_within
     matches = slot_index[None, :] == jnp.arange(owners * capacity, dtype=jnp.int32)[:, None]
-    occupied_entries = jnp.any(matches, axis=1)
-    source = jnp.sum(jnp.where(matches, row_order[None, :], 0), axis=1)
-    request = jnp.where(occupied_entries, jnp.take(replay_slot, source), -1).reshape(
+    request = jnp.sum(jnp.where(matches, replay_slot[None, :], 0), axis=1).reshape(
         owners, capacity
     )
     row_index = jnp.maximum(

time: 167 us -> 166 us (level)
    gather x2 -> x0, local copies, waits for them, and re-layouts: 2.04 us -> none  [per_device(): jnp.take(replay_slot, source)]
where the time goes in v7:
time: 166 us; the launch traced here: 165 us
  waiting for transfers between devices  79.5 us (48%)
  starting transfers between devices  44.2 us (27%)
  local copies, waits for them, and re-layouts  22.7 us (14%)
  matrix products  9.63 us (6%)
  other arithmetic  8.12 us (5%)
    all_to_all x1, waiting for transfers between devices, per_device(): lax.all_to_all(loss_derivative.reshape(2, owners, piece_len).transpose(1,...  27.9 us
    all_to_all x1, waiting for transfers between devices, per_device(): lax.all_to_all(packed, 'dp', split_axis=0, concat_axis=0, tiled=True)  25.3 us
    all_to_all x1, waiting for transfers between devices, per_device(): lax.all_to_all(jnp.broadcast_to(both_layers[None], (owners, 2, piece_len)...  20.7 us
    all_to_all x1, starting transfers between devices, per_device(): lax.all_to_all(request, 'dp', split_axis=0, concat_axis=0, tiled=True)  14.8 us
    all_to_all x1, starting transfers between devices, per_device(): lax.all_to_all(packed, 'dp', split_axis=0, concat_axis=0, tiled=True)  10.3 us
    all_to_all x1, starting transfers between devices, per_device(): lax.all_to_all(jnp.broadcast_to(both_layers[None], (owners, 2, piece_len)...  7.35 us
    conv_general_dilated x2, matrix products, conv_kernel_grad(): lax.conv_general_dilated(field, out_grad, (1, 1), ((1, 1), (1, 1)), dimen...  6.34 us
    slice x1, local copies, waits for them, and re-layouts, per_device(): second_weight = weights[1].reshape(9 * channels, channels)  6.22 us
  transfers between devices with their start and end apart: 6, of which 6 were waited for; matrix products, arithmetic and copies ran while one was open for 9% of the time, Pallas kernels for 0%

profile of v7, /device:TPU:1, one launch (start us, length us, event | category | flops | bytes accessed | tf_op | source)
XLA Modules:
  0.0 165.1 jit_solution(9412813176825717682)
XLA Ops:
  0.6 0.9 convert_reduce_fusion.1
  1.6 0.7 compare_and_fusion
  2.2 0.8 select_reduce_fusion.2
  3.0 0.8 all_to_all.15
  3.8 14.8 %all-to-all-start = ((s32[128,1,2]{2,1,0:T(1,128)}), s32[128,1,2]{2,1,0:T(1,128)S(1)}, u32[]{:S(2)}, u32[]{:S(2)}) async-start(s32[128,1,2]{2,1,0:T(1,128)} %bitcast.2), calls=%async_computation | async-start | bytes 131072 | tf_op jit(solution)/shard_map/all_to_all | solution.py:151
  18.6 4.5 %reshape.81 = bf16[512,2048]{1,0:T(8,128)(2,1)} reshape(bf16[512,4,4,128]{3,2,1,0:T(4,128)(2,1)} %param.11) | data formatting | bytes 4194304 | tf_op jit(solution)/shard_map/reshape | solution.py:157
  23.4 3.6 %concatenate.8 = bf16[512,2176]{1,0:T(8,128)(2,1)S(1)} concatenate(bf16[512,2048]{1,0:T(8,128)(2,1)} %reshape.81, bf16[512,18]{1,0:T(8,128)(2,1)S(1)} %copy.47, bf16[512,18]{1,0:T(8,128)(2,1)S(1)} %copy.48, bf16[512,92]{1,0:T(8,128)(2,1)S(1)} %broadcast_in_dim.72), dimensions={1} | concatenate | bytes 4456448 | tf_op jit(solution)/shard_map/concatenate | solution.py:155
  27.0 2.2 %all-to-all-done = s32[128,1,2]{2,1,0:T(1,128)S(1)} async-done(((s32[128,1,2]{2,1,0:T(1,128)}), s32[128,1,2]{2,1,0:T(1,128)S(1)}, u32[]{:S(2)}, u32[]{:S(2)}) %all-to-all-start) | async-done | bytes 1056 | tf_op jit(solution)/shard_map/all_to_all | solution.py:151
  29.6 1.5 gather_fusion
  31.9 2.1 %broadcast_select_fusion = bf16[128,2,2176]{2,1,0:T(2,128)(2,1)} fusion(bf16[128,2,2176]{2,1,0:T(2,128)(2,1)S(1)} %reshape.86, pred[128,2]{1,0:T(8,128)(4,1)S(1)} %copy.46), kind=kLoop, calls=%fused_computation.2 | loop fusion | flops 557056 | bytes 2228480 | tf_op jit(solution)/shard_map/jit(_take)/select_n | solution.py:164
  34.0 10.3 %all-to-all-start.1 = ((bf16[128,2,2176]{2,1,0:T(2,128)(2,1)}), bf16[128,2,2176]{2,1,0:T(2,128)(2,1)S(1)}, u32[]{:S(2)}, u32[]{:S(2)}) async-start(bf16[128,2,2176]{2,1,0:T(2,128)(2,1)} %broadcast_select_fusion), calls=%async_computation.1 | async-start | bytes 2228224 | tf_op jit(solution)/shard_map/all_to_all | solution.py:165
  44.4 6.2 %slice_reduce_fusion = (bf16[147456]{0:T(1024)(128)(2,1)S(1)}, bf16[147456]{0:T(1024)(128)(2,1)S(1)}) fusion(bf16[2,147456]{1,0:T(2,128)(2,1)S(1)} %copy-done.1), kind=kLoop, calls=%fused_computation.22 | loop fusion | bytes 1179648 | tf_op jit(solution)/shard_map/slice | solution.py:130
  50.6 25.3 %all-to-all-done.1 = bf16[128,2,2176]{2,1,0:T(2,128)(2,1)S(1)} async-done(((bf16[128,2,2176]{2,1,0:T(2,128)(2,1)}), bf16[128,2,2176]{2,1,0:T(2,128)(2,1)S(1)}, u32[]{:S(2)}, u32[]{:S(2)}) %all-to-all-start.1) | async-done | bytes 1114144 | tf_op jit(solution)/shard_map/all_to_all | solution.py:165
  76.0 0.6 reshape.82
  76.6 1.0 gather_fusion.1
  78.4 1.4 fusion.15
  80.0 1.4 convert_reduce_fusion
  82.3 1.4 fusion.5
  83.7 4.9 %fusion.4 = f32[3,3,128,128]{3,2,1,0:T(8,128)S(1)} fusion(bf16[128,4,4,128]{0,3,2,1:T(8,128)(2,1)S(1)} %bitcast.53, pred[128,4,4,128]{3,0,2,1:T(32,128)(4,1)S(1)} %and_convert_fusion.1, bf16[3,3,128,128]{2,3,1,0:T(8,128)(2,1)S(1)} %bitcast.57, bf16[128,128]{1,0:T(8,128)(2,1)S(1)} %convolution_multiply_fusion, u8[128,4,128]{2,0,1:T(8,128)(4,1)S(1)} %fusion.16), kind=kOutput, calls=%fused_computation.10 | convolution fusion | flops 840695808 | bytes 1769472 | tf_op jit(solution)/shard_map/conv_general_dilated | solution.py:43
  88.7 2.1 %maximum_bitcast_fusion = f32[128,2,1152]{2,1,0:T(2,128)} fusion(f32[1,128,1152]{2,0,1:T(1,128)S(1)} %bitcast.54, f32[1,128,1152]{2,0,1:T(1,128)S(1)} %bitcast.55), kind=kLoop, calls=%fused_computation.11 | loop fusion | flops 294912 | bytes 2359296 | tf_op jit(solution)/shard_map/transpose | solution.py:184
  90.7 6.2 %all-to-all-start.2 = ((f32[128,2,1152]{2,1,0:T(2,128)}), f32[128,2,1152]{2,1,0:T(2,128)S(1)}, u32[]{:S(2)}, u32[]{:S(2)}) async-start(f32[128,2,1152]{2,1,0:T(2,128)} %maximum_bitcast_fusion), calls=%async_computation.2 | async-start | bytes 2359296 | tf_op jit(solution)/shard_map/all_to_all | solution.py:183
  97.0 2.9 %collective-permute-start = (f32[3,1152]{1,0:T(4,128)S(1)}, f32[3,1152]{1,0:T(4,128)S(1)}, u32[]{:S(2)}, u32[]{:S(2)}) collective-permute-start(f32[3,1152]{1,0:T(4,128)S(1)} %pad_maximum_fusion), channel_id=1, source_target_pairs={{0,1},{1,0},{2,3},{3,2},{4,5},{5,4},{6,7},{7,6},{8,9},{9,8},{10,11... | collective-permute-start | bytes 41480 | tf_op jit(solution)/shard_map/ppermute | solution.py:134
  100.0 2.0 %collective-permute-done = f32[3,1152]{1,0:T(4,128)S(1)} collective-permute-done((f32[3,1152]{1,0:T(4,128)S(1)}, f32[3,1152]{1,0:T(4,128)S(1)}, u32[]{:S(2)}, u32[]{:S(2)}) %collective-permute-start) | collective-permute-done | bytes 13856 | tf_op jit(solution)/shard_map/ppermute | solution.py:134
  101.9 27.9 %all-to-all-done.2 = f32[128,2,1152]{2,1,0:T(2,128)S(1)} async-done(((f32[128,2,1152]{2,1,0:T(2,128)}), f32[128,2,1152]{2,1,0:T(2,128)S(1)}, u32[]{:S(2)}, u32[]{:S(2)}) %all-to-all-start.2) | async-done | bytes 1179680 | tf_op jit(solution)/shard_map/all_to_all | solution.py:183
  129.9 0.5 reduce_sum.69
  130.3 2.7 %collective-permute-start.1 = (f32[2,1152]{1,0:T(2,128)S(1)}, f32[2,1152]{1,0:T(2,128)S(1)}, u32[]{:S(2)}, u32[]{:S(2)}) collective-permute-start(f32[2,1152]{1,0:T(2,128)S(1)} %reduce_sum.69), channel_id=1, source_target_pairs={{0,1},{1,0},{2,3},{3,2},{4,5},{5,4},{6,7},{7,6},{8,9},{9,8},{10,11... | collective-permute-start | bytes 27656 | tf_op jit(solution)/shard_map/ppermute | solution.py:191
  133.1 1.3 collective-permute-done.1
  134.5 1.1 broadcast_in_dim.77
  135.6 7.4 %all-to-all-start.3 = ((bf16[128,2,1152]{2,1,0:T(2,128)(2,1)}), bf16[128,2,1152]{2,1,0:T(2,128)(2,1)S(1)}, u32[]{:S(2)}, u32[]{:S(2)}) async-start(bf16[128,2,1152]{2,1,0:T(2,128)(2,1)} %broadcast_in_dim.77), calls=%async_computation.3 | async-start | bytes 1179648 | tf_op jit(solution)/shard_map/all_to_all | solution.py:197
  142.9 0.6 constant_dynamic-slice_fusion
  143.5 20.7 %all-to-all-done.3 = bf16[128,2,1152]{2,1,0:T(2,128)(2,1)S(1)} async-done(((bf16[128,2,1152]{2,1,0:T(2,128)(2,1)}), bf16[128,2,1152]{2,1,0:T(2,128)(2,1)S(1)}, u32[]{:S(2)}, u32[]{:S(2)}) %all-to-all-start.3) | async-done | bytes 589856 | tf_op jit(solution)/shard_map/all_to_all | solution.py:197
  164.3 0.8 copy.68
  (50 shorter events, 3.4 us)
Async XLA Ops:
  0.6 81.2 %copy-start = (bf16[128,18]{0,1:T(8,128)(2,1)S(1)}, bf16[128,18]{0,1:T(8,128)(2,1)}, u32[]{:S(2)}) copy-start(bf16[128,18]{0,1:T(8,128)(2,1)} %param.18) | copy-start | bytes 13828
  3.8 25.4 %all-to-all-start = ((s32[128,1,2]{2,1,0:T(1,128)}), s32[128,1,2]{2,1,0:T(1,128)S(1)}, u32[]{:S(2)}, u32[]{:S(2)}) async-start(s32[128,1,2]{2,1,0:T(1,128)} %bitcast.2), calls=%async_computation | async-start | bytes 131072 | tf_op jit(solution)/shard_map/all_to_all | solution.py:151
  18.5 4.5 %copy-start.3 = (bf16[512,18]{0,1:T(8,128)(2,1)S(1)}, bf16[512,18]{0,1:T(8,128)(2,1)}, u32[]{:S(2)}) copy-start(bf16[512,18]{0,1:T(8,128)(2,1)} %param.12) | copy-start | bytes 55300
  18.6 4.7 %copy-start.4 = (bf16[512,18]{0,1:T(8,128)(2,1)S(1)}, bf16[512,18]{0,1:T(8,128)(2,1)}, u32[]{:S(2)}) copy-start(bf16[512,18]{0,1:T(8,128)(2,1)} %param.13) | copy-start | bytes 55300
  34.0 10.3 %copy-start.1 = (bf16[2,147456]{1,0:T(2,128)(2,1)S(1)}, bf16[2,147456]{1,0:T(2,128)(2,1)}, u32[]{:S(2)}) copy-start(bf16[2,147456]{1,0:T(2,128)(2,1)} %param.17) | copy-start | bytes 1769476
  34.0 41.9 %all-to-all-start.1 = ((bf16[128,2,2176]{2,1,0:T(2,128)(2,1)}), bf16[128,2,2176]{2,1,0:T(2,128)(2,1)S(1)}, u32[]{:S(2)}, u32[]{:S(2)}) async-start(bf16[128,2,2176]{2,1,0:T(2,128)(2,1)} %broadcast_select_fusion), calls=%async_computation.1 | async-start | bytes 2228224 | tf_op jit(solution)/shard_map/all_to_all | solution.py:165
  78.0 1.8 %copy-start.2 = (s32[128,20]{0,1:T(8,128)S(1)}, s32[128,20]{0,1:T(8,128)}, u32[]{:S(2)}) copy-start(s32[128,20]{0,1:T(8,128)} %param.16) | copy-start | bytes 30724
  90.7 6.2 %copy-start.5 = (f32[1,1152]{1,0:T(1,128)S(1)}, f32[1,1152]{1,0:T(1,128)}, u32[]{:S(2)}) copy-start(f32[1,1152]{1,0:T(1,128)} %param.21) | copy-start | bytes 13828
  90.7 6.2 %copy-start.6 = (f32[1,1152]{1,0:T(1,128)S(1)}, f32[1,1152]{1,0:T(1,128)}, u32[]{:S(2)}) copy-start(f32[1,1152]{1,0:T(1,128)} %param.20) | copy-start | bytes 13828
  90.7 6.2 %copy-start.7 = (f32[1,1152]{1,0:T(1,128)S(1)}, f32[1,1152]{1,0:T(1,128)}, u32[]{:S(2)}) copy-start(f32[1,1152]{1,0:T(1,128)} %param.19) | copy-start | bytes 13828
  90.7 39.1 %all-to-all-start.2 = ((f32[128,2,1152]{2,1,0:T(2,128)}), f32[128,2,1152]{2,1,0:T(2,128)S(1)}, u32[]{:S(2)}, u32[]{:S(2)}) async-start(f32[128,2,1152]{2,1,0:T(2,128)} %maximum_bitcast_fusion), calls=%async_computation.2 | async-start | bytes 2359296 | tf_op jit(solution)/shard_map/all_to_all | solution.py:183
  97.0 4.9 %collective-permute-start = (f32[3,1152]{1,0:T(4,128)S(1)}, f32[3,1152]{1,0:T(4,128)S(1)}, u32[]{:S(2)}, u32[]{:S(2)}) collective-permute-start(f32[3,1152]{1,0:T(4,128)S(1)} %pad_maximum_fusion), channel_id=1, source_target_pairs={{0,1},{1,0},{2,3},{3,2},{4,5},{5,4},{6,7},{7,6},{8,9},{9,8},{10,11... | collective-permute-start | bytes 41480 | tf_op jit(solution)/shard_map/ppermute | solution.py:134
  130.3 4.1 %collective-permute-start.1 = (f32[2,1152]{1,0:T(2,128)S(1)}, f32[2,1152]{1,0:T(2,128)S(1)}, u32[]{:S(2)}, u32[]{:S(2)}) collective-permute-start(f32[2,1152]{1,0:T(2,128)S(1)} %reduce_sum.69), channel_id=1, source_target_pairs={{0,1},{1,0},{2,3},{3,2},{4,5},{5,4},{6,7},{7,6},{8,9},{9,8},{10,11... | collective-permute-start | bytes 27656 | tf_op jit(solution)/shard_map/ppermute | solution.py:191
  135.6 28.7 %all-to-all-start.3 = ((bf16[128,2,1152]{2,1,0:T(2,128)(2,1)}), bf16[128,2,1152]{2,1,0:T(2,128)(2,1)S(1)}, u32[]{:S(2)}, u32[]{:S(2)}) async-start(bf16[128,2,1152]{2,1,0:T(2,128)(2,1)} %broadcast_in_dim.77), calls=%async_computation.3 | async-start | bytes 1179648 | tf_op jit(solution)/shard_map/all_to_all | solution.py:197

commit v8 on v7

--- a/solution.py
+++ b/solution.py
@@ -147,9 +147,6 @@
     request = jnp.sum(jnp.where(matches, replay_slot[None, :], 0), axis=1).reshape(
         owners, capacity
     )
-    row_index = jnp.maximum(
-        lax.all_to_all(request, "dp", split_axis=0, concat_axis=0, tiled=True), 0
-    )
     row_width = replay_rows.shape[1] * replay_rows.shape[2] * channels
     actions_n = qvalues.shape[1]
     table = jnp.concatenate(
@@ -160,6 +157,10 @@
             jnp.zeros((qvalues.shape[0], channels - 2 * actions_n), qvalues.dtype),
         ],
         axis=-1,
+    )
+    table, request = lax.optimization_barrier((table, request))
+    row_index = jnp.maximum(
+        lax.all_to_all(request, "dp", split_axis=0, concat_axis=0, tiled=True), 0
     )
     packed = jnp.take(table, row_index, axis=0)
     slots = lax.all_to_all(packed, "dp", split_axis=0, concat_axis=0, tiled=True)

time: 166 us -> 167 us (level)
  blocking collectives: 0 us -> 25.3 us
  starting transfers between devices: 44.2 us -> 25.1 us
  waiting for transfers between devices: 79.5 us -> 77.4 us
  other arithmetic: 8.12 us -> 6.08 us
    all_to_all x0 -> x1, blocking collectives: none -> 25.3 us  [per_device(): lax.all_to_all(request, 'dp', split_axis=0, concat_axis=0, tiled=True)]
    all_to_all x1 -> x0, starting transfers between devices: 14.8 us -> none  [per_device(): lax.all_to_all(request, 'dp', split_axis=0, concat_axis=0, tiled=True)]
    all_to_all x1, starting transfers between devices: 10.3 us -> 5.95 us  [per_device(): lax.all_to_all(packed, 'dp', split_axis=0, concat_axis=0, tiled=True)]
    all_to_all x1 -> x0, waiting for transfers between devices: 2.19 us -> none  [per_device(): lax.all_to_all(request, 'dp', split_axis=0, concat_axis=0, tiled=True)]
  transfers between devices with their start and end apart: 6 -> 5, of which waited for: 6 -> 5; matrix products, arithmetic and copies ran while one was open for 9% -> 4% of each run, Pallas kernels for 0% -> 0%
where the time goes in v8:
time: 167 us
  waiting for transfers between devices  77.4 us (46%)
  blocking collectives  25.3 us (15%)
  starting transfers between devices  25.1 us (15%)
  local copies, waits for them, and re-layouts  22.1 us (13%)
  matrix products  9.63 us (6%)
  other arithmetic  6.08 us (4%)
    all_to_all x1, waiting for transfers between devices, per_device(): lax.all_to_all(loss_derivative.reshape(2, owners, piece_len).transpose(1,...  27.9 us
    all_to_all x1, waiting for transfers between devices, per_device(): lax.all_to_all(packed, 'dp', split_axis=0, concat_axis=0, tiled=True)  25.4 us
    all_to_all x1, blocking collectives, per_device(): lax.all_to_all(request, 'dp', split_axis=0, concat_axis=0, tiled=True)  25.3 us
    all_to_all x1, waiting for transfers between devices, per_device(): lax.all_to_all(jnp.broadcast_to(both_layers[None], (owners, 2, piece_len)...  20.7 us
    all_to_all x1, starting transfers between devices, per_device(): lax.all_to_all(jnp.broadcast_to(both_layers[None], (owners, 2, piece_len)...  7.35 us
    conv_general_dilated x2, matrix products, conv_kernel_grad(): lax.conv_general_dilated(field, out_grad, (1, 1), ((1, 1), (1, 1)), dimen...  6.34 us
    slice x1, local copies, waits for them, and re-layouts, per_device(): second_weight = weights[1].reshape(9 * channels, channels)  6.22 us
    all_to_all x1, starting transfers between devices, per_device(): lax.all_to_all(loss_derivative.reshape(2, owners, piece_len).transpose(1,...  6.21 us
  transfers between devices with their start and end apart: 5, of which 5 were waited for; matrix products, arithmetic and copies ran while one was open for 4% of the time, Pallas kernels for 0%

profile of v8, /device:TPU:1, one launch (start us, length us, event | category | flops | bytes accessed | tf_op | source)
XLA Modules:
  0.0 166.6 jit_solution(15339159136153761611)
XLA Ops:
  0.7 4.5 %reshape.82 = bf16[512,2048]{1,0:T(8,128)(2,1)} reshape(bf16[512,4,4,128]{3,2,1,0:T(4,128)(2,1)} %param.11) | data formatting | bytes 4194304 | tf_op jit(solution)/shard_map/reshape | solution.py:154
  6.0 3.6 %concatenate.8 = bf16[512,2176]{1,0:T(8,128)(2,1)S(1)} concatenate(bf16[512,2048]{1,0:T(8,128)(2,1)} %reshape.82, bf16[512,18]{1,0:T(8,128)(2,1)S(1)} %copy.44, bf16[512,18]{1,0:T(8,128)(2,1)S(1)} %copy.45, bf16[512,92]{1,0:T(8,128)(2,1)S(1)} %broadcast_in_dim.45), dimensions={1} | concatenate | bytes 4456448 | tf_op jit(solution)/shard_map/concatenate | solution.py:152
  9.6 25.3 %all_to_all.24 = s32[128,1,2]{2,1,0:T(1,128)S(1)} all-to-all(s32[128,1,2]{2,1,0:T(1,128)S(1)} %bitcast.60), channel_id=1, replica_groups=mesh['dp'=128,'section'=2] {'dp'}, dimensions={0} | all-to-all | bytes 2048 | tf_op jit(solution)/shard_map/all_to_all | solution.py:163
  35.3 1.5 gather_fusion
  36.8 0.5 reshape.88
  37.7 2.1 %broadcast_select_fusion = bf16[128,2,2176]{2,1,0:T(2,128)(2,1)} fusion(bf16[128,2,2176]{2,1,0:T(2,128)(2,1)S(1)} %reshape.88, pred[128,2]{1,0:T(8,128)(4,1)S(1)} %copy.48), kind=kLoop, calls=%fused_computation.2 | loop fusion | flops 557056 | bytes 2228480 | tf_op jit(solution)/shard_map/jit(_take)/select_n | solution.py:165
  39.8 5.9 %all-to-all-start.1 = ((bf16[128,2,2176]{2,1,0:T(2,128)(2,1)}), bf16[128,2,2176]{2,1,0:T(2,128)(2,1)S(1)}, u32[]{:S(2)}, u32[]{:S(2)}) async-start(bf16[128,2,2176]{2,1,0:T(2,128)(2,1)} %broadcast_select_fusion), calls=%async_computation.1 | async-start | bytes 2228224 | tf_op jit(solution)/shard_map/all_to_all | solution.py:166
  45.7 6.2 %slice_reduce_fusion = (bf16[147456]{0:T(1024)(128)(2,1)S(1)}, bf16[147456]{0:T(1024)(128)(2,1)S(1)}) fusion(bf16[2,147456]{1,0:T(2,128)(2,1)S(1)} %copy-done.1), kind=kLoop, calls=%fused_computation.22 | loop fusion | bytes 1179648 | tf_op jit(solution)/shard_map/slice | solution.py:130
  52.0 25.4 %all-to-all-done.1 = bf16[128,2,2176]{2,1,0:T(2,128)(2,1)S(1)} async-done(((bf16[128,2,2176]{2,1,0:T(2,128)(2,1)}), bf16[128,2,2176]{2,1,0:T(2,128)(2,1)S(1)}, u32[]{:S(2)}, u32[]{:S(2)}) %all-to-all-start.1) | async-done | bytes 1114144 | tf_op jit(solution)/shard_map/all_to_all | solution.py:166
  77.5 0.6 reshape.84
  78.1 1.0 gather_fusion.1
  79.1 0.3 copy.49
  79.6 0.3 copy.50
  79.9 1.4 fusion.15
  81.5 1.4 convert_reduce_fusion
  83.1 0.2 and_convert_fusion.1
  83.5 0.3 convolution_multiply_fusion
  83.8 1.4 fusion.5
  85.2 4.9 %fusion.4 = f32[3,3,128,128]{3,2,1,0:T(8,128)S(1)} fusion(bf16[128,4,4,128]{0,3,2,1:T(8,128)(2,1)S(1)} %bitcast.55, pred[128,4,4,128]{3,0,2,1:T(32,128)(4,1)S(1)} %and_convert_fusion.1, bf16[3,3,128,128]{2,3,1,0:T(8,128)(2,1)S(1)} %bitcast.59, bf16[128,128]{1,0:T(8,128)(2,1)S(1)} %convolution_multiply_fusion, u8[128,4,128]{2,0,1:T(8,128)(4,1)S(1)} %fusion.16), kind=kOutput, calls=%fused_computation.10 | convolution fusion | flops 840695808 | bytes 1769472 | tf_op jit(solution)/shard_map/conv_general_dilated | solution.py:43
  90.2 2.1 %maximum_bitcast_fusion = f32[128,2,1152]{2,1,0:T(2,128)} fusion(f32[1,128,1152]{2,0,1:T(1,128)S(1)} %bitcast.56, f32[1,128,1152]{2,0,1:T(1,128)S(1)} %bitcast.57), kind=kLoop, calls=%fused_computation.11 | loop fusion | flops 294912 | bytes 2359296 | tf_op jit(solution)/shard_map/transpose | solution.py:185
  92.3 6.2 %all-to-all-start.2 = ((f32[128,2,1152]{2,1,0:T(2,128)}), f32[128,2,1152]{2,1,0:T(2,128)S(1)}, u32[]{:S(2)}, u32[]{:S(2)}) async-start(f32[128,2,1152]{2,1,0:T(2,128)} %maximum_bitcast_fusion), calls=%async_computation.2 | async-start | bytes 2359296 | tf_op jit(solution)/shard_map/all_to_all | solution.py:184
  98.5 2.9 %collective-permute-start = (f32[3,1152]{1,0:T(4,128)S(1)}, f32[3,1152]{1,0:T(4,128)S(1)}, u32[]{:S(2)}, u32[]{:S(2)}) collective-permute-start(f32[3,1152]{1,0:T(4,128)S(1)} %pad_maximum_fusion), channel_id=1, source_target_pairs={{0,1},{1,0},{2,3},{3,2},{4,5},{5,4},{6,7},{7,6},{8,9},{9,8},{10,11... | collective-permute-start | bytes 41480 | tf_op jit(solution)/shard_map/ppermute | solution.py:134
  101.5 2.0 %collective-permute-done = f32[3,1152]{1,0:T(4,128)S(1)} collective-permute-done((f32[3,1152]{1,0:T(4,128)S(1)}, f32[3,1152]{1,0:T(4,128)S(1)}, u32[]{:S(2)}, u32[]{:S(2)}) %collective-permute-start) | collective-permute-done | bytes 13856 | tf_op jit(solution)/shard_map/ppermute | solution.py:134
  103.5 27.9 %all-to-all-done.2 = f32[128,2,1152]{2,1,0:T(2,128)S(1)} async-done(((f32[128,2,1152]{2,1,0:T(2,128)}), f32[128,2,1152]{2,1,0:T(2,128)S(1)}, u32[]{:S(2)}, u32[]{:S(2)}) %all-to-all-start.2) | async-done | bytes 1179680 | tf_op jit(solution)/shard_map/all_to_all | solution.py:184
  131.4 0.5 reduce_sum.69
  131.8 2.7 %collective-permute-start.1 = (f32[2,1152]{1,0:T(2,128)S(1)}, f32[2,1152]{1,0:T(2,128)S(1)}, u32[]{:S(2)}, u32[]{:S(2)}) collective-permute-start(f32[2,1152]{1,0:T(2,128)S(1)} %reduce_sum.69), channel_id=1, source_target_pairs={{0,1},{1,0},{2,3},{3,2},{4,5},{5,4},{6,7},{7,6},{8,9},{9,8},{10,11... | collective-permute-start | bytes 27656 | tf_op jit(solution)/shard_map/ppermute | solution.py:192
  134.6 1.4 collective-permute-done.1
  136.0 1.1 broadcast_in_dim.77
  137.1 7.4 %all-to-all-start.3 = ((bf16[128,2,1152]{2,1,0:T(2,128)(2,1)}), bf16[128,2,1152]{2,1,0:T(2,128)(2,1)S(1)}, u32[]{:S(2)}, u32[]{:S(2)}) async-start(bf16[128,2,1152]{2,1,0:T(2,128)(2,1)} %broadcast_in_dim.77), calls=%async_computation.3 | async-start | bytes 1179648 | tf_op jit(solution)/shard_map/all_to_all | solution.py:198
  144.5 0.6 constant_dynamic-slice_fusion
  145.1 20.7 %all-to-all-done.3 = bf16[128,2,1152]{2,1,0:T(2,128)(2,1)S(1)} async-done(((bf16[128,2,1152]{2,1,0:T(2,128)(2,1)}), bf16[128,2,1152]{2,1,0:T(2,128)(2,1)S(1)}, u32[]{:S(2)}, u32[]{:S(2)}) %all-to-all-start.3) | async-done | bytes 589856 | tf_op jit(solution)/shard_map/all_to_all | solution.py:198
  165.8 0.8 copy.68
  (53 shorter events, 2.3 us)
Async XLA Ops:
  0.6 82.7 %copy-start = (bf16[128,18]{0,1:T(8,128)(2,1)S(1)}, bf16[128,18]{0,1:T(8,128)(2,1)}, u32[]{:S(2)}) copy-start(bf16[128,18]{0,1:T(8,128)(2,1)} %param.18) | copy-start | bytes 13828
  0.6 4.6 %copy-start.3 = (bf16[512,18]{0,1:T(8,128)(2,1)S(1)}, bf16[512,18]{0,1:T(8,128)(2,1)}, u32[]{:S(2)}) copy-start(bf16[512,18]{0,1:T(8,128)(2,1)} %param.12) | copy-start | bytes 55300
  0.7 4.7 %copy-start.4 = (bf16[512,18]{0,1:T(8,128)(2,1)S(1)}, bf16[512,18]{0,1:T(8,128)(2,1)}, u32[]{:S(2)}) copy-start(bf16[512,18]{0,1:T(8,128)(2,1)} %param.13) | copy-start | bytes 55300
  0.7 4.8 %copy-start.8 = (s32[128]{0:T(128)S(1)}, s32[128]{0:T(128)}, u32[]{:S(2)}) copy-start(s32[128]{0:T(128)} %param.14) | copy-start | bytes 1540
  0.7 5.0 %copy-start.9 = (s32[128]{0:T(128)S(1)}, s32[128]{0:T(128)}, u32[]{:S(2)}) copy-start(s32[128]{0:T(128)} %param.15) | copy-start | bytes 1540
  39.8 6.0 %copy-start.1 = (bf16[2,147456]{1,0:T(2,128)(2,1)S(1)}, bf16[2,147456]{1,0:T(2,128)(2,1)}, u32[]{:S(2)}) copy-start(bf16[2,147456]{1,0:T(2,128)(2,1)} %param.17) | copy-start | bytes 1769476
  39.8 37.7 %all-to-all-start.1 = ((bf16[128,2,2176]{2,1,0:T(2,128)(2,1)}), bf16[128,2,2176]{2,1,0:T(2,128)(2,1)S(1)}, u32[]{:S(2)}, u32[]{:S(2)}) async-start(bf16[128,2,2176]{2,1,0:T(2,128)(2,1)} %broadcast_select_fusion), calls=%async_computation.1 | async-start | bytes 2228224 | tf_op jit(solution)/shard_map/all_to_all | solution.py:166
  79.6 1.8 %copy-start.2 = (s32[128,20]{0,1:T(8,128)S(1)}, s32[128,20]{0,1:T(8,128)}, u32[]{:S(2)}) copy-start(s32[128,20]{0,1:T(8,128)} %param.16) | copy-start | bytes 30724
  92.2 6.2 %copy-start.5 = (f32[1,1152]{1,0:T(1,128)S(1)}, f32[1,1152]{1,0:T(1,128)}, u32[]{:S(2)}) copy-start(f32[1,1152]{1,0:T(1,128)} %param.21) | copy-start | bytes 13828
  92.2 6.2 %copy-start.6 = (f32[1,1152]{1,0:T(1,128)S(1)}, f32[1,1152]{1,0:T(1,128)}, u32[]{:S(2)}) copy-start(f32[1,1152]{1,0:T(1,128)} %param.20) | copy-start | bytes 13828
  92.3 6.2 %copy-start.7 = (f32[1,1152]{1,0:T(1,128)S(1)}, f32[1,1152]{1,0:T(1,128)}, u32[]{:S(2)}) copy-start(f32[1,1152]{1,0:T(1,128)} %param.19) | copy-start | bytes 13828
  92.3 39.1 %all-to-all-start.2 = ((f32[128,2,1152]{2,1,0:T(2,128)}), f32[128,2,1152]{2,1,0:T(2,128)S(1)}, u32[]{:S(2)}, u32[]{:S(2)}) async-start(f32[128,2,1152]{2,1,0:T(2,128)} %maximum_bitcast_fusion), calls=%async_computation.2 | async-start | bytes 2359296 | tf_op jit(solution)/shard_map/all_to_all | solution.py:184
  98.5 4.9 %collective-permute-start = (f32[3,1152]{1,0:T(4,128)S(1)}, f32[3,1152]{1,0:T(4,128)S(1)}, u32[]{:S(2)}, u32[]{:S(2)}) collective-permute-start(f32[3,1152]{1,0:T(4,128)S(1)} %pad_maximum_fusion), channel_id=1, source_target_pairs={{0,1},{1,0},{2,3},{3,2},{4,5},{5,4},{6,7},{7,6},{8,9},{9,8},{10,11... | collective-permute-start | bytes 41480 | tf_op jit(solution)/shard_map/ppermute | solution.py:134
  131.8 4.1 %collective-permute-start.1 = (f32[2,1152]{1,0:T(2,128)S(1)}, f32[2,1152]{1,0:T(2,128)S(1)}, u32[]{:S(2)}, u32[]{:S(2)}) collective-permute-start(f32[2,1152]{1,0:T(2,128)S(1)} %reduce_sum.69), channel_id=1, source_target_pairs={{0,1},{1,0},{2,3},{3,2},{4,5},{5,4},{6,7},{7,6},{8,9},{9,8},{10,11... | collective-permute-start | bytes 27656 | tf_op jit(solution)/shard_map/ppermute | solution.py:192
  137.1 28.7 %all-to-all-start.3 = ((bf16[128,2,1152]{2,1,0:T(2,128)(2,1)}), bf16[128,2,1152]{2,1,0:T(2,128)(2,1)S(1)}, u32[]{:S(2)}, u32[]{:S(2)}) async-start(bf16[128,2,1152]{2,1,0:T(2,128)(2,1)} %broadcast_in_dim.77), calls=%async_computation.3 | async-start | bytes 1179648 | tf_op jit(solution)/shard_map/all_to_all | solution.py:198

commit v9 on v7

--- a/solution.py
+++ b/solution.py
@@ -147,9 +147,7 @@
     request = jnp.sum(jnp.where(matches, replay_slot[None, :], 0), axis=1).reshape(
         owners, capacity
     )
-    row_index = jnp.maximum(
-        lax.all_to_all(request, "dp", split_axis=0, concat_axis=0, tiled=True), 0
-    )
+    row_index = lax.all_to_all(request, "dp", split_axis=0, concat_axis=0, tiled=True)
     row_width = replay_rows.shape[1] * replay_rows.shape[2] * channels
     actions_n = qvalues.shape[1]
     table = jnp.concatenate(

time: 166 us -> 165 us (level)
  no operation moved by 1% of the time
where the time goes in v9:
time: 165 us
  waiting for transfers between devices  79.5 us (48%)
  starting transfers between devices  44.2 us (27%)
  local copies, waits for them, and re-layouts  22.4 us (14%)
  matrix products  9.62 us (6%)
  other arithmetic  7.84 us (5%)
    all_to_all x1, waiting for transfers between devices, per_device(): lax.all_to_all(loss_derivative.reshape(2, owners, piece_len).transpose(1,...  27.9 us
    all_to_all x1, waiting for transfers between devices, per_device(): lax.all_to_all(packed, 'dp', split_axis=0, concat_axis=0, tiled=True)  25.3 us
    all_to_all x1, waiting for transfers between devices, per_device(): lax.all_to_all(jnp.broadcast_to(both_layers[None], (owners, 2, piece_len)...  20.7 us
    all_to_all x1, starting transfers between devices, per_device(): lax.all_to_all(request, 'dp', split_axis=0, concat_axis=0, tiled=True)  14.8 us
    all_to_all x1, starting transfers between devices, per_device(): lax.all_to_all(packed, 'dp', split_axis=0, concat_axis=0, tiled=True)  10.3 us
    all_to_all x1, starting transfers between devices, per_device(): lax.all_to_all(jnp.broadcast_to(both_layers[None], (owners, 2, piece_len)...  7.35 us
    conv_general_dilated x2, matrix products, conv_kernel_grad(): lax.conv_general_dilated(field, out_grad, (1, 1), ((1, 1), (1, 1)), dimen...  6.34 us
    slice x1, local copies, waits for them, and re-layouts, per_device(): second_weight = weights[1].reshape(9 * channels, channels)  6.22 us
  transfers between devices with their start and end apart: 6, of which 6 were waited for; matrix products, arithmetic and copies ran while one was open for 9% of the time, Pallas kernels for 0%

profile of v9, /device:TPU:1, one launch (start us, length us, event | category | flops | bytes accessed | tf_op | source)
XLA Modules:
  0.0 164.5 jit_solution(424659998619643300)
XLA Ops:
  0.6 0.9 convert_reduce_fusion.1
  1.6 0.7 compare_and_fusion.1
  2.2 0.8 select_reduce_fusion.2
  3.0 0.8 all_to_all.19
  3.8 14.8 %all-to-all-start = ((s32[128,1,2]{2,1,0:T(1,128)}), s32[128,1,2]{2,1,0:T(1,128)S(1)}, u32[]{:S(2)}, u32[]{:S(2)}) async-start(s32[128,1,2]{2,1,0:T(1,128)} %bitcast.2), calls=%async_computation | async-start | bytes 131072 | tf_op jit(solution)/shard_map/all_to_all | solution.py:150
  18.6 4.5 %reshape.93 = bf16[512,2048]{1,0:T(8,128)(2,1)} reshape(bf16[512,4,4,128]{3,2,1,0:T(4,128)(2,1)} %param.11) | data formatting | bytes 4194304 | tf_op jit(solution)/shard_map/reshape | solution.py:155
  23.4 3.6 %concatenate.8 = bf16[512,2176]{1,0:T(8,128)(2,1)S(1)} concatenate(bf16[512,2048]{1,0:T(8,128)(2,1)} %reshape.93, bf16[512,18]{1,0:T(8,128)(2,1)S(1)} %copy.34, bf16[512,18]{1,0:T(8,128)(2,1)S(1)} %copy.35, bf16[512,92]{1,0:T(8,128)(2,1)S(1)} %broadcast_in_dim.72), dimensions={1} | concatenate | bytes 4456448 | tf_op jit(solution)/shard_map/concatenate | solution.py:153
  27.0 2.2 %all-to-all-done = s32[128,1,2]{2,1,0:T(1,128)S(1)} async-done(((s32[128,1,2]{2,1,0:T(1,128)}), s32[128,1,2]{2,1,0:T(1,128)S(1)}, u32[]{:S(2)}, u32[]{:S(2)}) %all-to-all-start) | async-done | bytes 1056 | tf_op jit(solution)/shard_map/all_to_all | solution.py:150
  29.4 1.5 gather_fusion
  31.4 2.1 %broadcast_select_fusion = bf16[128,2,2176]{2,1,0:T(2,128)(2,1)} fusion(bf16[128,2,2176]{2,1,0:T(2,128)(2,1)S(1)} %reshape.98, pred[128,2]{1,0:T(8,128)(4,1)S(1)} %compare_and_fusion), kind=kLoop, calls=%fused_computation.2 | loop fusion | flops 557056 | bytes 2228480 | tf_op jit(solution)/shard_map/jit(_take)/select_n | solution.py:162
  33.5 10.3 %all-to-all-start.1 = ((bf16[128,2,2176]{2,1,0:T(2,128)(2,1)}), bf16[128,2,2176]{2,1,0:T(2,128)(2,1)S(1)}, u32[]{:S(2)}, u32[]{:S(2)}) async-start(bf16[128,2,2176]{2,1,0:T(2,128)(2,1)} %broadcast_select_fusion), calls=%async_computation.1 | async-start | bytes 2228224 | tf_op jit(solution)/shard_map/all_to_all | solution.py:163
  43.8 6.2 %slice_reduce_fusion = (bf16[147456]{0:T(1024)(128)(2,1)S(1)}, bf16[147456]{0:T(1024)(128)(2,1)S(1)}) fusion(bf16[2,147456]{1,0:T(2,128)(2,1)S(1)} %copy-done.1), kind=kLoop, calls=%fused_computation.22 | loop fusion | bytes 1179648 | tf_op jit(solution)/shard_map/slice | solution.py:130
  50.1 25.3 %all-to-all-done.1 = bf16[128,2,2176]{2,1,0:T(2,128)(2,1)S(1)} async-done(((bf16[128,2,2176]{2,1,0:T(2,128)(2,1)}), bf16[128,2,2176]{2,1,0:T(2,128)(2,1)S(1)}, u32[]{:S(2)}, u32[]{:S(2)}) %all-to-all-start.1) | async-done | bytes 1114144 | tf_op jit(solution)/shard_map/all_to_all | solution.py:163
  75.4 0.6 reshape.94
  76.1 1.0 gather_fusion.1
  77.8 1.4 fusion.15
  79.5 1.4 convert_reduce_fusion
  81.8 1.4 fusion.5
  83.2 4.9 %fusion.4 = f32[3,3,128,128]{3,2,1,0:T(8,128)S(1)} fusion(bf16[128,4,4,128]{0,3,2,1:T(8,128)(2,1)S(1)} %bitcast.56, pred[128,4,4,128]{3,0,2,1:T(32,128)(4,1)S(1)} %and_convert_fusion.1, bf16[3,3,128,128]{2,3,1,0:T(8,128)(2,1)S(1)} %bitcast.62, bf16[128,128]{1,0:T(8,128)(2,1)S(1)} %convolution_multiply_fusion, u8[128,4,128]{2,0,1:T(8,128)(4,1)S(1)} %fusion.16), kind=kOutput, calls=%fused_computation.10 | convolution fusion | flops 840695808 | bytes 1769472 | tf_op jit(solution)/shard_map/conv_general_dilated | solution.py:43
  88.1 2.1 %maximum_bitcast_fusion = f32[128,2,1152]{2,1,0:T(2,128)} fusion(f32[1,128,1152]{2,0,1:T(1,128)S(1)} %bitcast.59, f32[1,128,1152]{2,0,1:T(1,128)S(1)} %bitcast.60), kind=kLoop, calls=%fused_computation.11 | loop fusion | flops 294912 | bytes 2359296 | tf_op jit(solution)/shard_map/transpose | solution.py:182
  90.2 6.2 %all-to-all-start.2 = ((f32[128,2,1152]{2,1,0:T(2,128)}), f32[128,2,1152]{2,1,0:T(2,128)S(1)}, u32[]{:S(2)}, u32[]{:S(2)}) async-start(f32[128,2,1152]{2,1,0:T(2,128)} %maximum_bitcast_fusion), calls=%async_computation.2 | async-start | bytes 2359296 | tf_op jit(solution)/shard_map/all_to_all | solution.py:181
  96.5 2.9 %collective-permute-start = (f32[3,1152]{1,0:T(4,128)S(1)}, f32[3,1152]{1,0:T(4,128)S(1)}, u32[]{:S(2)}, u32[]{:S(2)}) collective-permute-start(f32[3,1152]{1,0:T(4,128)S(1)} %pad_maximum_fusion), channel_id=1, source_target_pairs={{0,1},{1,0},{2,3},{3,2},{4,5},{5,4},{6,7},{7,6},{8,9},{9,8},{10,11... | collective-permute-start | bytes 41480 | tf_op jit(solution)/shard_map/ppermute | solution.py:134
  99.4 2.0 %collective-permute-done = f32[3,1152]{1,0:T(4,128)S(1)} collective-permute-done((f32[3,1152]{1,0:T(4,128)S(1)}, f32[3,1152]{1,0:T(4,128)S(1)}, u32[]{:S(2)}, u32[]{:S(2)}) %collective-permute-start) | collective-permute-done | bytes 13856 | tf_op jit(solution)/shard_map/ppermute | solution.py:134
  101.4 27.9 %all-to-all-done.2 = f32[128,2,1152]{2,1,0:T(2,128)S(1)} async-done(((f32[128,2,1152]{2,1,0:T(2,128)}), f32[128,2,1152]{2,1,0:T(2,128)S(1)}, u32[]{:S(2)}, u32[]{:S(2)}) %all-to-all-start.2) | async-done | bytes 1179680 | tf_op jit(solution)/shard_map/all_to_all | solution.py:181
  129.3 0.5 reduce_sum.69
  129.8 2.7 %collective-permute-start.1 = (f32[2,1152]{1,0:T(2,128)S(1)}, f32[2,1152]{1,0:T(2,128)S(1)}, u32[]{:S(2)}, u32[]{:S(2)}) collective-permute-start(f32[2,1152]{1,0:T(2,128)S(1)} %reduce_sum.69), channel_id=1, source_target_pairs={{0,1},{1,0},{2,3},{3,2},{4,5},{5,4},{6,7},{7,6},{8,9},{9,8},{10,11... | collective-permute-start | bytes 27656 | tf_op jit(solution)/shard_map/ppermute | solution.py:189
  132.5 1.4 collective-permute-done.1
  133.9 1.1 broadcast_in_dim.77
  135.1 7.4 %all-to-all-start.3 = ((bf16[128,2,1152]{2,1,0:T(2,128)(2,1)}), bf16[128,2,1152]{2,1,0:T(2,128)(2,1)S(1)}, u32[]{:S(2)}, u32[]{:S(2)}) async-start(bf16[128,2,1152]{2,1,0:T(2,128)(2,1)} %broadcast_in_dim.77), calls=%async_computation.3 | async-start | bytes 1179648 | tf_op jit(solution)/shard_map/all_to_all | solution.py:195
  142.4 0.6 constant_dynamic-slice_fusion
  143.0 20.7 %all-to-all-done.3 = bf16[128,2,1152]{2,1,0:T(2,128)(2,1)S(1)} async-done(((bf16[128,2,1152]{2,1,0:T(2,128)(2,1)}), bf16[128,2,1152]{2,1,0:T(2,128)(2,1)S(1)}, u32[]{:S(2)}, u32[]{:S(2)}) %all-to-all-start.3) | async-done | bytes 589856 | tf_op jit(solution)/shard_map/all_to_all | solution.py:195
  163.7 0.8 copy.55
  (48 shorter events, 2.9 us)
Async XLA Ops:
  0.6 80.7 %copy-start = (bf16[128,18]{0,1:T(8,128)(2,1)S(1)}, bf16[128,18]{0,1:T(8,128)(2,1)}, u32[]{:S(2)}) copy-start(bf16[128,18]{0,1:T(8,128)(2,1)} %param.18) | copy-start | bytes 13828
  3.8 25.4 %all-to-all-start = ((s32[128,1,2]{2,1,0:T(1,128)}), s32[128,1,2]{2,1,0:T(1,128)S(1)}, u32[]{:S(2)}, u32[]{:S(2)}) async-start(s32[128,1,2]{2,1,0:T(1,128)} %bitcast.2), calls=%async_computation | async-start | bytes 131072 | tf_op jit(solution)/shard_map/all_to_all | solution.py:150
  18.5 4.5 %copy-start.3 = (bf16[512,18]{0,1:T(8,128)(2,1)S(1)}, bf16[512,18]{0,1:T(8,128)(2,1)}, u32[]{:S(2)}) copy-start(bf16[512,18]{0,1:T(8,128)(2,1)} %param.12) | copy-start | bytes 55300
  18.6 4.7 %copy-start.4 = (bf16[512,18]{0,1:T(8,128)(2,1)S(1)}, bf16[512,18]{0,1:T(8,128)(2,1)}, u32[]{:S(2)}) copy-start(bf16[512,18]{0,1:T(8,128)(2,1)} %param.13) | copy-start | bytes 55300
  33.5 10.3 %copy-start.1 = (bf16[2,147456]{1,0:T(2,128)(2,1)S(1)}, bf16[2,147456]{1,0:T(2,128)(2,1)}, u32[]{:S(2)}) copy-start(bf16[2,147456]{1,0:T(2,128)(2,1)} %param.17) | copy-start | bytes 1769476
  33.5 41.9 %all-to-all-start.1 = ((bf16[128,2,2176]{2,1,0:T(2,128)(2,1)}), bf16[128,2,2176]{2,1,0:T(2,128)(2,1)S(1)}, u32[]{:S(2)}, u32[]{:S(2)}) async-start(bf16[128,2,2176]{2,1,0:T(2,128)(2,1)} %broadcast_select_fusion), calls=%async_computation.1 | async-start | bytes 2228224 | tf_op jit(solution)/shard_map/all_to_all | solution.py:163
  77.5 1.8 %copy-start.2 = (s32[128,20]{0,1:T(8,128)S(1)}, s32[128,20]{0,1:T(8,128)}, u32[]{:S(2)}) copy-start(s32[128,20]{0,1:T(8,128)} %param.16) | copy-start | bytes 30724
  90.2 6.2 %copy-start.5 = (f32[1,1152]{1,0:T(1,128)S(1)}, f32[1,1152]{1,0:T(1,128)}, u32[]{:S(2)}) copy-start(f32[1,1152]{1,0:T(1,128)} %param.21) | copy-start | bytes 13828
  90.2 6.2 %copy-start.6 = (f32[1,1152]{1,0:T(1,128)S(1)}, f32[1,1152]{1,0:T(1,128)}, u32[]{:S(2)}) copy-start(f32[1,1152]{1,0:T(1,128)} %param.20) | copy-start | bytes 13828
  90.2 6.2 %copy-start.7 = (f32[1,1152]{1,0:T(1,128)S(1)}, f32[1,1152]{1,0:T(1,128)}, u32[]{:S(2)}) copy-start(f32[1,1152]{1,0:T(1,128)} %param.19) | copy-start | bytes 13828
  90.2 39.1 %all-to-all-start.2 = ((f32[128,2,1152]{2,1,0:T(2,128)}), f32[128,2,1152]{2,1,0:T(2,128)S(1)}, u32[]{:S(2)}, u32[]{:S(2)}) async-start(f32[128,2,1152]{2,1,0:T(2,128)} %maximum_bitcast_fusion), calls=%async_computation.2 | async-start | bytes 2359296 | tf_op jit(solution)/shard_map/all_to_all | solution.py:181
  96.5 4.9 %collective-permute-start = (f32[3,1152]{1,0:T(4,128)S(1)}, f32[3,1152]{1,0:T(4,128)S(1)}, u32[]{:S(2)}, u32[]{:S(2)}) collective-permute-start(f32[3,1152]{1,0:T(4,128)S(1)} %pad_maximum_fusion), channel_id=1, source_target_pairs={{0,1},{1,0},{2,3},{3,2},{4,5},{5,4},{6,7},{7,6},{8,9},{9,8},{10,11... | collective-permute-start | bytes 41480 | tf_op jit(solution)/shard_map/ppermute | solution.py:134
  129.8 4.1 %collective-permute-start.1 = (f32[2,1152]{1,0:T(2,128)S(1)}, f32[2,1152]{1,0:T(2,128)S(1)}, u32[]{:S(2)}, u32[]{:S(2)}) collective-permute-start(f32[2,1152]{1,0:T(2,128)S(1)} %reduce_sum.69), channel_id=1, source_target_pairs={{0,1},{1,0},{2,3},{3,2},{4,5},{5,4},{6,7},{7,6},{8,9},{9,8},{10,11... | collective-permute-start | bytes 27656 | tf_op jit(solution)/shard_map/ppermute | solution.py:189
  135.1 28.7 %all-to-all-start.3 = ((bf16[128,2,1152]{2,1,0:T(2,128)(2,1)}), bf16[128,2,1152]{2,1,0:T(2,128)(2,1)S(1)}, u32[]{:S(2)}, u32[]{:S(2)}) async-start(bf16[128,2,1152]{2,1,0:T(2,128)(2,1)} %broadcast_in_dim.77), calls=%async_computation.3 | async-start | bytes 1179648 | tf_op jit(solution)/shard_map/all_to_all | solution.py:195

commit v10 on v9

--- a/solution.py
+++ b/solution.py
@@ -176,16 +176,18 @@
         second_weight,
         head,
     )
-    loss_derivative = jnp.stack([grad_first.reshape(-1), grad_second.reshape(-1)])
-    piece_len = loss_derivative.shape[1] // owners
+    piece_len = grad_first.size // owners
     contributions = lax.all_to_all(
-        loss_derivative.reshape(2, owners, piece_len).transpose(1, 0, 2),
+        jnp.concatenate(
+            [grad_first.reshape(owners, piece_len), grad_second.reshape(owners, piece_len)],
+            axis=1,
+        ),
         "dp",
         split_axis=0,
         concat_axis=0,
         tiled=True,
     )
-    partial = jnp.sum(contributions, axis=0)
+    partial = jnp.sum(contributions, axis=0).reshape(2, piece_len)
     owned_grad = partial + lax.ppermute(partial, "section", swap)
     first = beta_first * state[1] + (1.0 - beta_first) * owned_grad
     second = beta_second * state[2] + (1.0 - beta_second) * owned_grad * owned_grad

time: 165 us -> 165 us (level)
  local copies, waits for them, and re-layouts: 22.4 us -> 24.5 us
  other arithmetic: 7.84 us -> 6.09 us
    transpose x1 -> x0, other arithmetic: 2.07 us -> none  [per_device(): loss_derivative.reshape(2, owners, piece_len).transpose(1, 0, 2)]
    all_to_all x0 -> x1, local copies, waits for them, and re-layouts: none -> 1.82 us  [per_device(): lax.all_to_all(jnp.concatenate([grad_first.reshape(owners, piece_len), gr...]
where the time goes in v10:
time: 165 us
  waiting for transfers between devices  79.7 us (48%)
  starting transfers between devices  44 us (27%)
  local copies, waits for them, and re-layouts  24.5 us (15%)
  matrix products  9.62 us (6%)
  other arithmetic  6.09 us (4%)
    all_to_all x1, waiting for transfers between devices, per_device(): lax.all_to_all(jnp.concatenate([grad_first.reshape(owners, piece_len), gr...  28.3 us
    all_to_all x1, waiting for transfers between devices, per_device(): lax.all_to_all(packed, 'dp', split_axis=0, concat_axis=0, tiled=True)  25.3 us
    all_to_all x1, waiting for transfers between devices, per_device(): lax.all_to_all(jnp.broadcast_to(both_layers[None], (owners, 2, piece_len)...  20.7 us
    all_to_all x1, starting transfers between devices, per_device(): lax.all_to_all(request, 'dp', split_axis=0, concat_axis=0, tiled=True)  14.8 us
    all_to_all x1, starting transfers between devices, per_device(): lax.all_to_all(packed, 'dp', split_axis=0, concat_axis=0, tiled=True)  10.3 us
    all_to_all x1, starting transfers between devices, per_device(): lax.all_to_all(jnp.broadcast_to(both_layers[None], (owners, 2, piece_len)...  7.35 us
    conv_general_dilated x2, matrix products, conv_kernel_grad(): lax.conv_general_dilated(field, out_grad, (1, 1), ((1, 1), (1, 1)), dimen...  6.34 us
    slice x1, local copies, waits for them, and re-layouts, per_device(): second_weight = weights[1].reshape(9 * channels, channels)  6.22 us
  transfers between devices with their start and end apart: 6, of which 6 were waited for; matrix products, arithmetic and copies ran while one was open for 9% of the time, Pallas kernels for 0%

profile of v10, /device:TPU:1, one launch (start us, length us, event | category | flops | bytes accessed | tf_op | source)
XLA Modules:
  0.0 164.9 jit_solution(231599646900762155)
XLA Ops:
  0.6 0.9 convert_reduce_fusion.1
  1.6 0.7 compare_and_fusion.1
  2.2 0.8 select_reduce_fusion.2
  3.0 0.8 all_to_all.22
  3.8 14.8 %all-to-all-start = ((s32[128,1,2]{2,1,0:T(1,128)}), s32[128,1,2]{2,1,0:T(1,128)S(1)}, u32[]{:S(2)}, u32[]{:S(2)}) async-start(s32[128,1,2]{2,1,0:T(1,128)} %bitcast.2), calls=%async_computation | async-start | bytes 131072 | tf_op jit(solution)/shard_map/all_to_all | solution.py:150
  18.6 4.5 %reshape.93 = bf16[512,2048]{1,0:T(8,128)(2,1)} reshape(bf16[512,4,4,128]{3,2,1,0:T(4,128)(2,1)} %param.11) | data formatting | bytes 4194304 | tf_op jit(solution)/shard_map/reshape | solution.py:155
  23.4 3.6 %concatenate.10 = bf16[512,2176]{1,0:T(8,128)(2,1)S(1)} concatenate(bf16[512,2048]{1,0:T(8,128)(2,1)} %reshape.93, bf16[512,18]{1,0:T(8,128)(2,1)S(1)} %copy.32, bf16[512,18]{1,0:T(8,128)(2,1)S(1)} %copy.33, bf16[512,92]{1,0:T(8,128)(2,1)S(1)} %broadcast_in_dim.72), dimensions={1} | concatenate | bytes 4456448 | tf_op jit(solution)/shard_map/concatenate | solution.py:153
  27.0 2.2 %all-to-all-done = s32[128,1,2]{2,1,0:T(1,128)S(1)} async-done(((s32[128,1,2]{2,1,0:T(1,128)}), s32[128,1,2]{2,1,0:T(1,128)S(1)}, u32[]{:S(2)}, u32[]{:S(2)}) %all-to-all-start) | async-done | bytes 1056 | tf_op jit(solution)/shard_map/all_to_all | solution.py:150
  29.4 1.5 gather_fusion
  31.4 2.1 %broadcast_select_fusion = bf16[128,2,2176]{2,1,0:T(2,128)(2,1)} fusion(bf16[128,2,2176]{2,1,0:T(2,128)(2,1)S(1)} %reshape.99, pred[128,2]{1,0:T(8,128)(4,1)S(1)} %compare_and_fusion), kind=kLoop, calls=%fused_computation.2 | loop fusion | flops 557056 | bytes 2228480 | tf_op jit(solution)/shard_map/jit(_take)/select_n | solution.py:162
  33.5 10.3 %all-to-all-start.1 = ((bf16[128,2,2176]{2,1,0:T(2,128)(2,1)}), bf16[128,2,2176]{2,1,0:T(2,128)(2,1)S(1)}, u32[]{:S(2)}, u32[]{:S(2)}) async-start(bf16[128,2,2176]{2,1,0:T(2,128)(2,1)} %broadcast_select_fusion), calls=%async_computation.1 | async-start | bytes 2228224 | tf_op jit(solution)/shard_map/all_to_all | solution.py:163
  43.8 6.2 %slice_reduce_fusion = (bf16[147456]{0:T(1024)(128)(2,1)S(1)}, bf16[147456]{0:T(1024)(128)(2,1)S(1)}) fusion(bf16[2,147456]{1,0:T(2,128)(2,1)S(1)} %copy-done.1), kind=kLoop, calls=%fused_computation.22 | loop fusion | bytes 1179648 | tf_op jit(solution)/shard_map/slice | solution.py:130
  50.1 25.3 %all-to-all-done.1 = bf16[128,2,2176]{2,1,0:T(2,128)(2,1)S(1)} async-done(((bf16[128,2,2176]{2,1,0:T(2,128)(2,1)}), bf16[128,2,2176]{2,1,0:T(2,128)(2,1)S(1)}, u32[]{:S(2)}, u32[]{:S(2)}) %all-to-all-start.1) | async-done | bytes 1114144 | tf_op jit(solution)/shard_map/all_to_all | solution.py:163
  75.4 0.6 reshape.94
  76.1 1.0 gather_fusion.1
  77.8 1.4 fusion.15
  79.5 1.4 convert_reduce_fusion
  81.6 1.4 fusion.5
  83.3 4.9 %fusion.4 = f32[3,3,128,128]{3,2,1,0:T(8,128)S(1)} fusion(bf16[128,4,4,128]{0,3,2,1:T(8,128)(2,1)S(1)} %bitcast.56, pred[128,4,4,128]{3,0,2,1:T(32,128)(4,1)S(1)} %and_convert_fusion.1, bf16[3,3,128,128]{2,3,1,0:T(8,128)(2,1)S(1)} %bitcast.60, bf16[128,128]{1,0:T(8,128)(2,1)S(1)} %convolution_multiply_fusion, u8[128,4,128]{2,0,1:T(8,128)(4,1)S(1)} %fusion.16), kind=kOutput, calls=%fused_computation.10 | convolution fusion | flops 840695808 | bytes 1769472 | tf_op jit(solution)/shard_map/conv_general_dilated | solution.py:43
  88.5 1.8 %all_to_all.27 = f32[128,1,2304]{2,1,0:T(1,128)} reshape(f32[128,2304]{1,0:T(8,128)S(1)} %pad_maximum_fusion) | data formatting | bytes 2359296 | tf_op jit(solution)/shard_map/all_to_all | solution.py:180
  90.3 6.2 %all-to-all-start.2 = ((f32[128,1,2304]{2,1,0:T(1,128)}), f32[128,1,2304]{2,1,0:T(1,128)S(1)}, u32[]{:S(2)}, u32[]{:S(2)}) async-start(f32[128,1,2304]{2,1,0:T(1,128)} %all_to_all.27), calls=%async_computation.2 | async-start | bytes 2359296 | tf_op jit(solution)/shard_map/all_to_all | solution.py:180
  96.6 2.7 %collective-permute-start = (f32[3,1152]{1,0:T(4,128)S(1)}, f32[3,1152]{1,0:T(4,128)S(1)}, u32[]{:S(2)}, u32[]{:S(2)}) collective-permute-start(f32[3,1152]{1,0:T(4,128)S(1)} %pad_maximum_fusion.1), channel_id=1, source_target_pairs={{0,1},{1,0},{2,3},{3,2},{4,5},{5,4},{6,7},{7,6},{8,9},{9,8},{10,11... | collective-permute-start | bytes 41480 | tf_op jit(solution)/shard_map/ppermute | solution.py:134
  99.3 1.8 %collective-permute-done = f32[3,1152]{1,0:T(4,128)S(1)} collective-permute-done((f32[3,1152]{1,0:T(4,128)S(1)}, f32[3,1152]{1,0:T(4,128)S(1)}, u32[]{:S(2)}, u32[]{:S(2)}) %collective-permute-start) | collective-permute-done | bytes 13856 | tf_op jit(solution)/shard_map/ppermute | solution.py:134
  101.1 28.3 %all-to-all-done.2 = f32[128,1,2304]{2,1,0:T(1,128)S(1)} async-done(((f32[128,1,2304]{2,1,0:T(1,128)}), f32[128,1,2304]{2,1,0:T(1,128)S(1)}, u32[]{:S(2)}, u32[]{:S(2)}) %all-to-all-start.2) | async-done | bytes 1179680 | tf_op jit(solution)/shard_map/all_to_all | solution.py:180
  129.4 0.7 reduce_sum.69
  130.1 2.7 %collective-permute-start.1 = (f32[2,1152]{1,0:T(2,128)S(1)}, f32[2,1152]{1,0:T(2,128)S(1)}, u32[]{:S(2)}, u32[]{:S(2)}) collective-permute-start(f32[2,1152]{1,0:T(2,128)S(1)} %reshape.96), channel_id=1, source_target_pairs={{0,1},{1,0},{2,3},{3,2},{4,5},{5,4},{6,7},{7,6},{8,9},{9,8},{10,11... | collective-permute-start | bytes 27656 | tf_op jit(solution)/shard_map/ppermute | solution.py:191
  132.9 1.4 collective-permute-done.1
  134.3 1.1 broadcast_in_dim.77
  135.4 7.4 %all-to-all-start.3 = ((bf16[128,2,1152]{2,1,0:T(2,128)(2,1)}), bf16[128,2,1152]{2,1,0:T(2,128)(2,1)S(1)}, u32[]{:S(2)}, u32[]{:S(2)}) async-start(bf16[128,2,1152]{2,1,0:T(2,128)(2,1)} %broadcast_in_dim.77), calls=%async_computation.3 | async-start | bytes 1179648 | tf_op jit(solution)/shard_map/all_to_all | solution.py:197
  142.8 0.6 constant_dynamic-slice_fusion
  143.4 20.7 %all-to-all-done.3 = bf16[128,2,1152]{2,1,0:T(2,128)(2,1)S(1)} async-done(((bf16[128,2,1152]{2,1,0:T(2,128)(2,1)}), bf16[128,2,1152]{2,1,0:T(2,128)(2,1)S(1)}, u32[]{:S(2)}, u32[]{:S(2)}) %all-to-all-start.3) | async-done | bytes 589856 | tf_op jit(solution)/shard_map/all_to_all | solution.py:197
  164.1 0.8 copy.51
  (52 shorter events, 3.2 us)
Async XLA Ops:
  0.6 80.4 %copy-start = (bf16[128,18]{0,1:T(8,128)(2,1)S(1)}, bf16[128,18]{0,1:T(8,128)(2,1)}, u32[]{:S(2)}) copy-start(bf16[128,18]{0,1:T(8,128)(2,1)} %param.18) | copy-start | bytes 13828
  3.8 25.4 %all-to-all-start = ((s32[128,1,2]{2,1,0:T(1,128)}), s32[128,1,2]{2,1,0:T(1,128)S(1)}, u32[]{:S(2)}, u32[]{:S(2)}) async-start(s32[128,1,2]{2,1,0:T(1,128)} %bitcast.2), calls=%async_computation | async-start | bytes 131072 | tf_op jit(solution)/shard_map/all_to_all | solution.py:150
  18.5 4.5 %copy-start.3 = (bf16[512,18]{0,1:T(8,128)(2,1)S(1)}, bf16[512,18]{0,1:T(8,128)(2,1)}, u32[]{:S(2)}) copy-start(bf16[512,18]{0,1:T(8,128)(2,1)} %param.12) | copy-start | bytes 55300
  18.6 4.7 %copy-start.4 = (bf16[512,18]{0,1:T(8,128)(2,1)S(1)}, bf16[512,18]{0,1:T(8,128)(2,1)}, u32[]{:S(2)}) copy-start(bf16[512,18]{0,1:T(8,128)(2,1)} %param.13) | copy-start | bytes 55300
  33.5 10.3 %copy-start.1 = (bf16[2,147456]{1,0:T(2,128)(2,1)S(1)}, bf16[2,147456]{1,0:T(2,128)(2,1)}, u32[]{:S(2)}) copy-start(bf16[2,147456]{1,0:T(2,128)(2,1)} %param.17) | copy-start | bytes 1769476
  33.5 41.9 %all-to-all-start.1 = ((bf16[128,2,2176]{2,1,0:T(2,128)(2,1)}), bf16[128,2,2176]{2,1,0:T(2,128)(2,1)S(1)}, u32[]{:S(2)}, u32[]{:S(2)}) async-start(bf16[128,2,2176]{2,1,0:T(2,128)(2,1)} %broadcast_select_fusion), calls=%async_computation.1 | async-start | bytes 2228224 | tf_op jit(solution)/shard_map/all_to_all | solution.py:163
  77.5 1.8 %copy-start.2 = (s32[128,20]{0,1:T(8,128)S(1)}, s32[128,20]{0,1:T(8,128)}, u32[]{:S(2)}) copy-start(s32[128,20]{0,1:T(8,128)} %param.16) | copy-start | bytes 30724
  90.3 6.2 %copy-start.5 = (f32[1,1152]{1,0:T(1,128)S(1)}, f32[1,1152]{1,0:T(1,128)}, u32[]{:S(2)}) copy-start(f32[1,1152]{1,0:T(1,128)} %param.21) | copy-start | bytes 13828
  90.3 6.2 %copy-start.6 = (f32[1,1152]{1,0:T(1,128)S(1)}, f32[1,1152]{1,0:T(1,128)}, u32[]{:S(2)}) copy-start(f32[1,1152]{1,0:T(1,128)} %param.20) | copy-start | bytes 13828
  90.3 6.3 %copy-start.7 = (f32[1,1152]{1,0:T(1,128)S(1)}, f32[1,1152]{1,0:T(1,128)}, u32[]{:S(2)}) copy-start(f32[1,1152]{1,0:T(1,128)} %param.19) | copy-start | bytes 13828
  90.3 39.1 %all-to-all-start.2 = ((f32[128,1,2304]{2,1,0:T(1,128)}), f32[128,1,2304]{2,1,0:T(1,128)S(1)}, u32[]{:S(2)}, u32[]{:S(2)}) async-start(f32[128,1,2304]{2,1,0:T(1,128)} %all_to_all.27), calls=%async_computation.2 | async-start | bytes 2359296 | tf_op jit(solution)/shard_map/all_to_all | solution.py:180
  96.6 4.5 %collective-permute-start = (f32[3,1152]{1,0:T(4,128)S(1)}, f32[3,1152]{1,0:T(4,128)S(1)}, u32[]{:S(2)}, u32[]{:S(2)}) collective-permute-start(f32[3,1152]{1,0:T(4,128)S(1)} %pad_maximum_fusion.1), channel_id=1, source_target_pairs={{0,1},{1,0},{2,3},{3,2},{4,5},{5,4},{6,7},{7,6},{8,9},{9,8},{10,11... | collective-permute-start | bytes 41480 | tf_op jit(solution)/shard_map/ppermute | solution.py:134
  130.1 4.1 %collective-permute-start.1 = (f32[2,1152]{1,0:T(2,128)S(1)}, f32[2,1152]{1,0:T(2,128)S(1)}, u32[]{:S(2)}, u32[]{:S(2)}) collective-permute-start(f32[2,1152]{1,0:T(2,128)S(1)} %reshape.96), channel_id=1, source_target_pairs={{0,1},{1,0},{2,3},{3,2},{4,5},{5,4},{6,7},{7,6},{8,9},{9,8},{10,11... | collective-permute-start | bytes 27656 | tf_op jit(solution)/shard_map/ppermute | solution.py:191
  135.4 28.7 %all-to-all-start.3 = ((bf16[128,2,1152]{2,1,0:T(2,128)(2,1)}), bf16[128,2,1152]{2,1,0:T(2,128)(2,1)S(1)}, u32[]{:S(2)}, u32[]{:S(2)}) async-start(bf16[128,2,1152]{2,1,0:T(2,128)(2,1)} %broadcast_in_dim.77), calls=%async_computation.3 | async-start | bytes 1179648 | tf_op jit(solution)/shard_map/all_to_all | solution.py:197

commit v11 on v9

--- a/solution.py
+++ b/solution.py
@@ -155,7 +155,6 @@
             replay_rows.reshape(-1, row_width),
             qvalues,
             target_logits,
-            jnp.zeros((qvalues.shape[0], channels - 2 * actions_n), qvalues.dtype),
         ],
         axis=-1,
     )

time: 165 us -> 166 us (level)
  no operation moved by 1% of the time
where the time goes in v11:
time: 166 us; the launch traced here: 165 us
  waiting for transfers between devices  79.7 us (48%)
  starting transfers between devices  44 us (27%)
  local copies, waits for them, and re-layouts  22.8 us (14%)
  matrix products  9.63 us (6%)
  other arithmetic  7.88 us (5%)
    all_to_all x1, waiting for transfers between devices, per_device(): lax.all_to_all(loss_derivative.reshape(2, owners, piece_len).transpose(1,...  28.3 us
    all_to_all x1, waiting for transfers between devices, per_device(): lax.all_to_all(packed, 'dp', split_axis=0, concat_axis=0, tiled=True)  25.3 us
    all_to_all x1, waiting for transfers between devices, per_device(): lax.all_to_all(jnp.broadcast_to(both_layers[None], (owners, 2, piece_len)...  20.7 us
    all_to_all x1, starting transfers between devices, per_device(): lax.all_to_all(request, 'dp', split_axis=0, concat_axis=0, tiled=True)  14.8 us
    all_to_all x1, starting transfers between devices, per_device(): lax.all_to_all(packed, 'dp', split_axis=0, concat_axis=0, tiled=True)  10.2 us
    all_to_all x1, starting transfers between devices, per_device(): lax.all_to_all(jnp.broadcast_to(both_layers[None], (owners, 2, piece_len)...  7.35 us
    conv_general_dilated x2, matrix products, conv_kernel_grad(): lax.conv_general_dilated(field, out_grad, (1, 1), ((1, 1), (1, 1)), dimen...  6.34 us
    slice x1, local copies, waits for them, and re-layouts, per_device(): second_weight = weights[1].reshape(9 * channels, channels)  6.22 us
  transfers between devices with their start and end apart: 6, of which 6 were waited for; matrix products, arithmetic and copies ran while one was open for 9% of the time, Pallas kernels for 0%

profile of v11, /device:TPU:1, one launch (start us, length us, event | category | flops | bytes accessed | tf_op | source)
XLA Modules:
  0.0 164.9 jit_solution(3503350841028517005)
XLA Ops:
  0.6 0.9 convert_reduce_fusion.1
  1.6 0.7 compare_and_fusion.1
  2.2 0.8 select_reduce_fusion.2
  3.0 0.8 all_to_all.19
  3.8 14.8 %all-to-all-start = ((s32[128,1,2]{2,1,0:T(1,128)}), s32[128,1,2]{2,1,0:T(1,128)S(1)}, u32[]{:S(2)}, u32[]{:S(2)}) async-start(s32[128,1,2]{2,1,0:T(1,128)} %bitcast.2), calls=%async_computation | async-start | bytes 131072 | tf_op jit(solution)/shard_map/all_to_all | solution.py:150
  18.6 4.5 %reshape.93 = bf16[512,2048]{1,0:T(8,128)(2,1)} reshape(bf16[512,4,4,128]{3,2,1,0:T(4,128)(2,1)} %param.11) | data formatting | bytes 4194304 | tf_op jit(solution)/shard_map/reshape | solution.py:155
  23.4 3.6 %concatenate.8 = bf16[512,2084]{1,0:T(8,128)(2,1)S(1)} concatenate(bf16[512,2048]{1,0:T(8,128)(2,1)} %reshape.93, bf16[512,18]{1,0:T(8,128)(2,1)S(1)} %copy.34, bf16[512,18]{1,0:T(8,128)(2,1)S(1)} %copy.35), dimensions={1} | concatenate | bytes 4268032 | tf_op jit(solution)/shard_map/concatenate | solution.py:153
  27.0 2.2 %all-to-all-done = s32[128,1,2]{2,1,0:T(1,128)S(1)} async-done(((s32[128,1,2]{2,1,0:T(1,128)}), s32[128,1,2]{2,1,0:T(1,128)S(1)}, u32[]{:S(2)}, u32[]{:S(2)}) %all-to-all-start) | async-done | bytes 1056 | tf_op jit(solution)/shard_map/all_to_all | solution.py:150
  29.4 1.5 gather_fusion
  30.9 0.5 reshape.98
  31.4 2.1 %broadcast_select_fusion = bf16[128,2,2084]{2,1,0:T(2,128)(2,1)} fusion(bf16[128,2,2084]{2,1,0:T(2,128)(2,1)S(1)} %reshape.98, pred[128,2]{1,0:T(8,128)(4,1)S(1)} %compare_and_fusion), kind=kLoop, calls=%fused_computation.2 | loop fusion | flops 533504 | bytes 2134272 | tf_op jit(solution)/shard_map/jit(_take)/select_n | solution.py:161
  33.5 10.2 %all-to-all-start.1 = ((bf16[128,2,2084]{2,1,0:T(2,128)(2,1)}), bf16[128,2,2084]{2,1,0:T(2,128)(2,1)S(1)}, u32[]{:S(2)}, u32[]{:S(2)}) async-start(bf16[128,2,2084]{2,1,0:T(2,128)(2,1)} %broadcast_select_fusion), calls=%async_computation.1 | async-start | bytes 2228224 | tf_op jit(solution)/shard_map/all_to_all | solution.py:162
  43.8 6.2 %slice_reduce_fusion = (bf16[147456]{0:T(1024)(128)(2,1)S(1)}, bf16[147456]{0:T(1024)(128)(2,1)S(1)}) fusion(bf16[2,147456]{1,0:T(2,128)(2,1)S(1)} %copy-done.1), kind=kLoop, calls=%fused_computation.22 | loop fusion | bytes 1179648 | tf_op jit(solution)/shard_map/slice | solution.py:130
  50.1 25.3 %all-to-all-done.1 = bf16[128,2,2084]{2,1,0:T(2,128)(2,1)S(1)} async-done(((bf16[128,2,2084]{2,1,0:T(2,128)(2,1)}), bf16[128,2,2084]{2,1,0:T(2,128)(2,1)S(1)}, u32[]{:S(2)}, u32[]{:S(2)}) %all-to-all-start.1) | async-done | bytes 1067040 | tf_op jit(solution)/shard_map/all_to_all | solution.py:162
  75.4 1.0 reshape.94
  76.4 1.0 gather_fusion.1
  78.2 1.4 fusion.15
  79.9 1.4 convert_reduce_fusion
  82.2 1.4 fusion.5
  83.6 4.9 %fusion.4 = f32[3,3,128,128]{3,2,1,0:T(8,128)S(1)} fusion(bf16[128,4,4,128]{0,3,2,1:T(8,128)(2,1)S(1)} %bitcast.56, pred[128,4,4,128]{3,0,2,1:T(32,128)(4,1)S(1)} %and_convert_fusion.1, bf16[3,3,128,128]{2,3,1,0:T(8,128)(2,1)S(1)} %bitcast.62, bf16[128,128]{1,0:T(8,128)(2,1)S(1)} %convolution_multiply_fusion, u8[128,4,128]{2,0,1:T(8,128)(4,1)S(1)} %fusion.16), kind=kOutput, calls=%fused_computation.10 | convolution fusion | flops 840695808 | bytes 1769472 | tf_op jit(solution)/shard_map/conv_general_dilated | solution.py:43
  88.5 2.1 %maximum_bitcast_fusion = f32[128,2,1152]{2,1,0:T(2,128)} fusion(f32[1,128,1152]{2,0,1:T(1,128)S(1)} %bitcast.59, f32[1,128,1152]{2,0,1:T(1,128)S(1)} %bitcast.60), kind=kLoop, calls=%fused_computation.11 | loop fusion | flops 294912 | bytes 2359296 | tf_op jit(solution)/shard_map/transpose | solution.py:181
  90.6 6.2 %all-to-all-start.2 = ((f32[128,2,1152]{2,1,0:T(2,128)}), f32[128,2,1152]{2,1,0:T(2,128)S(1)}, u32[]{:S(2)}, u32[]{:S(2)}) async-start(f32[128,2,1152]{2,1,0:T(2,128)} %maximum_bitcast_fusion), calls=%async_computation.2 | async-start | bytes 2359296 | tf_op jit(solution)/shard_map/all_to_all | solution.py:180
  96.9 2.7 %collective-permute-start = (f32[3,1152]{1,0:T(4,128)S(1)}, f32[3,1152]{1,0:T(4,128)S(1)}, u32[]{:S(2)}, u32[]{:S(2)}) collective-permute-start(f32[3,1152]{1,0:T(4,128)S(1)} %pad_maximum_fusion), channel_id=1, source_target_pairs={{0,1},{1,0},{2,3},{3,2},{4,5},{5,4},{6,7},{7,6},{8,9},{9,8},{10,11... | collective-permute-start | bytes 41480 | tf_op jit(solution)/shard_map/ppermute | solution.py:134
  99.6 1.7 %collective-permute-done = f32[3,1152]{1,0:T(4,128)S(1)} collective-permute-done((f32[3,1152]{1,0:T(4,128)S(1)}, f32[3,1152]{1,0:T(4,128)S(1)}, u32[]{:S(2)}, u32[]{:S(2)}) %collective-permute-start) | collective-permute-done | bytes 13856 | tf_op jit(solution)/shard_map/ppermute | solution.py:134
  101.4 28.3 %all-to-all-done.2 = f32[128,2,1152]{2,1,0:T(2,128)S(1)} async-done(((f32[128,2,1152]{2,1,0:T(2,128)}), f32[128,2,1152]{2,1,0:T(2,128)S(1)}, u32[]{:S(2)}, u32[]{:S(2)}) %all-to-all-start.2) | async-done | bytes 1179680 | tf_op jit(solution)/shard_map/all_to_all | solution.py:180
  130.2 2.7 %collective-permute-start.1 = (f32[2,1152]{1,0:T(2,128)S(1)}, f32[2,1152]{1,0:T(2,128)S(1)}, u32[]{:S(2)}, u32[]{:S(2)}) collective-permute-start(f32[2,1152]{1,0:T(2,128)S(1)} %reduce_sum.69), channel_id=1, source_target_pairs={{0,1},{1,0},{2,3},{3,2},{4,5},{5,4},{6,7},{7,6},{8,9},{9,8},{10,11... | collective-permute-start | bytes 27656 | tf_op jit(solution)/shard_map/ppermute | solution.py:188
  132.9 1.3 collective-permute-done.1
  134.3 1.1 broadcast_in_dim.73
  135.4 7.4 %all-to-all-start.3 = ((bf16[128,2,1152]{2,1,0:T(2,128)(2,1)}), bf16[128,2,1152]{2,1,0:T(2,128)(2,1)S(1)}, u32[]{:S(2)}, u32[]{:S(2)}) async-start(bf16[128,2,1152]{2,1,0:T(2,128)(2,1)} %broadcast_in_dim.73), calls=%async_computation.3 | async-start | bytes 1179648 | tf_op jit(solution)/shard_map/all_to_all | solution.py:194
  142.8 0.6 constant_dynamic-slice_fusion
  143.4 20.7 %all-to-all-done.3 = bf16[128,2,1152]{2,1,0:T(2,128)(2,1)S(1)} async-done(((bf16[128,2,1152]{2,1,0:T(2,128)(2,1)}), bf16[128,2,1152]{2,1,0:T(2,128)(2,1)S(1)}, u32[]{:S(2)}, u32[]{:S(2)}) %all-to-all-start.3) | async-done | bytes 589856 | tf_op jit(solution)/shard_map/all_to_all | solution.py:194
  164.1 0.8 copy.55
  (47 shorter events, 2.9 us)
Async XLA Ops:
  0.6 81.1 %copy-start = (bf16[128,18]{0,1:T(8,128)(2,1)S(1)}, bf16[128,18]{0,1:T(8,128)(2,1)}, u32[]{:S(2)}) copy-start(bf16[128,18]{0,1:T(8,128)(2,1)} %param.18) | copy-start | bytes 13828
  3.8 25.4 %all-to-all-start = ((s32[128,1,2]{2,1,0:T(1,128)}), s32[128,1,2]{2,1,0:T(1,128)S(1)}, u32[]{:S(2)}, u32[]{:S(2)}) async-start(s32[128,1,2]{2,1,0:T(1,128)} %bitcast.2), calls=%async_computation | async-start | bytes 131072 | tf_op jit(solution)/shard_map/all_to_all | solution.py:150
  18.5 4.5 %copy-start.3 = (bf16[512,18]{0,1:T(8,128)(2,1)S(1)}, bf16[512,18]{0,1:T(8,128)(2,1)}, u32[]{:S(2)}) copy-start(bf16[512,18]{0,1:T(8,128)(2,1)} %param.12) | copy-start | bytes 55300
  18.6 4.7 %copy-start.4 = (bf16[512,18]{0,1:T(8,128)(2,1)S(1)}, bf16[512,18]{0,1:T(8,128)(2,1)}, u32[]{:S(2)}) copy-start(bf16[512,18]{0,1:T(8,128)(2,1)} %param.13) | copy-start | bytes 55300
  33.5 10.2 %copy-start.1 = (bf16[2,147456]{1,0:T(2,128)(2,1)S(1)}, bf16[2,147456]{1,0:T(2,128)(2,1)}, u32[]{:S(2)}) copy-start(bf16[2,147456]{1,0:T(2,128)(2,1)} %param.17) | copy-start | bytes 1769476
  33.5 41.9 %all-to-all-start.1 = ((bf16[128,2,2084]{2,1,0:T(2,128)(2,1)}), bf16[128,2,2084]{2,1,0:T(2,128)(2,1)S(1)}, u32[]{:S(2)}, u32[]{:S(2)}) async-start(bf16[128,2,2084]{2,1,0:T(2,128)(2,1)} %broadcast_select_fusion), calls=%async_computation.1 | async-start | bytes 2228224 | tf_op jit(solution)/shard_map/all_to_all | solution.py:162
  77.9 1.8 %copy-start.2 = (s32[128,20]{0,1:T(8,128)S(1)}, s32[128,20]{0,1:T(8,128)}, u32[]{:S(2)}) copy-start(s32[128,20]{0,1:T(8,128)} %param.16) | copy-start | bytes 30724
  90.6 6.2 %copy-start.5 = (f32[1,1152]{1,0:T(1,128)S(1)}, f32[1,1152]{1,0:T(1,128)}, u32[]{:S(2)}) copy-start(f32[1,1152]{1,0:T(1,128)} %param.21) | copy-start | bytes 13828
  90.6 6.2 %copy-start.6 = (f32[1,1152]{1,0:T(1,128)S(1)}, f32[1,1152]{1,0:T(1,128)}, u32[]{:S(2)}) copy-start(f32[1,1152]{1,0:T(1,128)} %param.20) | copy-start | bytes 13828
  90.6 6.2 %copy-start.7 = (f32[1,1152]{1,0:T(1,128)S(1)}, f32[1,1152]{1,0:T(1,128)}, u32[]{:S(2)}) copy-start(f32[1,1152]{1,0:T(1,128)} %param.19) | copy-start | bytes 13828
  90.6 39.1 %all-to-all-start.2 = ((f32[128,2,1152]{2,1,0:T(2,128)}), f32[128,2,1152]{2,1,0:T(2,128)S(1)}, u32[]{:S(2)}, u32[]{:S(2)}) async-start(f32[128,2,1152]{2,1,0:T(2,128)} %maximum_bitcast_fusion), calls=%async_computation.2 | async-start | bytes 2359296 | tf_op jit(solution)/shard_map/all_to_all | solution.py:180
  96.9 4.5 %collective-permute-start = (f32[3,1152]{1,0:T(4,128)S(1)}, f32[3,1152]{1,0:T(4,128)S(1)}, u32[]{:S(2)}, u32[]{:S(2)}) collective-permute-start(f32[3,1152]{1,0:T(4,128)S(1)} %pad_maximum_fusion), channel_id=1, source_target_pairs={{0,1},{1,0},{2,3},{3,2},{4,5},{5,4},{6,7},{7,6},{8,9},{9,8},{10,11... | collective-permute-start | bytes 41480 | tf_op jit(solution)/shard_map/ppermute | solution.py:134
  130.2 4.1 %collective-permute-start.1 = (f32[2,1152]{1,0:T(2,128)S(1)}, f32[2,1152]{1,0:T(2,128)S(1)}, u32[]{:S(2)}, u32[]{:S(2)}) collective-permute-start(f32[2,1152]{1,0:T(2,128)S(1)} %reduce_sum.69), channel_id=1, source_target_pairs={{0,1},{1,0},{2,3},{3,2},{4,5},{5,4},{6,7},{7,6},{8,9},{9,8},{10,11... | collective-permute-start | bytes 27656 | tf_op jit(solution)/shard_map/ppermute | solution.py:188
  135.4 28.7 %all-to-all-start.3 = ((bf16[128,2,1152]{2,1,0:T(2,128)(2,1)}), bf16[128,2,1152]{2,1,0:T(2,128)(2,1)S(1)}, u32[]{:S(2)}, u32[]{:S(2)}) async-start(bf16[128,2,1152]{2,1,0:T(2,128)(2,1)} %broadcast_in_dim.73), calls=%async_computation.3 | async-start | bytes 1179648 | tf_op jit(solution)/shard_map/all_to_all | solution.py:194
